TPU v7x, 256 devices: a whole 4x4x8 slice. The times are simulated.
256 devices in a mesh: dp: 8 (over y, core), expert: 32 (over x, z).
Axes of the slice: x: 4, y: 4, z: 8, core: 2. Of those that a mesh axis runs over, the one named last changes fastest.
Arguments:
- tokens: bfloat16 [32768, 2048], P(('dp', 'expert')), may hold values from -6 to 6
- tangents: bfloat16 [32768, 2048], P(('dp', 'expert')), may hold values from -6 to 6
- cotangents: bfloat16 [32768, 2048], P(('dp', 'expert')), may hold values from -6 to 6
- routes: int32 [32768, 2], P(('dp', 'expert')), may hold values from 0 to 31, all different within a row; in each aligned block of 128 rows (0 to 127, 128 to 255, ...) at most 16 rows name the same one
- gates: bfloat16 [32768, 2], P(('dp', 'expert')), may hold values from 0.19921875 to 1
- w_up: bfloat16 [32, 2048, 768], P('expert'), may hold values from -0.125 to 0.125
- w_down: bfloat16 [32, 768, 2048], P('expert'), may hold values from -0.21875 to 0.21875
- v_up: bfloat16 [32, 2048, 768], P('expert'), may hold values from -0.125 to 0.125
Outputs:
- hvp_tokens: bfloat16 [32768, 2048], P(('dp', 'expert'))
- hvp_up: bfloat16 [32, 2048, 768], P('expert', 'dp')
- hvp_down: bfloat16 [32, 768, 2048], P('expert', None, 'dp')
Inputs may be any that keep to these rules, and one draw needn't show every extreme that they name: `routes`: A token's 2 experts differ. Among the 128 tokens of one device no expert is named more than 16 times, and in every draw some device names some expert exactly 16 times.
All inputs are finite; a program needn't handle non-finite values.
Results may differ from a plain program's by a relative error of at most 0.014.
Values may be sent and summed in bfloat16 or wider, within the bound.
No kernel may reach another device: no remote copies, remote signals or barrier semaphores. Data moves between devices by JAX's collectives and lax.ppermute only.
A program may use at most 128 MiB of HBM per device.

v0:
```python
import math

import jax
import jax.numpy as jnp
from jax import lax
from jax.sharding import PartitionSpec as P


def slot_table(route_ids, expert_count, capacity):
    token_count, route_count = route_ids.shape
    flat_ids = route_ids.reshape(token_count * route_count)
    onehot = (flat_ids[:, None] == jnp.arange(expert_count, dtype=jnp.int32)[None, :]).astype(
        jnp.int32
    )
    before = jnp.cumsum(onehot, axis=0) - onehot
    slot_rank = jnp.sum(before * onehot, axis=1)
    target = flat_ids * capacity + slot_rank
    slot_owner = (
        jnp.full((expert_count * capacity,), -1, jnp.int32)
        .at[target]
        .set(jnp.arange(token_count * route_count, dtype=jnp.int32))
    )
    return (target, slot_owner)


def gather_slots(rows, slot_owner, route_count):
    valid = slot_owner >= 0
    safe = jnp.where(valid, slot_owner, 0) // route_count
    picked = jnp.take(rows, safe, axis=0)
    return jnp.where(valid[:, None], picked, jnp.zeros_like(picked))


def gather_gates(gate_rows, slot_owner):
    valid = slot_owner >= 0
    flat_gate = gate_rows.reshape(-1)
    picked = jnp.take(flat_gate, jnp.where(valid, slot_owner, 0), axis=0)
    return jnp.where(valid, picked, jnp.zeros_like(picked))


def per_device(tokens, tangents, cotangents, routes, gates, w_up, w_down, v_up):
    token_count, width = tokens.shape
    route_count = routes.shape[1]
    expert_count = lax.axis_size("expert")
    replicas = lax.axis_size("dp")
    capacity = max(2, token_count * route_count * 2 // expert_count)
    scale = 1.0 / math.sqrt(token_count * route_count * replicas)
    target, slot_owner = slot_table(routes, expert_count, capacity)
    send_primal = gather_slots(tokens, slot_owner, route_count).reshape(
        expert_count, capacity, width
    )
    send_tangent = gather_slots(tangents, slot_owner, route_count).reshape(
        expert_count, capacity, width
    )
    send_cotan = gather_slots(cotangents, slot_owner, route_count).reshape(
        expert_count, capacity, width
    )
    send_gate = gather_gates(gates, slot_owner).reshape(expert_count, capacity)
    primal = lax.all_to_all(send_primal, "expert", split_axis=0, concat_axis=0, tiled=True)
    tangent = lax.all_to_all(send_tangent, "expert", split_axis=0, concat_axis=0, tiled=True)
    cotan, gate_slot = (
        lax.all_to_all(send_cotan, "expert", split_axis=0, concat_axis=0, tiled=True),
        lax.all_to_all(send_gate, "expert", split_axis=0, concat_axis=0, tiled=True),
    )
    slots = expert_count * capacity
    primal = primal.reshape(slots, width)
    tangent = tangent.reshape(slots, width)
    cotan = cotan.reshape(slots, width)
    gate_slot = gate_slot.reshape(slots)
    up_proj = w_up[0]
    down_proj = w_down[0]
    dir_up = v_up[0]
    pre_act = jnp.dot(primal, up_proj, preferred_element_type=jnp.float32)
    pre_tan = jnp.dot(tangent, up_proj, preferred_element_type=jnp.float32) + jnp.dot(
        primal, dir_up, preferred_element_type=jnp.float32
    )
    sigmoid_z = jax.nn.sigmoid(pre_act)
    first_der = sigmoid_z * (1.0 + pre_act * (1.0 - sigmoid_z))
    second_der = sigmoid_z * (1.0 - sigmoid_z) * (2.0 + pre_act * (1.0 - 2.0 * sigmoid_z))
    hidden_tan = (first_der * pre_tan).astype(jnp.bfloat16)
    scaled_cot = (gate_slot.astype(jnp.float32)[:, None] * cotan.astype(jnp.float32)).astype(
        jnp.bfloat16
    )
    back_hid = jnp.dot(scaled_cot, down_proj.T, preferred_element_type=jnp.float32)
    back_pre = (back_hid * first_der).astype(jnp.bfloat16)
    back_tan = (back_hid * second_der * pre_tan).astype(jnp.bfloat16)
    input_hvp = (
        jnp.dot(back_tan, up_proj.T, preferred_element_type=jnp.float32)
        + jnp.dot(back_pre, dir_up.T, preferred_element_type=jnp.float32)
    ).astype(jnp.bfloat16)
    returned = lax.all_to_all(
        input_hvp.reshape(expert_count, capacity, width),
        "expert",
        split_axis=0,
        concat_axis=0,
        tiled=True,
    )
    route_rows = jnp.take(returned.reshape(slots, width), target, axis=0).astype(jnp.float32)
    hvp_tokens = jnp.sum(route_rows.reshape(token_count, route_count, width), axis=1).astype(
        jnp.bfloat16
    )
    first = jnp.dot(tangent.T, back_pre, preferred_element_type=jnp.float32) + jnp.dot(
        primal.T, back_tan, preferred_element_type=jnp.float32
    )
    second = jnp.dot(scaled_cot.T, hidden_tan, preferred_element_type=jnp.float32)
    summed = lax.psum_scatter(
        (jnp.concatenate([first, second], axis=1) * scale).astype(jnp.bfloat16),
        "dp",
        scatter_dimension=0,
        tiled=True,
    ).astype(jnp.float32)
    hidden_units = up_proj.shape[1]
    hvp_up = summed[:, :hidden_units].astype(jnp.bfloat16)[None]
    hvp_down = summed[:, hidden_units:].T.astype(jnp.bfloat16)[None]
    return (hvp_tokens, hvp_up, hvp_down)


def solution(mesh):
    in_specs = (
        P(("dp", "expert"), None),
        P(("dp", "expert"), None),
        P(("dp", "expert"), None),
        P(("dp", "expert"), None),
        P(("dp", "expert"), None),
        P("expert", None, None),
        P("expert", None, None),
        P("expert", None, None),
    )
    out_specs = (P(("dp", "expert"), None), P("expert", "dp", None), P("expert", None, "dp"))
    return jax.shard_map(
        per_device, mesh=mesh, in_specs=in_specs, out_specs=out_specs, check_vma=False
    )
```

profile of v0, /device:TPU:2, one launch (start us, length us, event | category | flops | bytes accessed | tf_op | source)
XLA Modules:
  0.0 335.2 jit_solution(5844678368232431282)
XLA Ops:
  12.8 3.4 %gather_fusion = bf16[512]{0:T(512)(128)(2,1)S(1)} fusion(bf16[256]{0:T(256)(128)(2,1)S(1)} %reshape.130, s32[1024]{0:T(1024)S(1)} %pad_clamp_fusion.2), kind=kCustom, calls=%fused_computation.3 | custom fusion | bytes 4096 | tf_op jit(solution)/shard_map/jit(_take)/gather | solution.py:36
  16.9 11.6 %all-to-all-start = ((bf16[32,1,16]{2,1,0:T(2,128)(2,1)}), bf16[32,1,16]{2,1,0:T(2,128)(2,1)S(1)}, u32[]{:S(2)}, u32[]{:S(2)}) async-start(bf16[32,1,16]{2,1,0:T(2,128)(2,1)} %all_to_all.24), calls=%async_computation | async-start | bytes 32768 | tf_op jit(solution)/shard_map/all_to_all | solution.py:62
  28.5 6.4 %gather_fusion.4 = bf16[512,2048]{1,0:T(8,128)(2,1)} fusion(bf16[128,2048]{1,0:T(8,128)(2,1)} %param.11, s32[1024]{0:T(1024)S(1)} %pad_clamp_fusion.1), kind=kCustom, calls=%fused_computation.2.clone | custom fusion | bytes 4196352 | tf_op jit(solution)/shard_map/jit(_take)/gather | solution.py:29
  34.9 6.3 %gather_fusion.3 = bf16[512,2048]{1,0:T(8,128)(2,1)} fusion(bf16[128,2048]{1,0:T(8,128)(2,1)} %param.10, s32[1024]{0:T(1024)S(1)} %pad_clamp_fusion.1), kind=kCustom, calls=%fused_computation.1.clone | custom fusion | bytes 4196352 | tf_op jit(solution)/shard_map/jit(_take)/gather | solution.py:29
  41.2 6.4 %gather_fusion.2 = bf16[512,2048]{1,0:T(8,128)(2,1)} fusion(bf16[128,2048]{1,0:T(8,128)(2,1)} %param.12, s32[1024]{0:T(1024)S(1)} %pad_clamp_fusion.1), kind=kCustom, calls=%fused_computation.clone | custom fusion | bytes 4196352 | tf_op jit(solution)/shard_map/jit(_take)/gather | solution.py:29
  47.6 4.8 %select_select_fusion = (bf16[512,2048]{1,0:T(8,128)(2,1)}, bf16[512,2048]{1,0:T(8,128)(2,1)}, bf16[512,2048]{1,0:T(8,128)(2,1)}) fusion(bf16[512,2048]{1,0:T(8,128)(2,1)} %gather_fusion.4, pred[512]{0:T(512)(128)(4,1)S(1)} %get-tuple-element.16, pred[512]{0:T(512)(128)(4,1)S(1)} %get-tuple-element.18, bf16[512,2048]{1,0:T(8,128)(2,1)} %gather_fusion.3, ...), kind=kLoop, calls=%fused_computation.27 | loop fusion | flops 6291456 | bytes 12583936 | tf_op jit(solution)/shard_map/jit(_where)/select_n | solution.py:30
  52.4 58.3 %all_to_all.30 = bf16[32,16,2048]{2,1,0:T(8,128)(2,1)} all-to-all(bf16[32,16,2048]{2,1,0:T(8,128)(2,1)} %bitcast.77), channel_id=1, replica_groups=mesh['dp'=8,'expert'=32] {'expert'}, dimensions={0} | all-to-all | bytes 4194304 | tf_op jit(solution)/shard_map/all_to_all | solution.py:61
  110.7 55.6 %all_to_all.31 = bf16[32,16,2048]{2,1,0:T(8,128)(2,1)} all-to-all(bf16[32,16,2048]{2,1,0:T(8,128)(2,1)S(1)} %bitcast.76), channel_id=1, replica_groups=mesh['dp'=8,'expert'=32] {'expert'}, dimensions={0} | all-to-all | bytes 4194304 | tf_op jit(solution)/shard_map/all_to_all | solution.py:58
  166.2 7.5 %all-to-all-start.3 = ((bf16[32,16,2048]{2,1,0:T(8,128)(2,1)}), bf16[32,16,2048]{2,1,0:T(8,128)(2,1)}, u32[]{:S(2)}, u32[]{:S(2)}) async-start(bf16[32,16,2048]{2,1,0:T(8,128)(2,1)} %bitcast.75), calls=%async_computation.3 | async-start | bytes 4194304 | tf_op jit(solution)/shard_map/all_to_all | solution.py:59
  174.2 4.8 %fusion.10 = f32[512,768]{1,0:T(8,128)} fusion(bf16[512,2048]{1,0:T(8,128)(2,1)} %bitcast.72, bf16[1,2048,768]{2,1,0:T(8,128)(2,1)S(1)} %copy-done), kind=kOutput, calls=%fused_computation.21 | convolution fusion | flops 1610612736 | bytes 6815744 | tf_op jit(solution)/shard_map/dot_general | solution.py:72
  178.9 3.0 fusion.4
  183.8 3.0 fusion.12
  186.8 34.0 %all-to-all-done.3 = bf16[32,16,2048]{2,1,0:T(8,128)(2,1)} async-done(((bf16[32,16,2048]{2,1,0:T(8,128)(2,1)}), bf16[32,16,2048]{2,1,0:T(8,128)(2,1)}, u32[]{:S(2)}, u32[]{:S(2)}) %all-to-all-start.3) | async-done | bytes 2097184 | tf_op jit(solution)/shard_map/all_to_all | solution.py:59
  220.8 5.4 %fusion.19 = (bf16[512,768]{1,0:T(8,128)(2,1)S(1)}, bf16[512,768]{1,0:T(8,128)(2,1)S(1)}, f32[512,768]{1,0:T(8,128)S(1)}) fusion(f32[512,768]{1,0:T(8,128)} %fusion.12, f32[512,768]{1,0:T(8,128)} %fusion.10, f32[512,768]{1,0:T(8,128)} %fusion.4, bf16[512,2048]{1,0:T(8,128)(2,1)} %bitcast.11, bf16[1,2048,768]{2,1,0:T(8,128)(2,1)S(1)} %copy-done), kind=kOutput, calls=%fused_computation.34 | convolution fusion | flops 1618083840 | bytes 13107200 | tf_op jit(solution)/shard_map/dot_general | solution.py:73
  226.2 4.0 %fusion.37 = f32[2048,768]{0,1:T(8,128)S(1)} fusion(bf16[512,2048]{1,0:T(8,128)(2,1)} %bitcast.11, bf16[512,768]{1,0:T(8,128)(2,1)S(1)} %get-tuple-element.20), kind=kOutput, calls=%fused_computation.77 | convolution fusion | flops 1610612736 | bytes 9175040 | tf_op jit(solution)/shard_map/dot_general | solution.py:101
  231.7 4.7 %fusion.26 = f32[2048,768]{0,1:T(8,128)} fusion(bf16[512,2048]{1,0:T(8,128)(2,1)S(1)} %fusion.1, f32[512,768]{1,0:T(8,128)S(1)} %get-tuple-element.26, f32[512,768]{1,0:T(8,128)S(1)} %copy-done.12), kind=kOutput, calls=%fused_computation.42 | convolution fusion | flops 1614151680 | bytes 11534336 | tf_op jit(solution)/shard_map/dot_general | solution.py:104
  236.4 4.7 %convolution_add_fusion = f32[2048,768]{0,1:T(8,128)} fusion(f32[2048,768]{0,1:T(8,128)S(1)} %fusion.37, bf16[512,2048]{1,0:T(8,128)(2,1)S(1)} %bitcast.74, bf16[512,768]{1,0:T(8,128)(2,1)S(1)} %get-tuple-element.19), kind=kOutput, calls=%fused_computation.12 | convolution fusion | flops 1612185600 | bytes 15466496 | tf_op jit(solution)/shard_map/dot_general | solution.py:101
  241.1 9.1 %fusion = bf16[2048,1536]{0,1:T(8,128)(2,1)} fusion(f32[2048,768]{0,1:T(8,128)} %fusion.26, f32[2048,768]{0,1:T(8,128)} %convolution_add_fusion), kind=kLoop, calls=%fused_computation.7 | loop fusion | flops 9437184 | bytes 18874368 | tf_op jit(solution)/shard_map/convert_element_type | solution.py:106
  250.2 4.0 %fusion.2 = f32[512,2048]{1,0:T(8,128)S(1)} fusion(bf16[512,768]{1,0:T(8,128)(2,1)} %copy-done.8, bf16[1,2048,768]{2,1,0:T(8,128)(2,1)} %param.17), kind=kOutput, calls=%fused_computation.13 | convolution fusion | flops 1610612736 | bytes 8126464 | tf_op jit(solution)/shard_map/dot_general | solution.py:88
  254.2 3.2 add_convert_fusion
  257.4 8.8 %all-to-all-start.4 = ((bf16[32,16,2048]{2,1,0:T(8,128)(2,1)}), bf16[32,16,2048]{2,1,0:T(8,128)(2,1)}, u32[]{:S(2)}, u32[]{:S(2)}) async-start(bf16[32,16,2048]{2,1,0:T(8,128)(2,1)} %bitcast.78), calls=%async_computation.4 | async-start | bytes 4194304 | tf_op jit(solution)/shard_map/all_to_all | solution.py:90
  266.7 46.7 %all-to-all-done.4 = bf16[32,16,2048]{2,1,0:T(8,128)(2,1)} async-done(((bf16[32,16,2048]{2,1,0:T(8,128)(2,1)}), bf16[32,16,2048]{2,1,0:T(8,128)(2,1)}, u32[]{:S(2)}, u32[]{:S(2)}) %all-to-all-start.4) | async-done | bytes 2097184 | tf_op jit(solution)/shard_map/all_to_all | solution.py:90
  313.4 5.3 %gather_fusion.1 = bf16[256,2048]{1,0:T(8,128)(2,1)} fusion(bf16[512,2048]{1,0:T(8,128)(2,1)} %bitcast.14, s32[1024]{0:T(1024)S(1)} %pad_clamp_fusion), kind=kCustom, calls=%fused_computation.4 | custom fusion | bytes 2098176 | tf_op jit(solution)/shard_map/jit(_take)/gather | solution.py:97
  321.2 4.4 %fusion.25 = bf16[128,2048]{1,0:T(8,128)(2,1)} fusion(bf16[128,2,2048]{2,1,0:T(2,128)(2,1)} %gather.15, pred[128,2]{1,0:T(8,128)(4,1)S(1)} %copy.30), kind=kLoop, calls=%fused_computation.41 | loop fusion | flops 786432 | bytes 1573120 | tf_op jit(solution)/shard_map/reduce_sum | solution.py:98
  (66 shorter events, 15.7 us)
Async XLA Ops:
  7.2 167.0 %copy-start = (bf16[1,2048,768]{2,1,0:T(8,128)(2,1)S(1)}, bf16[1,2048,768]{2,1,0:T(8,128)(2,1)}, u32[]{:S(2)}) copy-start(bf16[1,2048,768]{2,1,0:T(8,128)(2,1)} %param.15) | copy-start | bytes 9437188
  16.9 35.5 %all-to-all-start = ((bf16[32,1,16]{2,1,0:T(2,128)(2,1)}), bf16[32,1,16]{2,1,0:T(2,128)(2,1)S(1)}, u32[]{:S(2)}, u32[]{:S(2)}) async-start(bf16[32,1,16]{2,1,0:T(2,128)(2,1)} %all_to_all.24), calls=%async_computation | async-start | bytes 32768 | tf_op jit(solution)/shard_map/all_to_all | solution.py:62
  52.4 58.3 %copy-start.5 = (bf16[512,2048]{1,0:T(8,128)(2,1)S(1)}, bf16[512,2048]{1,0:T(8,128)(2,1)}, u32[]{:S(2)}) copy-start(bf16[512,2048]{1,0:T(8,128)(2,1)} %get-tuple-element.24) | copy-start | bytes 6291460
  166.2 54.6 %all-to-all-start.3 = ((bf16[32,16,2048]{2,1,0:T(8,128)(2,1)}), bf16[32,16,2048]{2,1,0:T(8,128)(2,1)}, u32[]{:S(2)}, u32[]{:S(2)}) async-start(bf16[32,16,2048]{2,1,0:T(8,128)(2,1)} %bitcast.75), calls=%async_computation.3 | async-start | bytes 4194304 | tf_op jit(solution)/shard_map/all_to_all | solution.py:59
  173.7 151.8 %reduce-scatter.2.cloned.1.call-start = ((), (), s32[]{:S(2)}) async-start(), calls=%async_computation.6 | async-start | bytes 7077888 | tf_op jit(solution)/shard_map/reduce_scatter | solution.py:105
  174.1 4.8 %copy-start.3 = (bf16[32,16,2048]{2,1,0:T(8,128)(2,1)S(1)}, bf16[32,16,2048]{2,1,0:T(8,128)(2,1)}, u32[]{:S(2)}) copy-start(bf16[32,16,2048]{2,1,0:T(8,128)(2,1)} %all_to_all.31) | copy-start | bytes 6291460
  174.1 4.8 %copy-start.11 = (bf16[1,2048,768]{2,1,0:T(8,128)(2,1)S(1)}, bf16[1,2048,768]{2,1,0:T(8,128)(2,1)}, u32[]{:S(2)}) copy-start(bf16[1,2048,768]{2,1,0:T(8,128)(2,1)} %param.17) | copy-start | bytes 9437188
  178.9 3.0 copy-start.1
  181.9 1.9 copy-start.10
  226.2 4.1 %copy-start.8 = (bf16[512,768]{1,0:T(8,128)(2,1)}, bf16[512,768]{1,0:T(8,128)(2,1)S(1)}, u32[]{:S(2)}) copy-start(bf16[512,768]{1,0:T(8,128)(2,1)S(1)} %get-tuple-element.20) | copy-start | bytes 2359300
  226.2 10.2 %copy-start.6 = (bf16[512,768]{1,0:T(8,128)(2,1)}, bf16[512,768]{1,0:T(8,128)(2,1)S(1)}, u32[]{:S(2)}) copy-start(bf16[512,768]{1,0:T(8,128)(2,1)S(1)} %get-tuple-element.19) | copy-start | bytes 2359300
  226.2 4.1 %copy-start.2 = (bf16[32,16,2048]{2,1,0:T(8,128)(2,1)S(1)}, bf16[32,16,2048]{2,1,0:T(8,128)(2,1)}, u32[]{:S(2)}) copy-start(bf16[32,16,2048]{2,1,0:T(8,128)(2,1)} %all_to_all.30) | copy-start | bytes 6291460
  230.2 1.4 copy-start.12
  231.7 4.7 %copy-start.4 = (bf16[32,16,2048]{2,1,0:T(8,128)(2,1)S(1)}, bf16[32,16,2048]{2,1,0:T(8,128)(2,1)}, u32[]{:S(2)}) copy-start(bf16[32,16,2048]{2,1,0:T(8,128)(2,1)} %all_to_all.31) | copy-start | bytes 6291460
  250.2 4.0 %copy-start.7 = (bf16[512,768]{1,0:T(8,128)(2,1)S(1)}, bf16[512,768]{1,0:T(8,128)(2,1)}, u32[]{:S(2)}) copy-start(bf16[512,768]{1,0:T(8,128)(2,1)} %copy-done.6) | copy-start | bytes 2359300
  257.4 9.0 %copy-start.9 = (s32[128,2]{0,1:T(2,128)S(1)}, s32[128,2]{0,1:T(2,128)}, u32[]{:S(2)}) copy-start(s32[128,2]{0,1:T(2,128)} %param.13) | copy-start | bytes 3076
  257.4 55.9 %all-to-all-start.4 = ((bf16[32,16,2048]{2,1,0:T(8,128)(2,1)}), bf16[32,16,2048]{2,1,0:T(8,128)(2,1)}, u32[]{:S(2)}, u32[]{:S(2)}) async-start(bf16[32,16,2048]{2,1,0:T(8,128)(2,1)} %bitcast.78), calls=%async_computation.4 | async-start | bytes 4194304 | tf_op jit(solution)/shard_map/all_to_all | solution.py:90
Sparse Core Ops, SparseCore 0:
  250.3 45.9 reduce-scatter.1
where the time goes:
time: 338 us; the launch traced here: 335 us
  blocking collectives  114 us (34%)
  waiting for transfers between devices  80.7 us (24%)
  local copies, waits for them, and re-layouts  40.7 us (12%)
  matrix products  36.8 us (11%)
  starting transfers between devices  28.1 us (8%)
  other arithmetic  20.8 us (6%)
  between operations  14.3 us (4%)
    all_to_all x1, blocking collectives, per_device(): lax.all_to_all(send_cotan, 'expert', split_axis=0, concat_axis=0, tiled=T...  58.3 us
    all_to_all x1, blocking collectives, per_device(): lax.all_to_all(send_primal, 'expert', split_axis=0, concat_axis=0, tiled=...  55.6 us
    all_to_all x1, waiting for transfers between devices, per_device(): lax.all_to_all(input_hvp.reshape(expert_count, capacity, width), 'expert'...  46.7 us
    all_to_all x1, waiting for transfers between devices, per_device(): lax.all_to_all(send_tangent, 'expert', split_axis=0, concat_axis=0, tiled...  34 us
    gather x3, local copies, waits for them, and re-layouts, gather_slots(): picked = jnp.take(rows, safe, axis=0)  19.1 us
    all_to_all x1, starting transfers between devices, per_device(): lax.all_to_all(send_gate, 'expert', split_axis=0, concat_axis=0, tiled=True)  11.6 us
    convert_element_type x1, other arithmetic, per_device(): (jnp.concatenate([first, second], axis=1) * scale).astype(jnp.bfloat16)  9.09 us
    all_to_all x1, starting transfers between devices, per_device(): lax.all_to_all(input_hvp.reshape(expert_count, capacity, width), 'expert'...  8.83 us
  transfers between devices with their start and end apart: 4, of which 2 were waited for; matrix products, arithmetic and copies ran while one was open for 16% of the time, Pallas kernels for 0%

commit v1 on v0

v1 whole, which is shorter than its diff:
```python
import math

import jax
import jax.numpy as jnp
from jax import lax
from jax.sharding import PartitionSpec as P


def slot_matrices(route_ids, gate_rows, expert_count, capacity):
    token_count, route_count = route_ids.shape
    routes_total = token_count * route_count
    slots = expert_count * capacity
    flat_ids = route_ids.reshape(routes_total)
    onehot = (flat_ids[:, None] == jnp.arange(expert_count, dtype=jnp.int32)[None, :]).astype(
        jnp.bfloat16
    )
    order = jnp.arange(routes_total, dtype=jnp.int32)
    earlier = (order[None, :] < order[:, None]).astype(jnp.bfloat16)
    before = jnp.dot(earlier, onehot, preferred_element_type=jnp.float32)
    slot_rank = jnp.sum(before * onehot.astype(jnp.float32), axis=1).astype(jnp.int32)
    target = (flat_ids * capacity + slot_rank).reshape(token_count, route_count)
    slot_ids = jnp.arange(slots, dtype=jnp.int32)
    hit = target[:, :, None] == slot_ids[None, None, :]
    pick = jnp.any(hit, axis=1).astype(jnp.bfloat16)
    gate_pick = jnp.sum(
        jnp.where(hit, gate_rows.astype(jnp.float32)[:, :, None], 0.0), axis=1
    ).astype(jnp.bfloat16)
    return pick, gate_pick


def to_slots(pick, rows):
    return lax.dot_general(
        pick, rows, (((0,), (0,)), ((), ())), preferred_element_type=jnp.float32
    ).astype(jnp.bfloat16)


def per_device(tokens, tangents, cotangents, routes, gates, w_up, w_down, v_up):
    token_count, width = tokens.shape
    route_count = routes.shape[1]
    expert_count = lax.axis_size("expert")
    replicas = lax.axis_size("dp")
    capacity = max(2, token_count * route_count * 2 // expert_count)
    scale = 1.0 / math.sqrt(token_count * route_count * replicas)
    slots = expert_count * capacity
    pick, gate_pick = slot_matrices(routes, gates, expert_count, capacity)
    send_xt = jnp.concatenate([to_slots(pick, tokens), to_slots(pick, tangents)], axis=1)
    send_cot = to_slots(gate_pick, cotangents)
    recv_xt = lax.all_to_all(
        send_xt.reshape(expert_count, capacity, 2 * width),
        "expert",
        split_axis=0,
        concat_axis=0,
        tiled=True,
    ).reshape(slots, 2 * width)
    scaled_cot = lax.all_to_all(
        send_cot.reshape(expert_count, capacity, width),
        "expert",
        split_axis=0,
        concat_axis=0,
        tiled=True,
    ).reshape(slots, width)
    primal = recv_xt[:, :width]
    tangent = recv_xt[:, width:]
    up_proj = w_up[0]
    down_proj = w_down[0]
    dir_up = v_up[0]
    pre_act = jnp.dot(primal, up_proj, preferred_element_type=jnp.float32)
    pre_tan = jnp.dot(tangent, up_proj, preferred_element_type=jnp.float32) + jnp.dot(
        primal, dir_up, preferred_element_type=jnp.float32
    )
    sigmoid_z = jax.nn.sigmoid(pre_act)
    first_der = sigmoid_z * (1.0 + pre_act * (1.0 - sigmoid_z))
    second_der = sigmoid_z * (1.0 - sigmoid_z) * (2.0 + pre_act * (1.0 - 2.0 * sigmoid_z))
    hidden_tan = (first_der * pre_tan).astype(jnp.bfloat16)
    back_hid = jnp.dot(scaled_cot, down_proj.T, preferred_element_type=jnp.float32)
    back_pre = (back_hid * first_der).astype(jnp.bfloat16)
    back_tan = (back_hid * second_der * pre_tan).astype(jnp.bfloat16)
    input_hvp = (
        jnp.dot(back_tan, up_proj.T, preferred_element_type=jnp.float32)
        + jnp.dot(back_pre, dir_up.T, preferred_element_type=jnp.float32)
    ).astype(jnp.bfloat16)
    returned = lax.all_to_all(
        input_hvp.reshape(expert_count, capacity, width),
        "expert",
        split_axis=0,
        concat_axis=0,
        tiled=True,
    ).reshape(slots, width)
    hvp_tokens = jnp.dot(pick, returned, preferred_element_type=jnp.float32).astype(jnp.bfloat16)
    first = jnp.dot(tangent.T, back_pre, preferred_element_type=jnp.float32) + jnp.dot(
        primal.T, back_tan, preferred_element_type=jnp.float32
    )
    second = jnp.dot(scaled_cot.T, hidden_tan, preferred_element_type=jnp.float32)
    summed = lax.psum_scatter(
        (jnp.concatenate([first, second], axis=1) * scale).astype(jnp.bfloat16),
        "dp",
        scatter_dimension=0,
        tiled=True,
    ).astype(jnp.float32)
    hidden_units = up_proj.shape[1]
    hvp_up = summed[:, :hidden_units].astype(jnp.bfloat16)[None]
    hvp_down = summed[:, hidden_units:].T.astype(jnp.bfloat16)[None]
    return (hvp_tokens, hvp_up, hvp_down)


def solution(mesh):
    in_specs = (
        P(("dp", "expert"), None),
        P(("dp", "expert"), None),
        P(("dp", "expert"), None),
        P(("dp", "expert"), None),
        P(("dp", "expert"), None),
        P("expert", None, None),
        P("expert", None, None),
        P("expert", None, None),
    )
    out_specs = (P(("dp", "expert"), None), P("expert", "dp", None), P("expert", None, "dp"))
    return jax.shard_map(
        per_device, mesh=mesh, in_specs=in_specs, out_specs=out_specs, check_vma=False
    )
```

time: 338 us -> 289 us (0.86)
  blocking collectives: 114 us -> 56.4 us
  waiting for transfers between devices: 80.7 us -> 131 us
  local copies, waits for them, and re-layouts: 40.7 us -> 4.12 us
  matrix products: 36.8 us -> 46.2 us
  starting transfers between devices: 28.1 us -> 20.6 us
  other arithmetic: 20.8 us -> 13.6 us
    all_to_all x2 -> x1, blocking collectives: 114 us -> 56.4 us  [per_device(): lax.all_to_all(input_hvp.reshape(expert_count, capacity, width), 'expert'...]
    all_to_all x3 -> x2, waiting for transfers between devices: 80.7 us -> 131 us  [the longest x1 88.4 us: per_device(): lax.all_to_all(send_xt.reshape(expert_count, capacity, 2 * width), 'exper...]
    gather x6 -> x0, local copies, waits for them, and re-layouts: 30.3 us -> none  [the longest x3 19.1 us: gather_slots(): picked = jnp.take(rows, safe, axis=0)]
    all_to_all x3 -> x2, starting transfers between devices: 27.9 us -> 20.4 us  [the longest x1 11.7 us: per_device(): lax.all_to_all(send_cot.reshape(expert_count, capacity, width), 'expert',...]
    dot_general x0 -> x5, matrix products: none -> 7.14 us  [the longest x3 5.69 us: to_slots(): lax.dot_general(pick, rows, (((0,), (0,)), ((), ())), preferred_element_t...]
    select_n x4 -> x0, other arithmetic: 4.85 us -> none  [the longest x1 4.82 us: gather_slots(): return jnp.where(valid[:, None], picked, jnp.zeros_like(picked))]
    reduce_sum x2 -> x1, other arithmetic: 4.49 us -> 0.14 us  [slot_matrices(): jnp.sum(jnp.where(hit, gate_rows.astype(jnp.float32)[:, :, None], 0.0), a...]
  transfers between devices with their start and end apart: 4 -> 3, of which waited for: 2 -> 2; matrix products, arithmetic and copies ran while one was open for 16% -> 6% of each run, Pallas kernels for 0% -> 0%
where the time goes in v1:
time: 289 us; the launch traced here: 286 us
  waiting for transfers between devices  131 us (45%)
  blocking collectives  56.4 us (20%)
  matrix products  46.2 us (16%)
  starting transfers between devices  20.6 us (7%)
  between operations  14.2 us (5%)
  other arithmetic  13.6 us (5%)
  local copies, waits for them, and re-layouts  4.12 us (1%)
    all_to_all x1, waiting for transfers between devices, per_device(): lax.all_to_all(send_xt.reshape(expert_count, capacity, 2 * width), 'exper...  88.4 us
    all_to_all x1, blocking collectives, per_device(): lax.all_to_all(input_hvp.reshape(expert_count, capacity, width), 'expert'...  56.4 us
    all_to_all x1, waiting for transfers between devices, per_device(): lax.all_to_all(send_cot.reshape(expert_count, capacity, width), 'expert',...  42.3 us
    all_to_all x1, starting transfers between devices, per_device(): lax.all_to_all(send_cot.reshape(expert_count, capacity, width), 'expert',...  11.7 us
    convert_element_type x1, other arithmetic, per_device(): (jnp.concatenate([first, second], axis=1) * scale).astype(jnp.bfloat16)  9.32 us
    all_to_all x1, starting transfers between devices, per_device(): lax.all_to_all(send_xt.reshape(expert_count, capacity, 2 * width), 'exper...  8.75 us
    dot_general x1, matrix products, per_device(): jnp.dot(scaled_cot.T, hidden_tan, preferred_element_type=jnp.float32)  6.85 us
    dot_general x1, matrix products, per_device(): jnp.dot(primal.T, back_tan, preferred_element_type=jnp.float32)  6.23 us
  transfers between devices with their start and end apart: 3, of which 2 were waited for; matrix products, arithmetic and copies ran while one was open for 6% of the time, Pallas kernels for 0%

profile of v1, /device:TPU:2, one launch (start us, length us, event | category | flops | bytes accessed | tf_op | source)
XLA Modules:
  0.0 285.9 jit_solution(883334124071068639)
XLA Ops:
  7.2 0.8 convert_element_type.59
  8.0 0.9 copy.24
  10.3 3.1 %convolution_convert_fusion = bf16[512,2048]{1,0:T(8,128)(2,1)} fusion(bf16[128,2048]{1,0:T(8,128)(2,1)} %param.10, bf16[128,512]{1,0:T(8,128)(2,1)S(1)} %select_reduce_fusion), kind=kOutput, calls=%fused_computation.17 | convolution fusion | flops 269484032 | bytes 2752512 | tf_op jit(solution)/shard_map/dot_general | solution.py:32
  13.4 11.7 %all-to-all-start = ((bf16[32,16,2048]{2,1,0:T(8,128)(2,1)}), bf16[32,16,2048]{2,1,0:T(8,128)(2,1)}, u32[]{:S(2)}, u32[]{:S(2)}) async-start(bf16[32,16,2048]{2,1,0:T(8,128)(2,1)} %bitcast.48), calls=%async_computation | async-start | bytes 4194304 | tf_op jit(solution)/shard_map/all_to_all | solution.py:55
  25.3 1.8 convolution_convert_fusion.1
  27.1 0.8 convolution_convert_fusion.2
  27.9 2.5 pad_maximum_fusion
  30.3 42.3 %all-to-all-done = bf16[32,16,2048]{2,1,0:T(8,128)(2,1)} async-done(((bf16[32,16,2048]{2,1,0:T(8,128)(2,1)}), bf16[32,16,2048]{2,1,0:T(8,128)(2,1)}, u32[]{:S(2)}, u32[]{:S(2)}) %all-to-all-start) | async-done | bytes 2097184 | tf_op jit(solution)/shard_map/all_to_all | solution.py:55
  72.7 8.7 %all-to-all-start.1 = ((bf16[32,16,4096]{2,1,0:T(8,128)(2,1)}), bf16[32,16,4096]{2,1,0:T(8,128)(2,1)}, u32[]{:S(2)}, u32[]{:S(2)}) async-start(bf16[32,16,4096]{2,1,0:T(8,128)(2,1)} %bitcast.47), calls=%async_computation.1 | async-start | bytes 8388608 | tf_op jit(solution)/shard_map/all_to_all | solution.py:48
  81.6 5.6 %fusion.11 = f32[512,768]{1,0:T(8,128)} fusion(bf16[512,2048]{1,0:T(8,128)(2,1)} %bitcast.1, bf16[1,768,2048]{2,1,0:T(8,128)(2,1)} %param.14), kind=kOutput, calls=%fused_computation.15 | convolution fusion | flops 1610612736 | bytes 6815744 | tf_op jit(solution)/shard_map/dot_general | solution.py:75
  87.2 88.4 %all-to-all-done.1 = bf16[32,16,4096]{2,1,0:T(8,128)(2,1)} async-done(((bf16[32,16,4096]{2,1,0:T(8,128)(2,1)}), bf16[32,16,4096]{2,1,0:T(8,128)(2,1)}, u32[]{:S(2)}, u32[]{:S(2)}) %all-to-all-start.1) | async-done | bytes 4194336 | tf_op jit(solution)/shard_map/all_to_all | solution.py:48
  175.7 3.5 %fusion.9 = f32[512,768]{1,0:T(8,128)S(1)} fusion(bf16[1,2048,768]{2,1,0:T(8,128)(2,1)S(1)} %copy-done, bf16[512,4096]{1,0:T(8,128)(2,1)} %bitcast.4), kind=kOutput, calls=%fused_computation.13 | convolution fusion | flops 1610612736 | bytes 6815744 | tf_op jit(solution)/shard_map/dot_general | solution.py:67
  179.2 3.6 %fusion.3 = f32[512,768]{1,0:T(8,128)S(1)} fusion(bf16[1,2048,768]{2,1,0:T(8,128)(2,1)S(1)} %copy-done.5, bf16[512,4096]{1,0:T(8,128)(2,1)} %bitcast.4), kind=kOutput, calls=%fused_computation.7 | convolution fusion | flops 1610612736 | bytes 6815744 | tf_op jit(solution)/shard_map/dot_general | solution.py:68
  182.8 4.0 %fusion.24 = (bf16[512,768]{1,0:T(8,128)(2,1)S(1)}, bf16[512,768]{1,0:T(8,128)(2,1)S(1)}, f32[512,768]{1,0:T(8,128)S(1)}) fusion(f32[512,768]{1,0:T(8,128)S(1)} %copy-done.6, f32[512,768]{1,0:T(8,128)S(1)} %fusion.9, f32[512,768]{1,0:T(8,128)S(1)} %fusion.3, bf16[1,2048,768]{2,1,0:T(8,128)(2,1)S(1)} %copy-done, bf16[512,4096]{1,0:T(8,128)(2,1)} %bitcast.4), kind=kOutput, calls=%fused_computation.32 | convolution fusion | flops 1618083840 | bytes 13107200 | tf_op jit(solution)/shard_map/dot_general | solution.py:68
  186.8 6.8 %fusion.33 = f32[2048,768]{0,1:T(8,128)} fusion(bf16[512,2048]{1,0:T(8,128)(2,1)} %bitcast.1, f32[512,768]{1,0:T(8,128)S(1)} %get-tuple-element.19, f32[512,768]{1,0:T(8,128)S(1)} %fusion.9), kind=kOutput, calls=%fused_computation.41 | convolution fusion | flops 1614151680 | bytes 11534336 | tf_op jit(solution)/shard_map/dot_general | solution.py:93
  193.6 3.5 %fusion.15 = f32[2048,768]{0,1:T(8,128)S(1)} fusion(bf16[512,768]{1,0:T(8,128)(2,1)S(1)} %get-tuple-element.16, bf16[512,4096]{1,0:T(8,128)(2,1)} %bitcast.4), kind=kOutput, calls=%fused_computation.23 | convolution fusion | flops 1610612736 | bytes 9175040 | tf_op jit(solution)/shard_map/dot_general | solution.py:90
  197.2 6.2 %convolution_add_fusion = f32[2048,768]{0,1:T(8,128)} fusion(f32[2048,768]{0,1:T(8,128)S(1)} %fusion.15, bf16[512,768]{1,0:T(8,128)(2,1)S(1)} %get-tuple-element.15, bf16[512,4096]{1,0:T(8,128)(2,1)} %bitcast.4), kind=kOutput, calls=%fused_computation.4 | convolution fusion | flops 1612185600 | bytes 15466496 | tf_op jit(solution)/shard_map/dot_general | solution.py:90
  203.4 9.3 %fusion = bf16[2048,1536]{0,1:T(8,128)(2,1)} fusion(f32[2048,768]{0,1:T(8,128)} %fusion.33, f32[2048,768]{0,1:T(8,128)} %convolution_add_fusion), kind=kLoop, calls=%fused_computation.1 | loop fusion | flops 9437184 | bytes 18874368 | tf_op jit(solution)/shard_map/convert_element_type | solution.py:95
  212.7 4.0 %fusion.1 = f32[512,2048]{1,0:T(8,128)S(1)} fusion(bf16[512,768]{1,0:T(8,128)(2,1)} %copy-done.3, bf16[1,2048,768]{2,1,0:T(8,128)(2,1)} %param.15), kind=kOutput, calls=%fused_computation.5 | convolution fusion | flops 1610612736 | bytes 8126464 | tf_op jit(solution)/shard_map/dot_general | solution.py:80
  216.8 1.8 add_convert_fusion
  218.6 56.4 %all_to_all.15 = bf16[32,16,2048]{2,1,0:T(8,128)(2,1)S(1)} all-to-all(bf16[32,16,2048]{2,1,0:T(8,128)(2,1)S(1)} %bitcast.50), channel_id=1, replica_groups=mesh['dp'=8,'expert'=32] {'expert'}, dimensions={0} | all-to-all | bytes 4194304 | tf_op jit(solution)/shard_map/all_to_all | solution.py:82
  275.0 1.2 convolution_convert_fusion.3
  276.2 1.9 slice_bitcast_fusion
  278.2 0.9 copy.26
  (25 shorter events, 1.8 us)
Async XLA Ops:
  7.2 168.5 %copy-start = (bf16[1,2048,768]{2,1,0:T(8,128)(2,1)S(1)}, bf16[1,2048,768]{2,1,0:T(8,128)(2,1)}, u32[]{:S(2)}) copy-start(bf16[1,2048,768]{2,1,0:T(8,128)(2,1)} %param.13) | copy-start | bytes 9437188
  13.4 59.2 %all-to-all-start = ((bf16[32,16,2048]{2,1,0:T(8,128)(2,1)}), bf16[32,16,2048]{2,1,0:T(8,128)(2,1)}, u32[]{:S(2)}, u32[]{:S(2)}) async-start(bf16[32,16,2048]{2,1,0:T(8,128)(2,1)} %bitcast.48), calls=%async_computation | async-start | bytes 4194304 | tf_op jit(solution)/shard_map/all_to_all | solution.py:55
  25.1 2.0 copy-start.4
  72.7 103.0 %all-to-all-start.1 = ((bf16[32,16,4096]{2,1,0:T(8,128)(2,1)}), bf16[32,16,4096]{2,1,0:T(8,128)(2,1)}, u32[]{:S(2)}, u32[]{:S(2)}) async-start(bf16[32,16,4096]{2,1,0:T(8,128)(2,1)} %bitcast.47), calls=%async_computation.1 | async-start | bytes 8388608 | tf_op jit(solution)/shard_map/all_to_all | solution.py:48
  81.4 194.8 %reduce-scatter.2.cloned.1.call-start = ((), (), s32[]{:S(2)}) async-start(), calls=%async_computation.4 | async-start | bytes 7077888 | tf_op jit(solution)/shard_map/reduce_scatter | solution.py:94
  175.7 3.5 %copy-start.5 = (bf16[1,2048,768]{2,1,0:T(8,128)(2,1)S(1)}, bf16[1,2048,768]{2,1,0:T(8,128)(2,1)}, u32[]{:S(2)}) copy-start(bf16[1,2048,768]{2,1,0:T(8,128)(2,1)} %param.15) | copy-start | bytes 9437188
  179.2 3.6 %copy-start.6 = (f32[512,768]{1,0:T(8,128)S(1)}, f32[512,768]{1,0:T(8,128)}, u32[]{:S(2)}) copy-start(f32[512,768]{1,0:T(8,128)} %fusion.11) | copy-start | bytes 4718596
  186.7 6.9 %copy-start.3 = (bf16[512,768]{1,0:T(8,128)(2,1)}, bf16[512,768]{1,0:T(8,128)(2,1)S(1)}, u32[]{:S(2)}) copy-start(bf16[512,768]{1,0:T(8,128)(2,1)S(1)} %get-tuple-element.16) | copy-start | bytes 2359300
  186.8 10.4 %copy-start.1 = (bf16[512,768]{1,0:T(8,128)(2,1)}, bf16[512,768]{1,0:T(8,128)(2,1)S(1)}, u32[]{:S(2)}) copy-start(bf16[512,768]{1,0:T(8,128)(2,1)S(1)} %get-tuple-element.15) | copy-start | bytes 2359300
  212.7 4.0 %copy-start.2 = (bf16[512,768]{1,0:T(8,128)(2,1)S(1)}, bf16[512,768]{1,0:T(8,128)(2,1)}, u32[]{:S(2)}) copy-start(bf16[512,768]{1,0:T(8,128)(2,1)} %copy-done.1) | copy-start | bytes 2359300
Sparse Core Ops, SparseCore 0:
  212.9 45.3 reduce-scatter.1

commit v2 on v1

--- a/solution.py
+++ b/solution.py
@@ -52,6 +52,7 @@
         concat_axis=0,
         tiled=True,
     ).reshape(slots, 2 * width)
+    recv_xt, send_cot = lax.optimization_barrier((recv_xt, send_cot))
     scaled_cot = lax.all_to_all(
         send_cot.reshape(expert_count, capacity, width),
         "expert",
@@ -75,6 +76,10 @@
     back_hid = jnp.dot(scaled_cot, down_proj.T, preferred_element_type=jnp.float32)
     back_pre = (back_hid * first_der).astype(jnp.bfloat16)
     back_tan = (back_hid * second_der * pre_tan).astype(jnp.bfloat16)
+    second = jnp.dot(scaled_cot.T, hidden_tan, preferred_element_type=jnp.float32)
+    down_sum = lax.psum_scatter(
+        (second * scale).astype(jnp.bfloat16), "dp", scatter_dimension=0, tiled=True
+    )
     input_hvp = (
         jnp.dot(back_tan, up_proj.T, preferred_element_type=jnp.float32)
         + jnp.dot(back_pre, dir_up.T, preferred_element_type=jnp.float32)
@@ -90,16 +95,11 @@
     first = jnp.dot(tangent.T, back_pre, preferred_element_type=jnp.float32) + jnp.dot(
         primal.T, back_tan, preferred_element_type=jnp.float32
     )
-    second = jnp.dot(scaled_cot.T, hidden_tan, preferred_element_type=jnp.float32)
-    summed = lax.psum_scatter(
-        (jnp.concatenate([first, second], axis=1) * scale).astype(jnp.bfloat16),
-        "dp",
-        scatter_dimension=0,
-        tiled=True,
-    ).astype(jnp.float32)
-    hidden_units = up_proj.shape[1]
-    hvp_up = summed[:, :hidden_units].astype(jnp.bfloat16)[None]
-    hvp_down = summed[:, hidden_units:].T.astype(jnp.bfloat16)[None]
+    up_sum = lax.psum_scatter(
+        (first * scale).astype(jnp.bfloat16), "dp", scatter_dimension=0, tiled=True
+    )
+    hvp_up = up_sum[None]
+    hvp_down = down_sum.T[None]
     return (hvp_tokens, hvp_up, hvp_down)
 
 

time: 289 us -> 278 us (0.962); the launches traced: 286 us -> 278 us
  other arithmetic: 13.6 us -> 3.49 us
  waiting for transfers between devices: 131 us -> 134 us
    convert_element_type x1 -> x0, other arithmetic: 9.32 us -> none  [per_device(): (jnp.concatenate([first, second], axis=1) * scale).astype(jnp.bfloat16)]
    reduce_scatter x1 -> x2, waiting for transfers between devices: 0.01 us -> 4.57 us  [the longest x1 4.57 us: per_device(): lax.psum_scatter((first * scale).astype(jnp.bfloat16), 'dp', scatter_dime...]
    all_to_all x1, waiting for transfers between devices: 42.3 us -> 37.9 us  [per_device(): lax.all_to_all(send_cot.reshape(expert_count, capacity, width), 'expert',...]
    all_to_all x1, starting transfers between devices: 11.7 us -> 7.79 us  [per_device(): lax.all_to_all(send_cot.reshape(expert_count, capacity, width), 'expert',...]
    all_to_all x1, starting transfers between devices: 8.75 us -> 11.8 us  [per_device(): lax.all_to_all(send_xt.reshape(expert_count, capacity, 2 * width), 'exper...]
  transfers between devices with their start and end apart: 3 -> 4, of which waited for: 2 -> 3; matrix products, arithmetic and copies ran while one was open for 6% -> 11% of each run, Pallas kernels for 0% -> 0%
where the time goes in v2:
time: 278 us
  waiting for transfers between devices  134 us (48%)
  blocking collectives  57 us (21%)
  matrix products  46.2 us (17%)
  starting transfers between devices  20.1 us (7%)
  between operations  14.2 us (5%)
  other arithmetic  3.49 us (1%)
  local copies, waits for them, and re-layouts  3.23 us (1%)
    all_to_all x1, waiting for transfers between devices, per_device(): lax.all_to_all(send_xt.reshape(expert_count, capacity, 2 * width), 'exper...  91.2 us
    all_to_all x1, blocking collectives, per_device(): lax.all_to_all(input_hvp.reshape(expert_count, capacity, width), 'expert'...  57 us
    all_to_all x1, waiting for transfers between devices, per_device(): lax.all_to_all(send_cot.reshape(expert_count, capacity, width), 'expert',...  37.9 us
    all_to_all x1, starting transfers between devices, per_device(): lax.all_to_all(send_xt.reshape(expert_count, capacity, 2 * width), 'exper...  11.8 us
    all_to_all x1, starting transfers between devices, per_device(): lax.all_to_all(send_cot.reshape(expert_count, capacity, width), 'expert',...  7.79 us
    dot_general x3, matrix products, to_slots(): lax.dot_general(pick, rows, (((0,), (0,)), ((), ())), preferred_element_t...  5.64 us
  transfers between devices with their start and end apart: 4, of which 3 were waited for; matrix products, arithmetic and copies ran while one was open for 11% of the time, Pallas kernels for 0%

profile of v2, /device:TPU:2, one launch (start us, length us, event | category | flops | bytes accessed | tf_op | source)
XLA Modules:
  0.0 277.9 jit_solution(2888575966059512122)
XLA Ops:
  7.2 0.9 copy.24
  8.7 0.8 multiply_add_fusion
  9.6 1.8 convolution_convert_fusion.1
  11.4 0.8 convolution_convert_fusion.2
  12.1 2.5 pad_maximum_fusion
  14.6 11.8 %all-to-all-start = ((bf16[32,16,4096]{2,1,0:T(8,128)(2,1)}), bf16[32,16,4096]{2,1,0:T(8,128)(2,1)}, u32[]{:S(2)}, u32[]{:S(2)}) async-start(bf16[32,16,4096]{2,1,0:T(8,128)(2,1)} %bitcast.45), calls=%async_computation | async-start | bytes 8388608 | tf_op jit(solution)/shard_map/all_to_all | solution.py:48
  26.6 3.1 %convolution_convert_fusion = bf16[512,2048]{1,0:T(8,128)(2,1)} fusion(bf16[128,2048]{1,0:T(8,128)(2,1)} %param.10, bf16[128,512]{1,0:T(8,128)(2,1)S(1)} %select_reduce_fusion), kind=kOutput, calls=%fused_computation.16 | convolution fusion | flops 269484032 | bytes 2752512 | tf_op jit(solution)/shard_map/dot_general | solution.py:32
  29.7 91.2 %all-to-all-done = bf16[32,16,4096]{2,1,0:T(8,128)(2,1)} async-done(((bf16[32,16,4096]{2,1,0:T(8,128)(2,1)}), bf16[32,16,4096]{2,1,0:T(8,128)(2,1)}, u32[]{:S(2)}, u32[]{:S(2)}) %all-to-all-start) | async-done | bytes 4194336 | tf_op jit(solution)/shard_map/all_to_all | solution.py:48
  120.9 7.8 %all-to-all-start.1 = ((bf16[32,16,2048]{2,1,0:T(8,128)(2,1)}), bf16[32,16,2048]{2,1,0:T(8,128)(2,1)}, u32[]{:S(2)}, u32[]{:S(2)}) async-start(bf16[32,16,2048]{2,1,0:T(8,128)(2,1)} %bitcast.46), calls=%async_computation.1 | async-start | bytes 4194304 | tf_op jit(solution)/shard_map/all_to_all | solution.py:56
  129.0 4.7 %fusion.8 = f32[512,768]{1,0:T(8,128)} fusion(bf16[1,2048,768]{2,1,0:T(8,128)(2,1)S(1)} %copy-done, bf16[512,4096]{1,0:T(8,128)(2,1)} %bitcast.1), kind=kOutput, calls=%fused_computation.12 | convolution fusion | flops 1610612736 | bytes 6815744 | tf_op jit(solution)/shard_map/dot_general | solution.py:68
  133.7 4.6 %fusion.2 = f32[512,768]{1,0:T(8,128)} fusion(bf16[1,2048,768]{2,1,0:T(8,128)(2,1)S(1)} %copy-done.4, bf16[512,4096]{1,0:T(8,128)(2,1)} %bitcast.1), kind=kOutput, calls=%fused_computation.6 | convolution fusion | flops 1610612736 | bytes 6815744 | tf_op jit(solution)/shard_map/dot_general | solution.py:69
  138.3 37.9 %all-to-all-done.1 = bf16[32,16,2048]{2,1,0:T(8,128)(2,1)} async-done(((bf16[32,16,2048]{2,1,0:T(8,128)(2,1)}), bf16[32,16,2048]{2,1,0:T(8,128)(2,1)}, u32[]{:S(2)}, u32[]{:S(2)}) %all-to-all-start.1) | async-done | bytes 2097184 | tf_op jit(solution)/shard_map/all_to_all | solution.py:56
  176.2 4.5 %fusion.10 = f32[512,768]{1,0:T(8,128)S(1)} fusion(bf16[512,2048]{1,0:T(8,128)(2,1)} %bitcast.3, bf16[1,768,2048]{2,1,0:T(8,128)(2,1)} %param.14), kind=kOutput, calls=%fused_computation.14 | convolution fusion | flops 1610612736 | bytes 6815744 | tf_op jit(solution)/shard_map/dot_general | solution.py:76
  180.7 5.1 %fusion.23 = (bf16[512,768]{1,0:T(8,128)(2,1)}, bf16[512,768]{1,0:T(8,128)(2,1)}, f32[512,768]{1,0:T(8,128)S(1)}) fusion(f32[512,768]{1,0:T(8,128)S(1)} %fusion.10, f32[512,768]{1,0:T(8,128)S(1)} %copy-done.6, f32[512,768]{1,0:T(8,128)S(1)} %copy-done.7, bf16[1,2048,768]{2,1,0:T(8,128)(2,1)S(1)} %copy-done, bf16[512,4096]{1,0:T(8,128)(2,1)} %bitcast.1), kind=kOutput, calls=%fused_computation.31 | convolution fusion | flops 1618083840 | bytes 13107200 | tf_op jit(solution)/shard_map/dot_general | solution.py:69
  185.8 5.3 %multiply_convert_fusion = bf16[2048,768]{1,0:T(8,128)(2,1)} fusion(bf16[512,2048]{1,0:T(8,128)(2,1)} %bitcast.3, f32[512,768]{1,0:T(8,128)S(1)} %get-tuple-element.21, f32[512,768]{1,0:T(8,128)S(1)} %copy-done.6), kind=kOutput, calls=%fused_computation | convolution fusion | flops 1617297408 | bytes 8388608 | tf_op jit(solution)/shard_map/dot_general | solution.py:79
  191.1 0.3 reduce-scatter.3.cloned.1.call-start
  191.4 3.7 %fusion.14 = f32[2048,768]{1,0:T(8,128)S(1)} fusion(bf16[512,768]{1,0:T(8,128)(2,1)} %get-tuple-element.20, bf16[512,4096]{1,0:T(8,128)(2,1)} %bitcast.1), kind=kOutput, calls=%fused_computation.22 | convolution fusion | flops 1610612736 | bytes 9175040 | tf_op jit(solution)/shard_map/dot_general | solution.py:95
  195.1 5.4 %multiply_convert_fusion.1 = bf16[2048,768]{1,0:T(8,128)(2,1)} fusion(f32[2048,768]{1,0:T(8,128)S(1)} %fusion.14, bf16[512,768]{1,0:T(8,128)(2,1)S(1)} %copy-done.1, bf16[512,4096]{1,0:T(8,128)(2,1)} %bitcast.1), kind=kOutput, calls=%fused_computation.1 | convolution fusion | flops 1615331328 | bytes 12320768 | tf_op jit(solution)/shard_map/dot_general | solution.py:95
  200.5 4.0 %fusion = f32[512,2048]{1,0:T(8,128)S(1)} fusion(bf16[512,768]{1,0:T(8,128)(2,1)} %get-tuple-element.20, bf16[1,2048,768]{2,1,0:T(8,128)(2,1)} %param.15), kind=kOutput, calls=%fused_computation.4 | convolution fusion | flops 1610612736 | bytes 8126464 | tf_op jit(solution)/shard_map/dot_general | solution.py:85
  204.5 1.8 add_convert_fusion
  206.4 57.0 %all_to_all.15 = bf16[32,16,2048]{2,1,0:T(8,128)(2,1)S(1)} all-to-all(bf16[32,16,2048]{2,1,0:T(8,128)(2,1)S(1)} %bitcast.48), channel_id=1, replica_groups=mesh['dp'=8,'expert'=32] {'expert'}, dimensions={0} | all-to-all | bytes 4194304 | tf_op jit(solution)/shard_map/all_to_all | solution.py:87
  263.4 1.2 convolution_convert_fusion.3
  264.6 1.9 copy.26
  266.5 4.6 %reduce-scatter.3.cloned.1.call-done = bf16[256,768]{1,0:T(8,128)(2,1)} async-done(((bf16[2048,768]{1,0:T(8,128)(2,1)}), bf16[256,768]{1,0:T(8,128)(2,1)}) %reduce-scatter.3.cloned.1.call-update) | async-done | bytes 393232 | tf_op jit(solution)/shard_map/reduce_scatter | solution.py:98
  (28 shorter events, 1.1 us)
Async XLA Ops:
  7.2 121.8 %copy-start = (bf16[1,2048,768]{2,1,0:T(8,128)(2,1)S(1)}, bf16[1,2048,768]{2,1,0:T(8,128)(2,1)}, u32[]{:S(2)}) copy-start(bf16[1,2048,768]{2,1,0:T(8,128)(2,1)} %param.13) | copy-start | bytes 9437188
  8.7 2.7 copy-start.3
  14.6 11.8 %copy-start.5 = (bf16[128,2]{0,1:T(2,128)(2,1)S(1)}, bf16[128,2]{0,1:T(2,128)(2,1)}, u32[]{:S(2)}) copy-start(bf16[128,2]{0,1:T(2,128)(2,1)} %param.12) | copy-start | bytes 1540
  14.6 106.3 %all-to-all-start = ((bf16[32,16,4096]{2,1,0:T(8,128)(2,1)}), bf16[32,16,4096]{2,1,0:T(8,128)(2,1)}, u32[]{:S(2)}, u32[]{:S(2)}) async-start(bf16[32,16,4096]{2,1,0:T(8,128)(2,1)} %bitcast.45), calls=%async_computation | async-start | bytes 8388608 | tf_op jit(solution)/shard_map/all_to_all | solution.py:48
  120.9 55.3 %all-to-all-start.1 = ((bf16[32,16,2048]{2,1,0:T(8,128)(2,1)}), bf16[32,16,2048]{2,1,0:T(8,128)(2,1)}, u32[]{:S(2)}, u32[]{:S(2)}) async-start(bf16[32,16,2048]{2,1,0:T(8,128)(2,1)} %bitcast.46), calls=%async_computation.1 | async-start | bytes 4194304 | tf_op jit(solution)/shard_map/all_to_all | solution.py:56
  128.7 135.9 %reduce-scatter.5.cloned.1.call-start = ((), (), s32[]{:S(2)}) async-start(), calls=%async_computation.6 | async-start | bytes 3538944 | tf_op jit(solution)/shard_map/reduce_scatter | solution.py:80
  128.9 4.7 %copy-start.4 = (bf16[1,2048,768]{2,1,0:T(8,128)(2,1)S(1)}, bf16[1,2048,768]{2,1,0:T(8,128)(2,1)}, u32[]{:S(2)}) copy-start(bf16[1,2048,768]{2,1,0:T(8,128)(2,1)} %param.15) | copy-start | bytes 9437188
  176.2 4.5 %copy-start.6 = (f32[512,768]{1,0:T(8,128)S(1)}, f32[512,768]{1,0:T(8,128)}, u32[]{:S(2)}) copy-start(f32[512,768]{1,0:T(8,128)} %fusion.8) | copy-start | bytes 4718596
  176.2 4.5 %copy-start.7 = (f32[512,768]{1,0:T(8,128)S(1)}, f32[512,768]{1,0:T(8,128)}, u32[]{:S(2)}) copy-start(f32[512,768]{1,0:T(8,128)} %fusion.2) | copy-start | bytes 4718596
  191.1 80.0 %reduce-scatter.3.cloned.1.call-start = ((), (), s32[]{:S(2)}) async-start(), calls=%async_computation.5 | async-start | bytes 3538944 | tf_op jit(solution)/shard_map/reduce_scatter | solution.py:98
  191.4 3.7 %copy-start.1 = (bf16[512,768]{1,0:T(8,128)(2,1)S(1)}, bf16[512,768]{1,0:T(8,128)(2,1)}, u32[]{:S(2)}) copy-start(bf16[512,768]{1,0:T(8,128)(2,1)} %get-tuple-element.19) | copy-start | bytes 2359300
  200.5 4.1 %copy-start.2 = (bf16[512,768]{1,0:T(8,128)(2,1)S(1)}, bf16[512,768]{1,0:T(8,128)(2,1)}, u32[]{:S(2)}) copy-start(bf16[512,768]{1,0:T(8,128)(2,1)} %get-tuple-element.19) | copy-start | bytes 2359300
Sparse Core Ops, SparseCore 0:
  191.2 38.7 reduce-scatter.4
  233.1 37.9 reduce-scatter.2

commit v3 on v2

--- a/solution.py
+++ b/solution.py
@@ -43,47 +43,42 @@
     scale = 1.0 / math.sqrt(token_count * route_count * replicas)
     slots = expert_count * capacity
     pick, gate_pick = slot_matrices(routes, gates, expert_count, capacity)
-    send_xt = jnp.concatenate([to_slots(pick, tokens), to_slots(pick, tangents)], axis=1)
-    send_cot = to_slots(gate_pick, cotangents)
-    recv_xt = lax.all_to_all(
-        send_xt.reshape(expert_count, capacity, 2 * width),
+    send_xg = jnp.concatenate([to_slots(pick, tokens), to_slots(gate_pick, cotangents)], axis=1)
+    send_tan = to_slots(pick, tangents)
+    recv_xg = lax.all_to_all(
+        send_xg.reshape(expert_count, capacity, 2 * width),
         "expert",
         split_axis=0,
         concat_axis=0,
         tiled=True,
     ).reshape(slots, 2 * width)
-    recv_xt, send_cot = lax.optimization_barrier((recv_xt, send_cot))
-    scaled_cot = lax.all_to_all(
-        send_cot.reshape(expert_count, capacity, width),
+    recv_xg, send_tan = lax.optimization_barrier((recv_xg, send_tan))
+    tangent = lax.all_to_all(
+        send_tan.reshape(expert_count, capacity, width),
         "expert",
         split_axis=0,
         concat_axis=0,
         tiled=True,
     ).reshape(slots, width)
-    primal = recv_xt[:, :width]
-    tangent = recv_xt[:, width:]
+    primal = recv_xg[:, :width]
+    scaled_cot = recv_xg[:, width:]
     up_proj = w_up[0]
     down_proj = w_down[0]
     dir_up = v_up[0]
     pre_act = jnp.dot(primal, up_proj, preferred_element_type=jnp.float32)
-    pre_tan = jnp.dot(tangent, up_proj, preferred_element_type=jnp.float32) + jnp.dot(
-        primal, dir_up, preferred_element_type=jnp.float32
-    )
     sigmoid_z = jax.nn.sigmoid(pre_act)
     first_der = sigmoid_z * (1.0 + pre_act * (1.0 - sigmoid_z))
     second_der = sigmoid_z * (1.0 - sigmoid_z) * (2.0 + pre_act * (1.0 - 2.0 * sigmoid_z))
-    hidden_tan = (first_der * pre_tan).astype(jnp.bfloat16)
     back_hid = jnp.dot(scaled_cot, down_proj.T, preferred_element_type=jnp.float32)
     back_pre = (back_hid * first_der).astype(jnp.bfloat16)
+    pre_mix = jnp.dot(primal, dir_up, preferred_element_type=jnp.float32)
+    hvp_mix = jnp.dot(back_pre, dir_up.T, preferred_element_type=jnp.float32)
+    pre_tan = jnp.dot(tangent, up_proj, preferred_element_type=jnp.float32) + pre_mix
+    hidden_tan = (first_der * pre_tan).astype(jnp.bfloat16)
     back_tan = (back_hid * second_der * pre_tan).astype(jnp.bfloat16)
-    second = jnp.dot(scaled_cot.T, hidden_tan, preferred_element_type=jnp.float32)
-    down_sum = lax.psum_scatter(
-        (second * scale).astype(jnp.bfloat16), "dp", scatter_dimension=0, tiled=True
+    input_hvp = (jnp.dot(back_tan, up_proj.T, preferred_element_type=jnp.float32) + hvp_mix).astype(
+        jnp.bfloat16
     )
-    input_hvp = (
-        jnp.dot(back_tan, up_proj.T, preferred_element_type=jnp.float32)
-        + jnp.dot(back_pre, dir_up.T, preferred_element_type=jnp.float32)
-    ).astype(jnp.bfloat16)
     returned = lax.all_to_all(
         input_hvp.reshape(expert_count, capacity, width),
         "expert",
@@ -91,6 +86,10 @@
         concat_axis=0,
         tiled=True,
     ).reshape(slots, width)
+    second = jnp.dot(scaled_cot.T, hidden_tan, preferred_element_type=jnp.float32)
+    down_sum = lax.psum_scatter(
+        (second * scale).astype(jnp.bfloat16), "dp", scatter_dimension=0, tiled=True
+    )
     hvp_tokens = jnp.dot(pick, returned, preferred_element_type=jnp.float32).astype(jnp.bfloat16)
     first = jnp.dot(tangent.T, back_pre, preferred_element_type=jnp.float32) + jnp.dot(
         primal.T, back_tan, preferred_element_type=jnp.float32

time: 278 us -> 276 us (level)
  waiting for transfers between devices: 134 us -> 129 us
    all_to_all x2, waiting for transfers between devices: 129 us -> 124 us  [the longest x1 91.4 us: per_device(): lax.all_to_all(send_xg.reshape(expert_count, capacity, 2 * width), 'exper...]
  transfers between devices with their start and end apart: 4 -> 4, of which waited for: 3 -> 3; matrix products, arithmetic and copies ran while one was open for 11% -> 13% of each run, Pallas kernels for 0% -> 0%
where the time goes in v3:
time: 276 us; the launch traced here: 275 us
  waiting for transfers between devices  129 us (47%)
  blocking collectives  56.8 us (21%)
  matrix products  48.2 us (17%)
  starting transfers between devices  19.9 us (7%)
  between operations  14.2 us (5%)
  other arithmetic  4.3 us (2%)
  local copies, waits for them, and re-layouts  3.21 us (1%)
    all_to_all x1, waiting for transfers between devices, per_device(): lax.all_to_all(send_xg.reshape(expert_count, capacity, 2 * width), 'exper...  91.4 us
    all_to_all x1, blocking collectives, per_device(): lax.all_to_all(input_hvp.reshape(expert_count, capacity, width), 'expert'...  56.8 us
    all_to_all x1, waiting for transfers between devices, per_device(): lax.all_to_all(send_tan.reshape(expert_count, capacity, width), 'expert',...  33.1 us
    all_to_all x1, starting transfers between devices, per_device(): lax.all_to_all(send_xg.reshape(expert_count, capacity, 2 * width), 'exper...  11.7 us
    all_to_all x1, starting transfers between devices, per_device(): lax.all_to_all(send_tan.reshape(expert_count, capacity, width), 'expert',...  7.8 us
    dot_general x1, matrix products, per_device(): jnp.dot(tangent, up_proj, preferred_element_type=jnp.float32) + pre_mix  6.63 us
    dot_general x3, matrix products, to_slots(): lax.dot_general(pick, rows, (((0,), (0,)), ((), ())), preferred_element_t...  5.64 us
  transfers between devices with their start and end apart: 4, of which 3 were waited for; matrix products, arithmetic and copies ran while one was open for 13% of the time, Pallas kernels for 0%

profile of v3, /device:TPU:2, one launch (start us, length us, event | category | flops | bytes accessed | tf_op | source)
XLA Modules:
  0.0 275.4 jit_solution(12960942737241848981)
XLA Ops:
  7.2 0.8 convert_element_type.57
  8.0 0.9 copy.24
  9.5 0.8 multiply_add_fusion
  10.5 1.8 convolution_convert_fusion
  12.3 0.8 convolution_convert_fusion.2
  13.1 2.5 pad_maximum_fusion
  15.5 11.7 %all-to-all-start = ((bf16[32,16,4096]{2,1,0:T(8,128)(2,1)}), bf16[32,16,4096]{2,1,0:T(8,128)(2,1)}, u32[]{:S(2)}, u32[]{:S(2)}) async-start(bf16[32,16,4096]{2,1,0:T(8,128)(2,1)} %bitcast.45), calls=%async_computation | async-start | bytes 8388608 | tf_op jit(solution)/shard_map/all_to_all | solution.py:48
  27.2 3.1 %convolution_convert_fusion.1 = bf16[512,2048]{1,0:T(8,128)(2,1)} fusion(pred[128,512]{1,0:T(8,128)(4,1)S(1)} %fusion.29, bf16[128,2048]{1,0:T(8,128)(2,1)} %param.9), kind=kOutput, calls=%fused_computation.17 | convolution fusion | flops 269484032 | bytes 2686976 | tf_op jit(solution)/shard_map/dot_general | solution.py:32
  30.3 91.4 %all-to-all-done = bf16[32,16,4096]{2,1,0:T(8,128)(2,1)} async-done(((bf16[32,16,4096]{2,1,0:T(8,128)(2,1)}), bf16[32,16,4096]{2,1,0:T(8,128)(2,1)}, u32[]{:S(2)}, u32[]{:S(2)}) %all-to-all-start) | async-done | bytes 4194336 | tf_op jit(solution)/shard_map/all_to_all | solution.py:48
  121.7 7.8 %all-to-all-start.1 = ((bf16[32,16,2048]{2,1,0:T(8,128)(2,1)}), bf16[32,16,2048]{2,1,0:T(8,128)(2,1)}, u32[]{:S(2)}, u32[]{:S(2)}) async-start(bf16[32,16,2048]{2,1,0:T(8,128)(2,1)} %bitcast.46), calls=%async_computation.1 | async-start | bytes 4194304 | tf_op jit(solution)/shard_map/all_to_all | solution.py:56
  129.8 4.7 %fusion.8 = f32[512,768]{1,0:T(8,128)} fusion(bf16[1,2048,768]{2,1,0:T(8,128)(2,1)S(1)} %copy-done, bf16[512,4096]{1,0:T(8,128)(2,1)} %bitcast.1), kind=kOutput, calls=%fused_computation.12 | convolution fusion | flops 1610612736 | bytes 6815744 | tf_op jit(solution)/shard_map/dot_general | solution.py:68
  134.5 4.8 %fusion.2 = f32[512,768]{1,0:T(8,128)} fusion(bf16[1,2048,768]{2,1,0:T(8,128)(2,1)S(1)} %copy-done.5, bf16[512,4096]{1,0:T(8,128)(2,1)} %bitcast.1), kind=kOutput, calls=%fused_computation.6 | convolution fusion | flops 1610612736 | bytes 6815744 | tf_op jit(solution)/shard_map/dot_general | solution.py:74
  139.3 4.6 %fusion.10 = f32[512,768]{1,0:T(8,128)} fusion(bf16[1,768,2048]{2,1,0:T(8,128)(2,1)S(1)} %copy-done.4, bf16[512,4096]{1,0:T(8,128)(2,1)} %bitcast.1), kind=kOutput, calls=%fused_computation.14 | convolution fusion | flops 1610612736 | bytes 6815744 | tf_op jit(solution)/shard_map/dot_general | solution.py:72
  143.9 33.1 %all-to-all-done.1 = bf16[32,16,2048]{2,1,0:T(8,128)(2,1)} async-done(((bf16[32,16,2048]{2,1,0:T(8,128)(2,1)}), bf16[32,16,2048]{2,1,0:T(8,128)(2,1)}, u32[]{:S(2)}, u32[]{:S(2)}) %all-to-all-start.1) | async-done | bytes 2097184 | tf_op jit(solution)/shard_map/all_to_all | solution.py:56
  177.0 6.6 %fusion.22 = (bf16[512,768]{1,0:T(8,128)(2,1)}, bf16[512,768]{1,0:T(8,128)(2,1)}, f32[512,768]{1,0:T(8,128)S(1)}) fusion(f32[512,768]{1,0:T(8,128)} %fusion.10, f32[512,768]{1,0:T(8,128)} %fusion.8, f32[512,768]{1,0:T(8,128)} %fusion.2, bf16[512,2048]{1,0:T(8,128)(2,1)} %bitcast.5, bf16[1,2048,768]{2,1,0:T(8,128)(2,1)S(1)} %copy-done), kind=kOutput, calls=%fused_computation.30 | convolution fusion | flops 1618083840 | bytes 13107200 | tf_op jit(solution)/shard_map/dot_general | solution.py:76
  183.6 5.3 %multiply_convert_fusion = bf16[2048,768]{1,0:T(8,128)(2,1)} fusion(bf16[512,4096]{1,0:T(8,128)(2,1)} %bitcast.1, f32[512,768]{1,0:T(8,128)S(1)} %get-tuple-element.21, f32[512,768]{1,0:T(8,128)S(1)} %copy-done.6), kind=kOutput, calls=%fused_computation | convolution fusion | flops 1617297408 | bytes 8388608 | tf_op jit(solution)/shard_map/dot_general | solution.py:89
  189.2 3.7 %fusion.34 = f32[2048,768]{1,0:T(8,128)S(1)} fusion(bf16[512,2048]{1,0:T(8,128)(2,1)} %bitcast.5, bf16[512,768]{1,0:T(8,128)(2,1)} %get-tuple-element.20), kind=kOutput, calls=%fused_computation.48 | convolution fusion | flops 1610612736 | bytes 9175040 | tf_op jit(solution)/shard_map/dot_general | solution.py:94
  192.9 5.4 %multiply_convert_fusion.1 = bf16[2048,768]{1,0:T(8,128)(2,1)} fusion(f32[2048,768]{1,0:T(8,128)S(1)} %fusion.34, bf16[512,768]{1,0:T(8,128)(2,1)S(1)} %copy-done.1, bf16[512,4096]{1,0:T(8,128)(2,1)} %bitcast.1), kind=kOutput, calls=%fused_computation.1 | convolution fusion | flops 1615331328 | bytes 12320768 | tf_op jit(solution)/shard_map/dot_general | solution.py:94
  198.3 4.2 %fusion = f32[512,2048]{1,0:T(8,128)S(1)} fusion(bf16[512,768]{1,0:T(8,128)(2,1)} %get-tuple-element.20, bf16[1,2048,768]{2,1,0:T(8,128)(2,1)} %param.15), kind=kOutput, calls=%fused_computation.4 | convolution fusion | flops 1610612736 | bytes 8126464 | tf_op jit(solution)/shard_map/dot_general | solution.py:75
  202.5 1.8 add_convert_fusion
  204.4 56.8 %all_to_all.15 = bf16[32,16,2048]{2,1,0:T(8,128)(2,1)S(1)} all-to-all(bf16[32,16,2048]{2,1,0:T(8,128)(2,1)S(1)} %bitcast.48), channel_id=1, replica_groups=mesh['dp'=8,'expert'=32] {'expert'}, dimensions={0} | all-to-all | bytes 4194304 | tf_op jit(solution)/shard_map/all_to_all | solution.py:82
  261.2 1.2 convolution_convert_fusion.3
  262.4 1.9 copy.26
  264.3 4.3 %reduce-scatter.3.cloned.1.call-done = bf16[256,768]{1,0:T(8,128)(2,1)} async-done(((bf16[2048,768]{1,0:T(8,128)(2,1)}), bf16[256,768]{1,0:T(8,128)(2,1)}) %reduce-scatter.3.cloned.1.call-update) | async-done | bytes 393232 | tf_op jit(solution)/shard_map/reduce_scatter | solution.py:97
  (26 shorter events, 1.3 us)
Async XLA Ops:
  7.2 122.6 %copy-start = (bf16[1,2048,768]{2,1,0:T(8,128)(2,1)S(1)}, bf16[1,2048,768]{2,1,0:T(8,128)(2,1)}, u32[]{:S(2)}) copy-start(bf16[1,2048,768]{2,1,0:T(8,128)(2,1)} %param.13) | copy-start | bytes 9437188
  9.5 2.8 %copy-start.3 = (bf16[128,2048]{1,0:T(8,128)(2,1)S(1)}, bf16[128,2048]{1,0:T(8,128)(2,1)}, u32[]{:S(2)}) copy-start(bf16[128,2048]{1,0:T(8,128)(2,1)} %param.8) | copy-start | bytes 1572868
  15.5 106.2 %all-to-all-start = ((bf16[32,16,4096]{2,1,0:T(8,128)(2,1)}), bf16[32,16,4096]{2,1,0:T(8,128)(2,1)}, u32[]{:S(2)}, u32[]{:S(2)}) async-start(bf16[32,16,4096]{2,1,0:T(8,128)(2,1)} %bitcast.45), calls=%async_computation | async-start | bytes 8388608 | tf_op jit(solution)/shard_map/all_to_all | solution.py:48
  121.7 55.3 %all-to-all-start.1 = ((bf16[32,16,2048]{2,1,0:T(8,128)(2,1)}), bf16[32,16,2048]{2,1,0:T(8,128)(2,1)}, u32[]{:S(2)}, u32[]{:S(2)}) async-start(bf16[32,16,2048]{2,1,0:T(8,128)(2,1)} %bitcast.46), calls=%async_computation.1 | async-start | bytes 4194304 | tf_op jit(solution)/shard_map/all_to_all | solution.py:56
  129.5 132.9 %reduce-scatter.5.cloned.1.call-start = ((), (), s32[]{:S(2)}) async-start(), calls=%async_computation.6 | async-start | bytes 3538944 | tf_op jit(solution)/shard_map/reduce_scatter | solution.py:90
  129.7 4.7 %copy-start.5 = (bf16[1,2048,768]{2,1,0:T(8,128)(2,1)S(1)}, bf16[1,2048,768]{2,1,0:T(8,128)(2,1)}, u32[]{:S(2)}) copy-start(bf16[1,2048,768]{2,1,0:T(8,128)(2,1)} %param.15) | copy-start | bytes 9437188
  134.5 4.8 %copy-start.4 = (bf16[1,768,2048]{2,1,0:T(8,128)(2,1)S(1)}, bf16[1,768,2048]{2,1,0:T(8,128)(2,1)}, u32[]{:S(2)}) copy-start(bf16[1,768,2048]{2,1,0:T(8,128)(2,1)} %param.14) | copy-start | bytes 9437188
  177.0 6.6 %copy-start.6 = (f32[512,768]{1,0:T(8,128)S(1)}, f32[512,768]{1,0:T(8,128)}, u32[]{:S(2)}) copy-start(f32[512,768]{1,0:T(8,128)} %fusion.8) | copy-start | bytes 4718596
  188.9 79.7 %reduce-scatter.3.cloned.1.call-start = ((), (), s32[]{:S(2)}) async-start(), calls=%async_computation.5 | async-start | bytes 3538944 | tf_op jit(solution)/shard_map/reduce_scatter | solution.py:97
  189.2 3.7 %copy-start.1 = (bf16[512,768]{1,0:T(8,128)(2,1)S(1)}, bf16[512,768]{1,0:T(8,128)(2,1)}, u32[]{:S(2)}) copy-start(bf16[512,768]{1,0:T(8,128)(2,1)} %get-tuple-element.19) | copy-start | bytes 2359300
  198.3 4.2 %copy-start.2 = (bf16[512,768]{1,0:T(8,128)(2,1)S(1)}, bf16[512,768]{1,0:T(8,128)(2,1)}, u32[]{:S(2)}) copy-start(bf16[512,768]{1,0:T(8,128)(2,1)} %get-tuple-element.19) | copy-start | bytes 2359300
Sparse Core Ops, SparseCore 0:
  189.0 38.4 reduce-scatter.4
  230.7 37.8 reduce-scatter.2

commit v4 on v3

--- a/solution.py
+++ b/solution.py
@@ -86,19 +86,20 @@
         concat_axis=0,
         tiled=True,
     ).reshape(slots, width)
-    second = jnp.dot(scaled_cot.T, hidden_tan, preferred_element_type=jnp.float32)
-    down_sum = lax.psum_scatter(
-        (second * scale).astype(jnp.bfloat16), "dp", scatter_dimension=0, tiled=True
-    )
     hvp_tokens = jnp.dot(pick, returned, preferred_element_type=jnp.float32).astype(jnp.bfloat16)
     first = jnp.dot(tangent.T, back_pre, preferred_element_type=jnp.float32) + jnp.dot(
         primal.T, back_tan, preferred_element_type=jnp.float32
     )
-    up_sum = lax.psum_scatter(
-        (first * scale).astype(jnp.bfloat16), "dp", scatter_dimension=0, tiled=True
+    second = jnp.dot(scaled_cot.T, hidden_tan, preferred_element_type=jnp.float32)
+    summed = lax.psum_scatter(
+        (jnp.concatenate([first, second], axis=1) * scale).astype(jnp.bfloat16),
+        "dp",
+        scatter_dimension=0,
+        tiled=True,
     )
-    hvp_up = up_sum[None]
-    hvp_down = down_sum.T[None]
+    hidden_units = up_proj.shape[1]
+    hvp_up = summed[:, :hidden_units][None]
+    hvp_down = summed[:, hidden_units:].T[None]
     return (hvp_tokens, hvp_up, hvp_down)
 
 

time: 276 us -> 285 us (1.033)
  other arithmetic: 4.3 us -> 13.6 us
  waiting for transfers between devices: 129 us -> 125 us
    convert_element_type x0 -> x1, other arithmetic: none -> 9.31 us  [per_device(): (jnp.concatenate([first, second], axis=1) * scale).astype(jnp.bfloat16)]
    reduce_scatter x2 -> x1, waiting for transfers between devices: 4.28 us -> 0.01 us  [per_device(): lax.psum_scatter((jnp.concatenate([first, second], axis=1) * scale).astyp...]
  transfers between devices with their start and end apart: 4 -> 3, of which waited for: 3 -> 2; matrix products, arithmetic and copies ran while one was open for 13% -> 9% of each run, Pallas kernels for 0% -> 0%
where the time goes in v4:
time: 285 us; the launch traced here: 282 us
  waiting for transfers between devices  125 us (44%)
  blocking collectives  56.9 us (20%)
  matrix products  49.2 us (17%)
  starting transfers between devices  19.6 us (7%)
  between operations  14.2 us (5%)
  other arithmetic  13.6 us (5%)
  local copies, waits for them, and re-layouts  4.13 us (1%)
    all_to_all x1, waiting for transfers between devices, per_device(): lax.all_to_all(send_xg.reshape(expert_count, capacity, 2 * width), 'exper...  91.3 us
    all_to_all x1, blocking collectives, per_device(): lax.all_to_all(input_hvp.reshape(expert_count, capacity, width), 'expert'...  56.9 us
    all_to_all x1, waiting for transfers between devices, per_device(): lax.all_to_all(send_tan.reshape(expert_count, capacity, width), 'expert',...  33.2 us
    all_to_all x1, starting transfers between devices, per_device(): lax.all_to_all(send_xg.reshape(expert_count, capacity, 2 * width), 'exper...  11.7 us
    convert_element_type x1, other arithmetic, per_device(): (jnp.concatenate([first, second], axis=1) * scale).astype(jnp.bfloat16)  9.31 us
    all_to_all x1, starting transfers between devices, per_device(): lax.all_to_all(send_tan.reshape(expert_count, capacity, width), 'expert',...  7.68 us
    dot_general x1, matrix products, per_device(): jnp.dot(scaled_cot.T, hidden_tan, preferred_element_type=jnp.float32)  6.88 us
    dot_general x1, matrix products, per_device(): jnp.dot(primal.T, back_tan, preferred_element_type=jnp.float32)  6.23 us
  transfers between devices with their start and end apart: 3, of which 2 were waited for; matrix products, arithmetic and copies ran while one was open for 9% of the time, Pallas kernels for 0%

profile of v4, /device:TPU:2, one launch (start us, length us, event | category | flops | bytes accessed | tf_op | source)
XLA Modules:
  0.0 282.1 jit_solution(16887454856874216750)
XLA Ops:
  7.2 0.8 convert_element_type.54
  8.0 0.9 copy.24
  9.5 0.8 multiply_add_fusion
  10.5 1.8 convolution_convert_fusion
  13.1 2.5 pad_maximum_fusion
  15.5 11.7 %all-to-all-start = ((bf16[32,16,4096]{2,1,0:T(8,128)(2,1)}), bf16[32,16,4096]{2,1,0:T(8,128)(2,1)}, u32[]{:S(2)}, u32[]{:S(2)}) async-start(bf16[32,16,4096]{2,1,0:T(8,128)(2,1)} %bitcast.47), calls=%async_computation | async-start | bytes 8388608 | tf_op jit(solution)/shard_map/all_to_all | solution.py:48
  27.2 3.2 %convolution_convert_fusion.1 = bf16[512,2048]{1,0:T(8,128)(2,1)} fusion(pred[128,512]{1,0:T(8,128)(4,1)S(1)} %fusion.31, bf16[128,2048]{1,0:T(8,128)(2,1)} %param.9), kind=kOutput, calls=%fused_computation.18 | convolution fusion | flops 269484032 | bytes 2686976 | tf_op jit(solution)/shard_map/dot_general | solution.py:32
  30.4 91.3 %all-to-all-done = bf16[32,16,4096]{2,1,0:T(8,128)(2,1)} async-done(((bf16[32,16,4096]{2,1,0:T(8,128)(2,1)}), bf16[32,16,4096]{2,1,0:T(8,128)(2,1)}, u32[]{:S(2)}, u32[]{:S(2)}) %all-to-all-start) | async-done | bytes 4194336 | tf_op jit(solution)/shard_map/all_to_all | solution.py:48
  121.7 7.7 %all-to-all-start.1 = ((bf16[32,16,2048]{2,1,0:T(8,128)(2,1)}), bf16[32,16,2048]{2,1,0:T(8,128)(2,1)}, u32[]{:S(2)}, u32[]{:S(2)}) async-start(bf16[32,16,2048]{2,1,0:T(8,128)(2,1)} %bitcast.48), calls=%async_computation.1 | async-start | bytes 4194304 | tf_op jit(solution)/shard_map/all_to_all | solution.py:56
  129.7 4.7 %fusion.9 = f32[512,768]{1,0:T(8,128)} fusion(bf16[1,2048,768]{2,1,0:T(8,128)(2,1)S(1)} %copy-done, bf16[512,4096]{1,0:T(8,128)(2,1)} %bitcast.1), kind=kOutput, calls=%fused_computation.13 | convolution fusion | flops 1610612736 | bytes 6815744 | tf_op jit(solution)/shard_map/dot_general | solution.py:68
  134.3 4.8 %fusion.3 = f32[512,768]{1,0:T(8,128)} fusion(bf16[1,2048,768]{2,1,0:T(8,128)(2,1)S(1)} %copy-done.6, bf16[512,4096]{1,0:T(8,128)(2,1)} %bitcast.1), kind=kOutput, calls=%fused_computation.7 | convolution fusion | flops 1610612736 | bytes 6815744 | tf_op jit(solution)/shard_map/dot_general | solution.py:74
  139.1 4.6 %fusion.11 = f32[512,768]{1,0:T(8,128)} fusion(bf16[1,768,2048]{2,1,0:T(8,128)(2,1)S(1)} %copy-done.5, bf16[512,4096]{1,0:T(8,128)(2,1)} %bitcast.1), kind=kOutput, calls=%fused_computation.15 | convolution fusion | flops 1610612736 | bytes 6815744 | tf_op jit(solution)/shard_map/dot_general | solution.py:72
  143.7 33.2 %all-to-all-done.1 = bf16[32,16,2048]{2,1,0:T(8,128)(2,1)} async-done(((bf16[32,16,2048]{2,1,0:T(8,128)(2,1)}), bf16[32,16,2048]{2,1,0:T(8,128)(2,1)}, u32[]{:S(2)}, u32[]{:S(2)}) %all-to-all-start.1) | async-done | bytes 2097184 | tf_op jit(solution)/shard_map/all_to_all | solution.py:56
  176.9 5.5 %fusion.24 = (bf16[512,768]{1,0:T(8,128)(2,1)S(1)}, bf16[512,768]{1,0:T(8,128)(2,1)S(1)}, f32[512,768]{1,0:T(8,128)S(1)}) fusion(f32[512,768]{1,0:T(8,128)} %fusion.11, f32[512,768]{1,0:T(8,128)} %fusion.9, f32[512,768]{1,0:T(8,128)} %fusion.3, bf16[512,2048]{1,0:T(8,128)(2,1)} %bitcast.5, bf16[1,2048,768]{2,1,0:T(8,128)(2,1)S(1)} %copy-done), kind=kOutput, calls=%fused_computation.32 | convolution fusion | flops 1618083840 | bytes 13107200 | tf_op jit(solution)/shard_map/dot_general | solution.py:76
  182.4 6.9 %fusion.15 = f32[2048,768]{0,1:T(8,128)} fusion(bf16[512,4096]{1,0:T(8,128)(2,1)} %bitcast.1, f32[512,768]{1,0:T(8,128)S(1)} %get-tuple-element.23, f32[512,768]{1,0:T(8,128)S(1)} %copy-done.7), kind=kOutput, calls=%fused_computation.23 | convolution fusion | flops 1614151680 | bytes 11534336 | tf_op jit(solution)/shard_map/dot_general | solution.py:93
  189.3 3.5 %fusion.36 = f32[2048,768]{0,1:T(8,128)S(1)} fusion(bf16[512,2048]{1,0:T(8,128)(2,1)} %bitcast.5, bf16[512,768]{1,0:T(8,128)(2,1)S(1)} %get-tuple-element.20), kind=kOutput, calls=%fused_computation.52 | convolution fusion | flops 1610612736 | bytes 9175040 | tf_op jit(solution)/shard_map/dot_general | solution.py:90
  192.8 6.2 %convolution_add_fusion = f32[2048,768]{0,1:T(8,128)} fusion(f32[2048,768]{0,1:T(8,128)S(1)} %fusion.36, bf16[512,768]{1,0:T(8,128)(2,1)S(1)} %get-tuple-element.19, bf16[512,4096]{1,0:T(8,128)(2,1)} %bitcast.1), kind=kOutput, calls=%fused_computation.4 | convolution fusion | flops 1612185600 | bytes 15466496 | tf_op jit(solution)/shard_map/dot_general | solution.py:90
  199.1 9.3 %fusion = bf16[2048,1536]{0,1:T(8,128)(2,1)} fusion(f32[2048,768]{0,1:T(8,128)} %fusion.15, f32[2048,768]{0,1:T(8,128)} %convolution_add_fusion), kind=kLoop, calls=%fused_computation.1 | loop fusion | flops 9437184 | bytes 18874368 | tf_op jit(solution)/shard_map/convert_element_type | solution.py:95
  208.4 4.0 %fusion.1 = f32[512,2048]{1,0:T(8,128)S(1)} fusion(bf16[512,768]{1,0:T(8,128)(2,1)} %copy-done.3, bf16[1,2048,768]{2,1,0:T(8,128)(2,1)} %param.15), kind=kOutput, calls=%fused_computation.5 | convolution fusion | flops 1610612736 | bytes 8126464 | tf_op jit(solution)/shard_map/dot_general | solution.py:75
  212.4 1.8 add_convert_fusion
  214.3 56.9 %all_to_all.15 = bf16[32,16,2048]{2,1,0:T(8,128)(2,1)S(1)} all-to-all(bf16[32,16,2048]{2,1,0:T(8,128)(2,1)S(1)} %bitcast.50), channel_id=1, replica_groups=mesh['dp'=8,'expert'=32] {'expert'}, dimensions={0} | all-to-all | bytes 4194304 | tf_op jit(solution)/shard_map/all_to_all | solution.py:82
  271.2 1.2 convolution_convert_fusion.3
  272.4 1.9 slice_bitcast_fusion
  274.4 0.9 copy.26
  (27 shorter events, 1.8 us)
Async XLA Ops:
  7.2 122.5 %copy-start = (bf16[1,2048,768]{2,1,0:T(8,128)(2,1)S(1)}, bf16[1,2048,768]{2,1,0:T(8,128)(2,1)}, u32[]{:S(2)}) copy-start(bf16[1,2048,768]{2,1,0:T(8,128)(2,1)} %param.13) | copy-start | bytes 9437188
  9.5 2.8 copy-start.4
  15.5 106.2 %all-to-all-start = ((bf16[32,16,4096]{2,1,0:T(8,128)(2,1)}), bf16[32,16,4096]{2,1,0:T(8,128)(2,1)}, u32[]{:S(2)}, u32[]{:S(2)}) async-start(bf16[32,16,4096]{2,1,0:T(8,128)(2,1)} %bitcast.47), calls=%async_computation | async-start | bytes 8388608 | tf_op jit(solution)/shard_map/all_to_all | solution.py:48
  121.7 55.2 %all-to-all-start.1 = ((bf16[32,16,2048]{2,1,0:T(8,128)(2,1)}), bf16[32,16,2048]{2,1,0:T(8,128)(2,1)}, u32[]{:S(2)}, u32[]{:S(2)}) async-start(bf16[32,16,2048]{2,1,0:T(8,128)(2,1)} %bitcast.48), calls=%async_computation.1 | async-start | bytes 4194304 | tf_op jit(solution)/shard_map/all_to_all | solution.py:56
  129.4 143.0 %reduce-scatter.2.cloned.1.call-start = ((), (), s32[]{:S(2)}) async-start(), calls=%async_computation.4 | async-start | bytes 7077888 | tf_op jit(solution)/shard_map/reduce_scatter | solution.py:94
  129.6 4.7 %copy-start.6 = (bf16[1,2048,768]{2,1,0:T(8,128)(2,1)S(1)}, bf16[1,2048,768]{2,1,0:T(8,128)(2,1)}, u32[]{:S(2)}) copy-start(bf16[1,2048,768]{2,1,0:T(8,128)(2,1)} %param.15) | copy-start | bytes 9437188
  134.3 4.8 %copy-start.5 = (bf16[1,768,2048]{2,1,0:T(8,128)(2,1)S(1)}, bf16[1,768,2048]{2,1,0:T(8,128)(2,1)}, u32[]{:S(2)}) copy-start(bf16[1,768,2048]{2,1,0:T(8,128)(2,1)} %param.14) | copy-start | bytes 9437188
  176.9 5.5 %copy-start.7 = (f32[512,768]{1,0:T(8,128)S(1)}, f32[512,768]{1,0:T(8,128)}, u32[]{:S(2)}) copy-start(f32[512,768]{1,0:T(8,128)} %fusion.9) | copy-start | bytes 4718596
  182.4 6.9 %copy-start.3 = (bf16[512,768]{1,0:T(8,128)(2,1)}, bf16[512,768]{1,0:T(8,128)(2,1)S(1)}, u32[]{:S(2)}) copy-start(bf16[512,768]{1,0:T(8,128)(2,1)S(1)} %get-tuple-element.20) | copy-start | bytes 2359300
  182.4 10.5 %copy-start.1 = (bf16[512,768]{1,0:T(8,128)(2,1)}, bf16[512,768]{1,0:T(8,128)(2,1)S(1)}, u32[]{:S(2)}) copy-start(bf16[512,768]{1,0:T(8,128)(2,1)S(1)} %get-tuple-element.19) | copy-start | bytes 2359300
  208.4 4.0 %copy-start.2 = (bf16[512,768]{1,0:T(8,128)(2,1)S(1)}, bf16[512,768]{1,0:T(8,128)(2,1)}, u32[]{:S(2)}) copy-start(bf16[512,768]{1,0:T(8,128)(2,1)} %copy-done.1) | copy-start | bytes 2359300
Sparse Core Ops, SparseCore 0:
  208.5 45.7 reduce-scatter.1

commit v5 on v3

--- a/solution.py
+++ b/solution.py
@@ -32,6 +32,25 @@
     return lax.dot_general(
         pick, rows, (((0,), (0,)), ((), ())), preferred_element_type=jnp.float32
     ).astype(jnp.bfloat16)
+
+
+def reduce_over_dp(part, replicas):
+    half = replicas // 2
+    me = lax.axis_index("dp")
+    core = me % 2
+    row = me // 2
+    blocks = part.reshape(half, 2, part.shape[0] // replicas, part.shape[1])
+    keep = lax.dynamic_index_in_dim(blocks, core, axis=1, keepdims=False)
+    give = lax.dynamic_index_in_dim(blocks, 1 - core, axis=1, keepdims=False)
+    got = lax.ppermute(give, "dp", [(i, i ^ 1) for i in range(replicas)])
+    partial = keep.astype(jnp.float32) + got.astype(jnp.float32)
+    wire = partial.astype(jnp.bfloat16)
+    total = lax.dynamic_index_in_dim(partial, row, axis=0, keepdims=False)
+    for step in range(1, half):
+        send = lax.dynamic_index_in_dim(wire, (row + step) % half, axis=0, keepdims=False)
+        pairs = [(i, (i + 2 * step) % replicas) for i in range(replicas)]
+        total = total + lax.ppermute(send, "dp", pairs).astype(jnp.float32)
+    return total.astype(jnp.bfloat16)
 
 
 def per_device(tokens, tangents, cotangents, routes, gates, w_up, w_down, v_up):
@@ -87,16 +106,12 @@
         tiled=True,
     ).reshape(slots, width)
     second = jnp.dot(scaled_cot.T, hidden_tan, preferred_element_type=jnp.float32)
-    down_sum = lax.psum_scatter(
-        (second * scale).astype(jnp.bfloat16), "dp", scatter_dimension=0, tiled=True
-    )
+    down_sum = reduce_over_dp((second * scale).astype(jnp.bfloat16), replicas)
     hvp_tokens = jnp.dot(pick, returned, preferred_element_type=jnp.float32).astype(jnp.bfloat16)
     first = jnp.dot(tangent.T, back_pre, preferred_element_type=jnp.float32) + jnp.dot(
         primal.T, back_tan, preferred_element_type=jnp.float32
     )
-    up_sum = lax.psum_scatter(
-        (first * scale).astype(jnp.bfloat16), "dp", scatter_dimension=0, tiled=True
-    )
+    up_sum = reduce_over_dp((first * scale).astype(jnp.bfloat16), replicas)
     hvp_up = up_sum[None]
     hvp_down = down_sum.T[None]
     return (hvp_tokens, hvp_up, hvp_down)

time: 276 us -> 262 us (0.949)
  blocking collectives: 56.8 us -> 0 us
  starting transfers between devices: 19.9 us -> 36.8 us
  local copies, waits for them, and re-layouts: 3.21 us -> 16.7 us
  between operations: 14.2 us -> 0.86 us
  waiting for transfers between devices: 129 us -> 142 us
  other arithmetic: 4.3 us -> 14.5 us
    all_to_all x1 -> x0, blocking collectives: 56.8 us -> none  [per_device(): lax.all_to_all(input_hvp.reshape(expert_count, capacity, width), 'expert'...]
    ppermute x0 -> x8, waiting for transfers between devices: none -> 17.3 us  [the longest x6 17.3 us: reduce_over_dp(): total = total + lax.ppermute(send, 'dp', pairs).astype(jnp.float32)]
    dynamic_slice x0 -> x6, local copies, waits for them, and re-layouts: none -> 9 us  [the longest x4 5.79 us: reduce_over_dp(): lax.dynamic_index_in_dim(wire, (row + step) % half, axis=0, keepdims=False)]
    ppermute x0 -> x8, starting transfers between devices: none -> 8.8 us  [the longest x6 8.79 us: reduce_over_dp(): total = total + lax.ppermute(send, 'dp', pairs).astype(jnp.float32)]
    all_to_all x0 -> x1, starting transfers between devices: none -> 8.65 us  [per_device(): lax.all_to_all(input_hvp.reshape(expert_count, capacity, width), 'expert'...]
    convert_element_type x0 -> x2, other arithmetic: none -> 5.47 us  [reduce_over_dp(): wire = partial.astype(jnp.bfloat16)]
    broadcast_in_dim x0 -> x2, other arithmetic: none -> 4.7 us  [the longest x1 2.55 us: per_device(): hvp_up = up_sum[None]]
    reduce_scatter x2 -> x0, waiting for transfers between devices: 4.28 us -> none  [the longest x1 4.28 us: per_device(): lax.psum_scatter((first * scale).astype(jnp.bfloat16), 'dp', scatter_dime...]
  transfers between devices with their start and end apart: 4 -> 11, of which waited for: 3 -> 6; matrix products, arithmetic and copies ran while one was open for 13% -> 19% of each run, Pallas kernels for 0% -> 0%
where the time goes in v5:
time: 262 us; the launch traced here: 261 us
  waiting for transfers between devices  142 us (54%)
  matrix products  49.7 us (19%)
  starting transfers between devices  36.8 us (14%)
  local copies, waits for them, and re-layouts  16.7 us (6%)
  other arithmetic  14.5 us (6%)
    all_to_all x1, waiting for transfers between devices, per_device(): lax.all_to_all(send_xg.reshape(expert_count, capacity, 2 * width), 'exper...  91.4 us
    all_to_all x1, waiting for transfers between devices, per_device(): lax.all_to_all(send_tan.reshape(expert_count, capacity, width), 'expert',...  33.4 us
    ppermute x6, waiting for transfers between devices, reduce_over_dp(): total = total + lax.ppermute(send, 'dp', pairs).astype(jnp.float32)  17.3 us
    all_to_all x1, starting transfers between devices, per_device(): lax.all_to_all(send_xg.reshape(expert_count, capacity, 2 * width), 'exper...  11.7 us
    ppermute x6, starting transfers between devices, reduce_over_dp(): total = total + lax.ppermute(send, 'dp', pairs).astype(jnp.float32)  8.79 us
    all_to_all x1, starting transfers between devices, per_device(): lax.all_to_all(input_hvp.reshape(expert_count, capacity, width), 'expert'...  8.65 us
    all_to_all x1, starting transfers between devices, per_device(): lax.all_to_all(send_tan.reshape(expert_count, capacity, width), 'expert',...  7.66 us
    dot_general x1, matrix products, per_device(): jnp.dot(tangent, up_proj, preferred_element_type=jnp.float32) + pre_mix  6.43 us
  transfers between devices with their start and end apart: 11, of which 6 were waited for; matrix products, arithmetic and copies ran while one was open for 19% of the time, Pallas kernels for 0%

profile of v5, /device:TPU:2, one launch (start us, length us, event | category | flops | bytes accessed | tf_op | source)
XLA Modules:
  0.0 260.6 jit_solution(6522305407023125453)
XLA Ops:
  6.5 2.5 pad_maximum_fusion
  9.0 11.7 %all-to-all-start = ((bf16[32,16,4096]{2,1,0:T(8,128)(2,1)}), bf16[32,16,4096]{2,1,0:T(8,128)(2,1)}, u32[]{:S(2)}, u32[]{:S(2)}) async-start(bf16[32,16,4096]{2,1,0:T(8,128)(2,1)} %bitcast.90), calls=%async_computation | async-start | bytes 8388608 | tf_op jit(solution)/shard_map/all_to_all | solution.py:67
  20.7 3.1 %convolution_convert_fusion.1 = bf16[512,2048]{1,0:T(8,128)(2,1)} fusion(pred[128,512]{1,0:T(8,128)(4,1)S(1)} %fusion.35, bf16[128,2048]{1,0:T(8,128)(2,1)} %param.9), kind=kOutput, calls=%fused_computation.19 | convolution fusion | flops 269484032 | bytes 2686976 | tf_op jit(solution)/shard_map/dot_general | solution.py:32
  23.8 91.4 %all-to-all-done = bf16[32,16,4096]{2,1,0:T(8,128)(2,1)} async-done(((bf16[32,16,4096]{2,1,0:T(8,128)(2,1)}), bf16[32,16,4096]{2,1,0:T(8,128)(2,1)}, u32[]{:S(2)}, u32[]{:S(2)}) %all-to-all-start) | async-done | bytes 4194336 | tf_op jit(solution)/shard_map/all_to_all | solution.py:67
  115.2 7.7 %all-to-all-start.1 = ((bf16[32,16,2048]{2,1,0:T(8,128)(2,1)}), bf16[32,16,2048]{2,1,0:T(8,128)(2,1)}, u32[]{:S(2)}, u32[]{:S(2)}) async-start(bf16[32,16,2048]{2,1,0:T(8,128)(2,1)} %bitcast.93), calls=%async_computation.1 | async-start | bytes 4194304 | tf_op jit(solution)/shard_map/all_to_all | solution.py:75
  122.9 4.7 %fusion.8 = f32[512,768]{1,0:T(8,128)} fusion(bf16[1,2048,768]{2,1,0:T(8,128)(2,1)S(1)} %copy-done, bf16[512,4096]{1,0:T(8,128)(2,1)} %bitcast.1), kind=kOutput, calls=%fused_computation.14 | convolution fusion | flops 1610612736 | bytes 6815744 | tf_op jit(solution)/shard_map/dot_general | solution.py:87
  127.7 4.8 %fusion.2 = f32[512,768]{1,0:T(8,128)} fusion(bf16[1,2048,768]{2,1,0:T(8,128)(2,1)S(1)} %copy-done.10, bf16[512,4096]{1,0:T(8,128)(2,1)} %bitcast.1), kind=kOutput, calls=%fused_computation.8 | convolution fusion | flops 1610612736 | bytes 6815744 | tf_op jit(solution)/shard_map/dot_general | solution.py:93
  132.5 4.6 %fusion.10 = f32[512,768]{1,0:T(8,128)} fusion(bf16[1,768,2048]{2,1,0:T(8,128)(2,1)S(1)} %copy-done.9, bf16[512,4096]{1,0:T(8,128)(2,1)} %bitcast.1), kind=kOutput, calls=%fused_computation.16 | convolution fusion | flops 1610612736 | bytes 6815744 | tf_op jit(solution)/shard_map/dot_general | solution.py:91
  137.1 33.4 %all-to-all-done.1 = bf16[32,16,2048]{2,1,0:T(8,128)(2,1)} async-done(((bf16[32,16,2048]{2,1,0:T(8,128)(2,1)}), bf16[32,16,2048]{2,1,0:T(8,128)(2,1)}, u32[]{:S(2)}, u32[]{:S(2)}) %all-to-all-start.1) | async-done | bytes 2097184 | tf_op jit(solution)/shard_map/all_to_all | solution.py:75
  170.4 6.4 %fusion.22 = (bf16[512,768]{1,0:T(8,128)(2,1)S(1)}, bf16[512,768]{1,0:T(8,128)(2,1)S(1)}, f32[512,768]{1,0:T(8,128)}) fusion(f32[512,768]{1,0:T(8,128)} %fusion.10, f32[512,768]{1,0:T(8,128)} %fusion.8, f32[512,768]{1,0:T(8,128)} %fusion.2, bf16[512,2048]{1,0:T(8,128)(2,1)} %bitcast.5, bf16[1,2048,768]{2,1,0:T(8,128)(2,1)S(1)} %copy-done), kind=kOutput, calls=%fused_computation.32 | convolution fusion | flops 1618083840 | bytes 13107200 | tf_op jit(solution)/shard_map/dot_general | solution.py:95
  176.9 6.4 %fusion.44 = f32[2048,768]{1,0:T(8,128)} fusion(bf16[512,2048]{1,0:T(8,128)(2,1)} %bitcast.5, bf16[512,768]{1,0:T(8,128)(2,1)S(1)} %get-tuple-element.12), kind=kOutput, calls=%fused_computation.71 | convolution fusion | flops 1610612736 | bytes 9175040 | tf_op jit(solution)/shard_map/dot_general | solution.py:111
  185.1 3.1 %add_convert_fusion = bf16[512,2048]{1,0:T(8,128)(2,1)} fusion(f32[512,2048]{1,0:T(8,128)S(1)} %fusion, bf16[512,768]{1,0:T(8,128)(2,1)S(1)} %get-tuple-element.11, bf16[1,2048,768]{2,1,0:T(8,128)(2,1)S(1)} %copy-done), kind=kOutput, calls=%fused_computation.3 | convolution fusion | flops 1612709888 | bytes 10223616 | tf_op jit(solution)/shard_map/dot_general | solution.py:98
  188.3 8.6 %all-to-all-start.2 = ((bf16[32,16,2048]{2,1,0:T(8,128)(2,1)}), bf16[32,16,2048]{2,1,0:T(8,128)(2,1)}, u32[]{:S(2)}, u32[]{:S(2)}) async-start(bf16[32,16,2048]{2,1,0:T(8,128)(2,1)} %bitcast.96), calls=%async_computation.2 | async-start | bytes 4194304 | tf_op jit(solution)/shard_map/all_to_all | solution.py:101
  196.9 5.5 %multiply_convert_fusion.1 = bf16[2048,768]{1,0:T(8,128)(2,1)S(1)} fusion(f32[2048,768]{1,0:T(8,128)} %fusion.44, bf16[512,768]{1,0:T(8,128)(2,1)} %copy-done.7, bf16[512,4096]{1,0:T(8,128)(2,1)} %bitcast.1), kind=kOutput, calls=%fused_computation.1 | convolution fusion | flops 1615331328 | bytes 12320768 | tf_op jit(solution)/shard_map/dot_general | solution.py:111
  204.9 3.6 %multiply_convert_fusion = bf16[2048,768]{1,0:T(8,128)(2,1)S(1)} fusion(bf16[512,4096]{1,0:T(8,128)(2,1)} %bitcast.1, f32[512,768]{1,0:T(8,128)S(1)} %copy-done.13, f32[512,768]{1,0:T(8,128)S(1)} %copy-done.12), kind=kOutput, calls=%fused_computation | convolution fusion | flops 1617297408 | bytes 8388608 | tf_op jit(solution)/shard_map/dot_general | solution.py:108
  211.4 3.7 %fusion.43 = (bf16[4,256,768]{2,1,0:T(8,128)(2,1)S(1)}, f32[4,256,768]{2,1,0:T(8,128)}) fusion(bf16[4,256,768]{2,1,0:T(8,128)(2,1)} %collective-permute-done, bf16[4,2,256,768]{3,2,1,0:T(8,128)(2,1)S(1)} %bitcast.92, s32[]{:T(128)S(6)} %select_n.65), kind=kLoop, calls=%fused_computation.70 | loop fusion | flops 3145728 | bytes 7864324 | tf_op jit(solution)/shard_map/convert_element_type | solution.py:47
  224.1 1.9 copy.36
  226.0 1.9 copy.38
  233.5 2.3 copy.35
  235.8 8.9 %collective-permute-done.3 = bf16[256,768]{1,0:T(8,128)(2,1)} collective-permute-done((bf16[256,768]{1,0:T(8,128)(2,1)}, bf16[256,768]{1,0:T(8,128)(2,1)}, u32[]{:S(2)}, u32[]{:S(2)}) %collective-permute-start.3) | collective-permute-done | bytes 393248 | tf_op jit(solution)/shard_map/ppermute | solution.py:52
  244.7 2.6 fusion.36
  247.7 6.8 %collective-permute-done.7 = bf16[256,768]{0,1:T(8,128)(2,1)} collective-permute-done((bf16[256,768]{0,1:T(8,128)(2,1)}, bf16[256,768]{0,1:T(8,128)(2,1)}, u32[]{:S(2)}, u32[]{:S(2)}) %collective-permute-start.7) | collective-permute-done | bytes 393248 | tf_op jit(solution)/shard_map/ppermute | solution.py:52
  255.6 2.1 fusion.37
  257.7 2.8 %convolution_convert_fusion.3 = bf16[128,2048]{1,0:T(8,128)(2,1)} fusion(pred[128,512]{1,0:T(8,128)(4,1)S(1)} %copy-done.6, bf16[512,2048]{1,0:T(8,128)(2,1)} %bitcast.8), kind=kOutput, calls=%fused_computation.21 | convolution fusion | flops 268697600 | bytes 2686976 | tf_op jit(solution)/shard_map/dot_general | solution.py:110
  (63 shorter events, 29.1 us)
Async XLA Ops:
  0.6 122.3 %copy-start = (bf16[1,2048,768]{2,1,0:T(8,128)(2,1)S(1)}, bf16[1,2048,768]{2,1,0:T(8,128)(2,1)}, u32[]{:S(2)}) copy-start(bf16[1,2048,768]{2,1,0:T(8,128)(2,1)} %param.13) | copy-start | bytes 9437188
  2.9 2.8 %copy-start.8 = (bf16[128,2048]{1,0:T(8,128)(2,1)S(1)}, bf16[128,2048]{1,0:T(8,128)(2,1)}, u32[]{:S(2)}) copy-start(bf16[128,2048]{1,0:T(8,128)(2,1)} %param.8) | copy-start | bytes 1572868
  3.8 16.9 %copy-start.5 = (pred[128,512]{1,0:T(8,128)(4,1)}, pred[128,512]{1,0:T(8,128)(4,1)S(1)}, u32[]{:S(2)}) copy-start(pred[128,512]{1,0:T(8,128)(4,1)S(1)} %fusion.35) | copy-start | bytes 196612
  9.0 106.2 %all-to-all-start = ((bf16[32,16,4096]{2,1,0:T(8,128)(2,1)}), bf16[32,16,4096]{2,1,0:T(8,128)(2,1)}, u32[]{:S(2)}, u32[]{:S(2)}) async-start(bf16[32,16,4096]{2,1,0:T(8,128)(2,1)} %bitcast.90), calls=%async_computation | async-start | bytes 8388608 | tf_op jit(solution)/shard_map/all_to_all | solution.py:67
  115.2 55.2 %all-to-all-start.1 = ((bf16[32,16,2048]{2,1,0:T(8,128)(2,1)}), bf16[32,16,2048]{2,1,0:T(8,128)(2,1)}, u32[]{:S(2)}, u32[]{:S(2)}) async-start(bf16[32,16,2048]{2,1,0:T(8,128)(2,1)} %bitcast.93), calls=%async_computation.1 | async-start | bytes 4194304 | tf_op jit(solution)/shard_map/all_to_all | solution.py:75
  122.9 4.7 %copy-start.10 = (bf16[1,2048,768]{2,1,0:T(8,128)(2,1)S(1)}, bf16[1,2048,768]{2,1,0:T(8,128)(2,1)}, u32[]{:S(2)}) copy-start(bf16[1,2048,768]{2,1,0:T(8,128)(2,1)} %param.15) | copy-start | bytes 9437188
  127.7 4.8 %copy-start.9 = (bf16[1,768,2048]{2,1,0:T(8,128)(2,1)S(1)}, bf16[1,768,2048]{2,1,0:T(8,128)(2,1)}, u32[]{:S(2)}) copy-start(bf16[1,768,2048]{2,1,0:T(8,128)(2,1)} %param.14) | copy-start | bytes 9437188
  176.9 8.3 %copy-start.7 = (bf16[512,768]{1,0:T(8,128)(2,1)}, bf16[512,768]{1,0:T(8,128)(2,1)S(1)}, u32[]{:S(2)}) copy-start(bf16[512,768]{1,0:T(8,128)(2,1)S(1)} %get-tuple-element.11) | copy-start | bytes 2359300
  176.9 6.4 %copy-start.11 = (bf16[1,2048,768]{2,1,0:T(8,128)(2,1)S(1)}, bf16[1,2048,768]{2,1,0:T(8,128)(2,1)}, u32[]{:S(2)}) copy-start(bf16[1,2048,768]{2,1,0:T(8,128)(2,1)} %param.15) | copy-start | bytes 9437188
  188.3 69.4 %all-to-all-start.2 = ((bf16[32,16,2048]{2,1,0:T(8,128)(2,1)}), bf16[32,16,2048]{2,1,0:T(8,128)(2,1)}, u32[]{:S(2)}, u32[]{:S(2)}) async-start(bf16[32,16,2048]{2,1,0:T(8,128)(2,1)} %bitcast.96), calls=%async_computation.2 | async-start | bytes 4194304 | tf_op jit(solution)/shard_map/all_to_all | solution.py:101
  202.5 2.0 copy-start.12
  202.5 2.4 copy-start.13
  203.8 7.7 %collective-permute-start = (bf16[4,256,768]{2,1,0:T(8,128)(2,1)}, bf16[4,256,768]{2,1,0:T(8,128)(2,1)}, u32[]{:S(2)}, u32[]{:S(2)}) collective-permute-start(bf16[4,256,768]{2,1,0:T(8,128)(2,1)} %dynamic-slice_bitcast_fusion.1), channel_id=1, source_target_pairs={{0,32},{32,0},{64,96},{96,64},{128,160},{160,128},{192,224},{224,1... | collective-permute-start | bytes 4718600 | tf_op jit(solution)/shard_map/ppermute | solution.py:45
  211.4 9.8 %collective-permute-start.4 = (bf16[4,256,768]{2,1,0:T(8,128)(2,1)}, bf16[4,256,768]{2,1,0:T(8,128)(2,1)}, u32[]{:S(2)}, u32[]{:S(2)}) collective-permute-start(bf16[4,256,768]{2,1,0:T(8,128)(2,1)} %dynamic-slice_bitcast_fusion), channel_id=1, source_target_pairs={{0,32},{32,0},{64,96},{96,64},{128,160},{160,128},{192,224},{224,1... | collective-permute-start | bytes 4718600 | tf_op jit(solution)/shard_map/ppermute | solution.py:45
  211.4 9.8 %copy-start.4 = (bf16[2048,768]{1,0:T(8,128)(2,1)S(1)}, bf16[2048,768]{1,0:T(8,128)(2,1)}, u32[]{:S(2)}) copy-start(bf16[2048,768]{1,0:T(8,128)(2,1)} %copy-done.3) | copy-start | bytes 9437188
  216.1 16.1 %collective-permute-start.1 = (bf16[256,768]{1,0:T(8,128)(2,1)}, bf16[256,768]{1,0:T(8,128)(2,1)}, u32[]{:S(2)}, u32[]{:S(2)}) collective-permute-start(bf16[256,768]{1,0:T(8,128)(2,1)} %get-tuple-element.16), channel_id=1, source_target_pairs={{0,64},{32,96},{64,128},{96,160},{128,192},{160,224},{192,0},{224,... | collective-permute-start | bytes 1179656 | tf_op jit(solution)/shard_map/ppermute | solution.py:52
  217.6 27.1 %collective-permute-start.3 = (bf16[256,768]{1,0:T(8,128)(2,1)}, bf16[256,768]{1,0:T(8,128)(2,1)}, u32[]{:S(2)}, u32[]{:S(2)}) collective-permute-start(bf16[256,768]{1,0:T(8,128)(2,1)} %get-tuple-element.17), channel_id=1, source_target_pairs={{0,192},{32,224},{64,0},{96,32},{128,64},{160,96},{192,128},{224,1... | collective-permute-start | bytes 1179656 | tf_op jit(solution)/shard_map/ppermute | solution.py:52
  219.4 25.3 %collective-permute-start.2 = (bf16[256,768]{1,0:T(8,128)(2,1)}, bf16[256,768]{1,0:T(8,128)(2,1)}, u32[]{:S(2)}, u32[]{:S(2)}) collective-permute-start(bf16[256,768]{1,0:T(8,128)(2,1)} %get-tuple-element.18), channel_id=1, source_target_pairs={{0,128},{32,160},{64,192},{96,224},{128,0},{160,32},{192,64},{224,... | collective-permute-start | bytes 1179656 | tf_op jit(solution)/shard_map/ppermute | solution.py:52
  228.9 18.8 %collective-permute-start.6 = (bf16[256,768]{0,1:T(8,128)(2,1)}, bf16[256,768]{0,1:T(8,128)(2,1)}, u32[]{:S(2)}, u32[]{:S(2)}) collective-permute-start(bf16[256,768]{0,1:T(8,128)(2,1)} %bitcast.99), channel_id=1, source_target_pairs={{0,128},{32,160},{64,192},{96,224},{128,0},{160,32},{192,64},{224,... | collective-permute-start | bytes 1179656 | tf_op jit(solution)/shard_map/ppermute | solution.py:52
  230.5 24.0 %collective-permute-start.7 = (bf16[256,768]{0,1:T(8,128)(2,1)}, bf16[256,768]{0,1:T(8,128)(2,1)}, u32[]{:S(2)}, u32[]{:S(2)}) collective-permute-start(bf16[256,768]{0,1:T(8,128)(2,1)} %bitcast.98), channel_id=1, source_target_pairs={{0,192},{32,224},{64,0},{96,32},{128,64},{160,96},{192,128},{224,1... | collective-permute-start | bytes 1179656 | tf_op jit(solution)/shard_map/ppermute | solution.py:52
  232.2 23.4 %collective-permute-start.5 = (bf16[256,768]{0,1:T(8,128)(2,1)}, bf16[256,768]{0,1:T(8,128)(2,1)}, u32[]{:S(2)}, u32[]{:S(2)}) collective-permute-start(bf16[256,768]{0,1:T(8,128)(2,1)} %bitcast.97), channel_id=1, source_target_pairs={{0,64},{32,96},{64,128},{96,160},{128,192},{160,224},{192,0},{224,... | collective-permute-start | bytes 1179656 | tf_op jit(solution)/shard_map/ppermute | solution.py:52
  235.7 19.8 %copy-start.2 = (f32[1,256,768]{1,2,0:T(8,128)S(1)}, f32[1,256,768]{1,2,0:T(8,128)}, u32[]{:S(2)}) copy-start(f32[1,256,768]{1,2,0:T(8,128)} %copy.35) | copy-start | bytes 2359300
  244.7 13.1 %copy-start.6 = (pred[128,512]{1,0:T(8,128)(4,1)S(1)}, pred[128,512]{1,0:T(8,128)(4,1)}, u32[]{:S(2)}) copy-start(pred[128,512]{1,0:T(8,128)(4,1)} %copy-done.5) | copy-start | bytes 196612
  244.7 15.9 %copy-start.1 = (bf16[1,2048,768]{2,1,0:T(8,128)(2,1)S(1)}, bf16[1,2048,768]{2,1,0:T(8,128)(2,1)}, u32[]{:S(2)}) copy-start(bf16[1,2048,768]{2,1,0:T(8,128)(2,1)} %param.13) | copy-start | bytes 9437188
  (1 other events, 1.6 us)

commit v6 on v3

--- a/solution.py
+++ b/solution.py
@@ -32,6 +32,33 @@
     return lax.dot_general(
         pick, rows, (((0,), (0,)), ((), ())), preferred_element_type=jnp.float32
     ).astype(jnp.bfloat16)
+
+
+def reduce_over_dp(parts, replicas):
+    half = replicas // 2
+    me = lax.axis_index("dp")
+    core = me % 2
+    row = me // 2
+    rows, cols = parts[0].shape
+    blocks = [p.reshape(half, 2, rows // replicas, cols) for p in parts]
+    swaps = [(i, i ^ 1) for i in range(replicas)]
+    partial = jnp.stack(
+        [
+            lax.dynamic_index_in_dim(b, core, axis=1, keepdims=False).astype(jnp.float32)
+            + lax.ppermute(
+                lax.dynamic_index_in_dim(b, 1 - core, axis=1, keepdims=False), "dp", swaps
+            ).astype(jnp.float32)
+            for b in blocks
+        ],
+        1,
+    )
+    rolled = lax.dynamic_slice_in_dim(jnp.concatenate([partial, partial], 0), row, half, 0)
+    wire = rolled.astype(jnp.bfloat16)
+    total = rolled[0]
+    for step in range(1, half):
+        pairs = [(i, (i + 2 * step) % replicas) for i in range(replicas)]
+        total = total + lax.ppermute(wire[step], "dp", pairs).astype(jnp.float32)
+    return total.astype(jnp.bfloat16)
 
 
 def per_device(tokens, tangents, cotangents, routes, gates, w_up, w_down, v_up):
@@ -86,19 +113,16 @@
         concat_axis=0,
         tiled=True,
     ).reshape(slots, width)
+    hvp_tokens = jnp.dot(pick, returned, preferred_element_type=jnp.float32).astype(jnp.bfloat16)
     second = jnp.dot(scaled_cot.T, hidden_tan, preferred_element_type=jnp.float32)
-    down_sum = lax.psum_scatter(
-        (second * scale).astype(jnp.bfloat16), "dp", scatter_dimension=0, tiled=True
-    )
-    hvp_tokens = jnp.dot(pick, returned, preferred_element_type=jnp.float32).astype(jnp.bfloat16)
     first = jnp.dot(tangent.T, back_pre, preferred_element_type=jnp.float32) + jnp.dot(
         primal.T, back_tan, preferred_element_type=jnp.float32
     )
-    up_sum = lax.psum_scatter(
-        (first * scale).astype(jnp.bfloat16), "dp", scatter_dimension=0, tiled=True
+    summed = reduce_over_dp(
+        ((first * scale).astype(jnp.bfloat16), (second * scale).astype(jnp.bfloat16)), replicas
     )
-    hvp_up = up_sum[None]
-    hvp_down = down_sum.T[None]
+    hvp_up = summed[0][None]
+    hvp_down = summed[1].T[None]
     return (hvp_tokens, hvp_up, hvp_down)
 
 

time: 276 us -> 271 us (0.982)
  blocking collectives: 56.8 us -> 0 us
  waiting for transfers between devices: 129 us -> 159 us
  starting transfers between devices: 19.9 us -> 33.4 us
  between operations: 14.2 us -> 0.91 us
  local copies, waits for them, and re-layouts: 3.21 us -> 16.4 us
  other arithmetic: 4.3 us -> 10.1 us
    all_to_all x1 -> x0, blocking collectives: 56.8 us -> none  [per_device(): lax.all_to_all(input_hvp.reshape(expert_count, capacity, width), 'expert'...]
    ppermute x0 -> x5, waiting for transfers between devices: none -> 35.4 us  [the longest x3 35.4 us: reduce_over_dp(): total = total + lax.ppermute(wire[step], 'dp', pairs).astype(jnp.float32)]
    all_to_all x0 -> x1, starting transfers between devices: none -> 8.75 us  [per_device(): lax.all_to_all(input_hvp.reshape(expert_count, capacity, width), 'expert'...]
    dynamic_slice x0 -> x3, local copies, waits for them, and re-layouts: none -> 8.05 us  [the longest x2 5.23 us: reduce_over_dp(): lax.dynamic_index_in_dim(b, 1 - core, axis=1, keepdims=False)]
    ppermute x0 -> x5, starting transfers between devices: none -> 5.2 us  [the longest x3 4.69 us: reduce_over_dp(): total = total + lax.ppermute(wire[step], 'dp', pairs).astype(jnp.float32)]
    reduce_scatter x2 -> x0, waiting for transfers between devices: 4.28 us -> none  [the longest x1 4.28 us: per_device(): lax.psum_scatter((first * scale).astype(jnp.bfloat16), 'dp', scatter_dime...]
    unnamed x16 -> x20, local copies, waits for them, and re-layouts: 2.88 us -> 7.05 us
    another operation x0 -> x2, other arithmetic: none -> 4.09 us  [reduce_over_dp(): jnp.stack([lax.dynamic_index_in_dim(b, core, axis=1, keepdims=False).asty...]
  transfers between devices with their start and end apart: 4 -> 8, of which waited for: 3 -> 4; matrix products, arithmetic and copies ran while one was open for 13% -> 14% of each run, Pallas kernels for 0% -> 0%
where the time goes in v6:
time: 271 us; the launch traced here: 269 us
  waiting for transfers between devices  159 us (59%)
  matrix products  49.4 us (18%)
  starting transfers between devices  33.4 us (12%)
  local copies, waits for them, and re-layouts  16.4 us (6%)
  other arithmetic  10.1 us (4%)
    all_to_all x1, waiting for transfers between devices, per_device(): lax.all_to_all(send_xg.reshape(expert_count, capacity, 2 * width), 'exper...  91.4 us
    ppermute x3, waiting for transfers between devices, reduce_over_dp(): total = total + lax.ppermute(wire[step], 'dp', pairs).astype(jnp.float32)  35.4 us
    all_to_all x1, waiting for transfers between devices, per_device(): lax.all_to_all(send_tan.reshape(expert_count, capacity, width), 'expert',...  32.5 us
    all_to_all x1, starting transfers between devices, per_device(): lax.all_to_all(send_xg.reshape(expert_count, capacity, 2 * width), 'exper...  11.7 us
    all_to_all x1, starting transfers between devices, per_device(): lax.all_to_all(input_hvp.reshape(expert_count, capacity, width), 'expert'...  8.75 us
    all_to_all x1, starting transfers between devices, per_device(): lax.all_to_all(send_tan.reshape(expert_count, capacity, width), 'expert',...  7.74 us
    unnamed x20, local copies, waits for them, and re-layouts  7.05 us
    dot_general x3, matrix products, to_slots(): lax.dot_general(pick, rows, (((0,), (0,)), ((), ())), preferred_element_t...  5.65 us
  transfers between devices with their start and end apart: 8, of which 4 were waited for; matrix products, arithmetic and copies ran while one was open for 14% of the time, Pallas kernels for 0%

profile of v6, /device:TPU:2, one launch (start us, length us, event | category | flops | bytes accessed | tf_op | source)
XLA Modules:
  0.0 269.4 jit_solution(5330396346983024131)
XLA Ops:
  8.9 11.7 %all-to-all-start = ((bf16[32,16,4096]{2,1,0:T(8,128)(2,1)}), bf16[32,16,4096]{2,1,0:T(8,128)(2,1)}, u32[]{:S(2)}, u32[]{:S(2)}) async-start(bf16[32,16,4096]{2,1,0:T(8,128)(2,1)} %bitcast.77), calls=%async_computation | async-start | bytes 8388608 | tf_op jit(solution)/shard_map/all_to_all | solution.py:75
  20.6 3.1 %convolution_convert_fusion.1 = bf16[512,2048]{1,0:T(8,128)(2,1)} fusion(pred[128,512]{1,0:T(8,128)(4,1)S(1)} %fusion.38, bf16[128,2048]{1,0:T(8,128)(2,1)} %param.9), kind=kOutput, calls=%fused_computation.28 | convolution fusion | flops 269484032 | bytes 2686976 | tf_op jit(solution)/shard_map/dot_general | solution.py:32
  23.7 91.4 %all-to-all-done = bf16[32,16,4096]{2,1,0:T(8,128)(2,1)} async-done(((bf16[32,16,4096]{2,1,0:T(8,128)(2,1)}), bf16[32,16,4096]{2,1,0:T(8,128)(2,1)}, u32[]{:S(2)}, u32[]{:S(2)}) %all-to-all-start) | async-done | bytes 4194336 | tf_op jit(solution)/shard_map/all_to_all | solution.py:75
  115.0 7.7 %all-to-all-start.1 = ((bf16[32,16,2048]{2,1,0:T(8,128)(2,1)}), bf16[32,16,2048]{2,1,0:T(8,128)(2,1)}, u32[]{:S(2)}, u32[]{:S(2)}) async-start(bf16[32,16,2048]{2,1,0:T(8,128)(2,1)} %bitcast.79), calls=%async_computation.1 | async-start | bytes 4194304 | tf_op jit(solution)/shard_map/all_to_all | solution.py:83
  122.8 5.5 %fusion.15 = f32[512,768]{1,0:T(8,128)} fusion(bf16[1,768,2048]{2,1,0:T(8,128)(2,1)} %param.14, bf16[512,4096]{1,0:T(8,128)(2,1)} %bitcast.1), kind=kOutput, calls=%fused_computation.25 | convolution fusion | flops 1610612736 | bytes 6815744 | tf_op jit(solution)/shard_map/dot_general | solution.py:99
  128.3 4.7 %fusion.13 = f32[512,768]{1,0:T(8,128)} fusion(bf16[1,2048,768]{2,1,0:T(8,128)(2,1)S(1)} %copy-done, bf16[512,4096]{1,0:T(8,128)(2,1)} %bitcast.1), kind=kOutput, calls=%fused_computation.23 | convolution fusion | flops 1610612736 | bytes 6815744 | tf_op jit(solution)/shard_map/dot_general | solution.py:95
  133.0 4.6 %fusion.7 = f32[512,768]{1,0:T(8,128)} fusion(bf16[1,2048,768]{2,1,0:T(8,128)(2,1)S(1)} %copy-done.5, bf16[512,4096]{1,0:T(8,128)(2,1)} %bitcast.1), kind=kOutput, calls=%fused_computation.17 | convolution fusion | flops 1610612736 | bytes 6815744 | tf_op jit(solution)/shard_map/dot_general | solution.py:101
  137.6 32.5 %all-to-all-done.1 = bf16[32,16,2048]{2,1,0:T(8,128)(2,1)} async-done(((bf16[32,16,2048]{2,1,0:T(8,128)(2,1)}), bf16[32,16,2048]{2,1,0:T(8,128)(2,1)}, u32[]{:S(2)}, u32[]{:S(2)}) %all-to-all-start.1) | async-done | bytes 2097184 | tf_op jit(solution)/shard_map/all_to_all | solution.py:83
  170.1 5.5 %fusion.27 = (bf16[512,768]{1,0:T(8,128)(2,1)S(1)}, bf16[512,768]{1,0:T(8,128)(2,1)S(1)}, f32[512,768]{1,0:T(8,128)S(1)}) fusion(f32[512,768]{1,0:T(8,128)} %fusion.15, f32[512,768]{1,0:T(8,128)} %fusion.13, f32[512,768]{1,0:T(8,128)} %fusion.7, bf16[512,2048]{1,0:T(8,128)(2,1)} %bitcast.5, bf16[1,2048,768]{2,1,0:T(8,128)(2,1)S(1)} %copy-done), kind=kOutput, calls=%fused_computation.41 | convolution fusion | flops 1618083840 | bytes 13107200 | tf_op jit(solution)/shard_map/dot_general | solution.py:103
  175.6 3.8 %fusion.5 = f32[512,2048]{1,0:T(8,128)} fusion(bf16[512,768]{1,0:T(8,128)(2,1)S(1)} %get-tuple-element.29, bf16[1,2048,768]{2,1,0:T(8,128)(2,1)S(1)} %copy-done.6), kind=kOutput, calls=%fused_computation.15 | convolution fusion | flops 1610612736 | bytes 8126464 | tf_op jit(solution)/shard_map/dot_general | solution.py:102
  179.4 3.6 %fusion.45 = f32[2048,768]{1,0:T(8,128)S(1)} fusion(bf16[512,2048]{1,0:T(8,128)(2,1)} %bitcast.5, bf16[512,768]{1,0:T(8,128)(2,1)S(1)} %get-tuple-element.29), kind=kOutput, calls=%fused_computation.73 | convolution fusion | flops 1610612736 | bytes 9175040 | tf_op jit(solution)/shard_map/dot_general | solution.py:118
  183.0 3.6 %multiply_convert_fusion = bf16[2048,768]{1,0:T(8,128)(2,1)S(1)} fusion(bf16[512,4096]{1,0:T(8,128)(2,1)} %bitcast.1, f32[512,768]{1,0:T(8,128)S(1)} %get-tuple-element.32, f32[512,768]{1,0:T(8,128)S(1)} %copy-done.7), kind=kOutput, calls=%fused_computation.7 | convolution fusion | flops 1617297408 | bytes 8388608 | tf_op jit(solution)/shard_map/dot_general | solution.py:117
  186.6 3.9 %multiply_convert_fusion.1 = bf16[2048,768]{1,0:T(8,128)(2,1)S(1)} fusion(f32[2048,768]{1,0:T(8,128)S(1)} %fusion.45, bf16[512,768]{1,0:T(8,128)(2,1)S(1)} %get-tuple-element.28, bf16[512,4096]{1,0:T(8,128)(2,1)} %bitcast.1), kind=kOutput, calls=%fused_computation.8 | convolution fusion | flops 1615331328 | bytes 12320768 | tf_op jit(solution)/shard_map/dot_general | solution.py:118
  190.5 2.8 %constant_dynamic-slice_fusion.1 = (bf16[4,1,256,768]{3,2,1,0:T(8,128)(2,1)}, bf16[4,1,256,768]{3,2,1,0:T(8,128)(2,1)}, bf16[4,1,256,768]{3,2,1,0:T(8,128)(2,1)}, bf16[4,1,256,768]{3,2,1,0:T(8,128)(2,1)}) fusion(bf16[4,2,256,768]{3,2,1,0:T(8,128)(2,1)S(1)} %bitcast.80, s32[]{:T(128)S(6)} %select_n.29, s32[]{:T(128)S(6)} %select_n.30, ...), kind=kLoop, calls=%fused_computation.68 | loop fusion | bytes 12582920 | tf_op jit(solution)/shard_map/jit(dynamic_index_in_dim)/dynamic_slice | solution.py:47
  193.3 2.7 copy.41
  195.9 2.6 copy.39
  199.0 5.6 %add_convert_fusion = bf16[512,2048]{1,0:T(8,128)(2,1)} fusion(f32[512,2048]{1,0:T(8,128)} %fusion.5, bf16[512,768]{1,0:T(8,128)(2,1)} %copy-done.3, bf16[1,2048,768]{2,1,0:T(8,128)(2,1)S(1)} %copy-done), kind=kOutput, calls=%fused_computation.10 | convolution fusion | flops 1612709888 | bytes 10223616 | tf_op jit(solution)/shard_map/dot_general | solution.py:106
  204.6 8.7 %all-to-all-start.2 = ((bf16[32,16,2048]{2,1,0:T(8,128)(2,1)}), bf16[32,16,2048]{2,1,0:T(8,128)(2,1)}, u32[]{:S(2)}, u32[]{:S(2)}) async-start(bf16[32,16,2048]{2,1,0:T(8,128)(2,1)} %bitcast.81), calls=%async_computation.2 | async-start | bytes 4194304 | tf_op jit(solution)/shard_map/all_to_all | solution.py:109
  213.4 2.6 copy.44
  216.0 2.6 copy.43
  224.3 3.1 %collective-permute-start.4 = (bf16[2,256,768]{1,2,0:T(8,128)(2,1)S(1)}, bf16[2,256,768]{1,2,0:T(8,128)(2,1)S(1)}, u32[]{:S(2)}, u32[]{:S(2)}) collective-permute-start(bf16[2,256,768]{1,2,0:T(8,128)(2,1)S(1)} %get-tuple-element.22), channel_id=1, source_target_pairs={{0,192},{32,224},{64,0},{96,32},{128,64},{160,96},{192,128},{224,1... | collective-permute-start | bytes 2359304 | tf_op jit(solution)/shard_map/ppermute | solution.py:60
  229.0 31.7 %collective-permute-done.4 = bf16[2,256,768]{1,2,0:T(8,128)(2,1)S(1)} collective-permute-done((bf16[2,256,768]{1,2,0:T(8,128)(2,1)S(1)}, bf16[2,256,768]{1,2,0:T(8,128)(2,1)S(1)}, u32[]{:S(2)}, u32[]{:S(2)}) %collective-permute-start.4) | collective-permute-done | bytes 786464 | tf_op jit(solution)/shard_map/ppermute | solution.py:60
  260.6 3.7 %collective-permute-done.2 = bf16[2,256,768]{1,2,0:T(8,128)(2,1)S(1)} collective-permute-done((bf16[2,256,768]{1,2,0:T(8,128)(2,1)S(1)}, bf16[2,256,768]{1,2,0:T(8,128)(2,1)S(1)}, u32[]{:S(2)}, u32[]{:S(2)}) %collective-permute-start.2) | collective-permute-done | bytes 786464 | tf_op jit(solution)/shard_map/ppermute | solution.py:60
  266.5 2.9 %convolution_convert_fusion.3 = bf16[128,2048]{1,0:T(8,128)(2,1)} fusion(pred[128,512]{1,0:T(8,128)(4,1)} %copy-done.2, bf16[512,2048]{1,0:T(8,128)(2,1)} %bitcast.8), kind=kOutput, calls=%fused_computation.30 | convolution fusion | flops 268697600 | bytes 2686976 | tf_op jit(solution)/shard_map/dot_general | solution.py:116
  (44 shorter events, 18.1 us)
Async XLA Ops:
  0.6 127.7 %copy-start = (bf16[1,2048,768]{2,1,0:T(8,128)(2,1)S(1)}, bf16[1,2048,768]{2,1,0:T(8,128)(2,1)}, u32[]{:S(2)}) copy-start(bf16[1,2048,768]{2,1,0:T(8,128)(2,1)} %param.13) | copy-start | bytes 9437188
  2.1 3.5 %copy-start.4 = (bf16[128,2048]{1,0:T(8,128)(2,1)S(1)}, bf16[128,2048]{1,0:T(8,128)(2,1)}, u32[]{:S(2)}) copy-start(bf16[128,2048]{1,0:T(8,128)(2,1)} %param.8) | copy-start | bytes 1572868
  3.0 17.5 %copy-start.2 = (pred[128,512]{1,0:T(8,128)(4,1)}, pred[128,512]{1,0:T(8,128)(4,1)S(1)}, u32[]{:S(2)}) copy-start(pred[128,512]{1,0:T(8,128)(4,1)S(1)} %fusion.38) | copy-start | bytes 196612
  8.9 106.2 %all-to-all-start = ((bf16[32,16,4096]{2,1,0:T(8,128)(2,1)}), bf16[32,16,4096]{2,1,0:T(8,128)(2,1)}, u32[]{:S(2)}, u32[]{:S(2)}) async-start(bf16[32,16,4096]{2,1,0:T(8,128)(2,1)} %bitcast.77), calls=%async_computation | async-start | bytes 8388608 | tf_op jit(solution)/shard_map/all_to_all | solution.py:75
  115.0 55.0 %all-to-all-start.1 = ((bf16[32,16,2048]{2,1,0:T(8,128)(2,1)}), bf16[32,16,2048]{2,1,0:T(8,128)(2,1)}, u32[]{:S(2)}, u32[]{:S(2)}) async-start(bf16[32,16,2048]{2,1,0:T(8,128)(2,1)} %bitcast.79), calls=%async_computation.1 | async-start | bytes 4194304 | tf_op jit(solution)/shard_map/all_to_all | solution.py:83
  128.3 4.7 %copy-start.5 = (bf16[1,2048,768]{2,1,0:T(8,128)(2,1)S(1)}, bf16[1,2048,768]{2,1,0:T(8,128)(2,1)}, u32[]{:S(2)}) copy-start(bf16[1,2048,768]{2,1,0:T(8,128)(2,1)} %param.15) | copy-start | bytes 9437188
  170.1 5.5 %copy-start.6 = (bf16[1,2048,768]{2,1,0:T(8,128)(2,1)S(1)}, bf16[1,2048,768]{2,1,0:T(8,128)(2,1)}, u32[]{:S(2)}) copy-start(bf16[1,2048,768]{2,1,0:T(8,128)(2,1)} %param.15) | copy-start | bytes 9437188
  175.6 11.0 %copy-start.3 = (bf16[512,768]{1,0:T(8,128)(2,1)}, bf16[512,768]{1,0:T(8,128)(2,1)S(1)}, u32[]{:S(2)}) copy-start(bf16[512,768]{1,0:T(8,128)(2,1)S(1)} %get-tuple-element.28) | copy-start | bytes 2359300
  179.4 3.6 %copy-start.7 = (f32[512,768]{1,0:T(8,128)S(1)}, f32[512,768]{1,0:T(8,128)}, u32[]{:S(2)}) copy-start(f32[512,768]{1,0:T(8,128)} %fusion.13) | copy-start | bytes 4718596
  195.9 22.6 %collective-permute-start.1 = (bf16[4,256,768]{1,2,0:T(8,128)(2,1)}, bf16[4,256,768]{1,2,0:T(8,128)(2,1)}, u32[]{:S(2)}, u32[]{:S(2)}) collective-permute-start(bf16[4,256,768]{1,2,0:T(8,128)(2,1)} %bitcast.83), channel_id=1, source_target_pairs={{0,32},{32,0},{64,96},{96,64},{128,160},{160,128},{192,224},{224,1... | collective-permute-start | bytes 4718600 | tf_op jit(solution)/shard_map/ppermute | solution.py:48
  198.5 22.4 %collective-permute-start = (bf16[4,256,768]{1,2,0:T(8,128)(2,1)}, bf16[4,256,768]{1,2,0:T(8,128)(2,1)}, u32[]{:S(2)}, u32[]{:S(2)}) collective-permute-start(bf16[4,256,768]{1,2,0:T(8,128)(2,1)} %bitcast.82), channel_id=1, source_target_pairs={{0,32},{32,0},{64,96},{96,64},{128,160},{160,128},{192,224},{224,1... | collective-permute-start | bytes 4718600 | tf_op jit(solution)/shard_map/ppermute | solution.py:48
  204.6 61.9 %all-to-all-start.2 = ((bf16[32,16,2048]{2,1,0:T(8,128)(2,1)}), bf16[32,16,2048]{2,1,0:T(8,128)(2,1)}, u32[]{:S(2)}, u32[]{:S(2)}) async-start(bf16[32,16,2048]{2,1,0:T(8,128)(2,1)} %bitcast.81), calls=%async_computation.2 | async-start | bytes 4194304 | tf_op jit(solution)/shard_map/all_to_all | solution.py:109
  218.6 2.4 copy-start.1
  224.3 36.4 %collective-permute-start.4 = (bf16[2,256,768]{1,2,0:T(8,128)(2,1)S(1)}, bf16[2,256,768]{1,2,0:T(8,128)(2,1)S(1)}, u32[]{:S(2)}, u32[]{:S(2)}) collective-permute-start(bf16[2,256,768]{1,2,0:T(8,128)(2,1)S(1)} %get-tuple-element.22), channel_id=1, source_target_pairs={{0,192},{32,224},{64,0},{96,32},{128,64},{160,96},{192,128},{224,1... | collective-permute-start | bytes 2359304 | tf_op jit(solution)/shard_map/ppermute | solution.py:60
  227.4 33.3 %collective-permute-start.3 = (bf16[2,256,768]{1,2,0:T(8,128)(2,1)S(1)}, bf16[2,256,768]{1,2,0:T(8,128)(2,1)S(1)}, u32[]{:S(2)}, u32[]{:S(2)}) collective-permute-start(bf16[2,256,768]{1,2,0:T(8,128)(2,1)S(1)} %get-tuple-element.23), channel_id=1, source_target_pairs={{0,128},{32,160},{64,192},{96,224},{128,0},{160,32},{192,64},{224,... | collective-permute-start | bytes 2359304 | tf_op jit(solution)/shard_map/ppermute | solution.py:60
  228.0 36.3 %collective-permute-start.2 = (bf16[2,256,768]{1,2,0:T(8,128)(2,1)S(1)}, bf16[2,256,768]{1,2,0:T(8,128)(2,1)S(1)}, u32[]{:S(2)}, u32[]{:S(2)}) collective-permute-start(bf16[2,256,768]{1,2,0:T(8,128)(2,1)S(1)} %get-tuple-element.21), channel_id=1, source_target_pairs={{0,64},{32,96},{64,128},{96,160},{128,192},{160,224},{192,0},{224,... | collective-permute-start | bytes 2359304 | tf_op jit(solution)/shard_map/ppermute | solution.py:60

commit v7 on v5

--- a/solution.py
+++ b/solution.py
@@ -45,11 +45,11 @@
     got = lax.ppermute(give, "dp", [(i, i ^ 1) for i in range(replicas)])
     partial = keep.astype(jnp.float32) + got.astype(jnp.float32)
     wire = partial.astype(jnp.bfloat16)
+    wire = lax.dynamic_slice_in_dim(jnp.concatenate([wire, wire], 0), row, half, 0)
     total = lax.dynamic_index_in_dim(partial, row, axis=0, keepdims=False)
     for step in range(1, half):
-        send = lax.dynamic_index_in_dim(wire, (row + step) % half, axis=0, keepdims=False)
         pairs = [(i, (i + 2 * step) % replicas) for i in range(replicas)]
-        total = total + lax.ppermute(send, "dp", pairs).astype(jnp.float32)
+        total = total + lax.ppermute(wire[step], "dp", pairs).astype(jnp.float32)
     return total.astype(jnp.bfloat16)
 
 

time: 262 us -> 265 us (1.011)
  waiting for transfers between devices: 142 us -> 147 us
  local copies, waits for them, and re-layouts: 16.7 us -> 13.4 us
  other arithmetic: 14.5 us -> 17.7 us
    ppermute x6, waiting for transfers between devices: 17.3 us -> 22.4 us  [reduce_over_dp(): total = total + lax.ppermute(wire[step], 'dp', pairs).astype(jnp.float32)]
    dynamic_slice x6 -> x2, local copies, waits for them, and re-layouts: 9 us -> 4.54 us  [the longest x1 2.59 us: reduce_over_dp(): give = lax.dynamic_index_in_dim(blocks, 1 - core, axis=1, keepdims=False)]
    add x0 -> x1, other arithmetic: none -> 3.95 us  [reduce_over_dp(): partial = keep.astype(jnp.float32) + got.astype(jnp.float32)]
    dot_general x1, matrix products: 6.43 us -> 3.71 us  [per_device(): jnp.dot(tangent.T, back_pre, preferred_element_type=jnp.float32)]
    convert_element_type x2 -> x1, other arithmetic: 5.47 us -> 3.51 us  [reduce_over_dp(): wire = partial.astype(jnp.bfloat16)]
where the time goes in v7:
time: 265 us; the launch traced here: 264 us
  waiting for transfers between devices  147 us (55%)
  matrix products  47.6 us (18%)
  starting transfers between devices  37.8 us (14%)
  other arithmetic  17.7 us (7%)
  local copies, waits for them, and re-layouts  13.4 us (5%)
    all_to_all x1, waiting for transfers between devices, per_device(): lax.all_to_all(send_xg.reshape(expert_count, capacity, 2 * width), 'exper...  91.3 us
    all_to_all x1, waiting for transfers between devices, per_device(): lax.all_to_all(send_tan.reshape(expert_count, capacity, width), 'expert',...  33.5 us
    ppermute x6, waiting for transfers between devices, reduce_over_dp(): total = total + lax.ppermute(wire[step], 'dp', pairs).astype(jnp.float32)  22.4 us
    all_to_all x1, starting transfers between devices, per_device(): lax.all_to_all(send_xg.reshape(expert_count, capacity, 2 * width), 'exper...  11.7 us
    ppermute x6, starting transfers between devices, reduce_over_dp(): total = total + lax.ppermute(wire[step], 'dp', pairs).astype(jnp.float32)  9.61 us
    all_to_all x1, starting transfers between devices, per_device(): lax.all_to_all(input_hvp.reshape(expert_count, capacity, width), 'expert'...  8.85 us
    all_to_all x1, starting transfers between devices, per_device(): lax.all_to_all(send_tan.reshape(expert_count, capacity, width), 'expert',...  7.69 us
    dot_general x1, matrix products, per_device(): jnp.dot(tangent, up_proj, preferred_element_type=jnp.float32) + pre_mix  6.62 us
  transfers between devices with their start and end apart: 11, of which 6 were waited for; matrix products, arithmetic and copies ran while one was open for 19% of the time, Pallas kernels for 0%

profile of v7, /device:TPU:2, one launch (start us, length us, event | category | flops | bytes accessed | tf_op | source)
XLA Modules:
  0.0 264.5 jit_solution(13430622523239261554)
XLA Ops:
  9.0 11.7 %all-to-all-start = ((bf16[32,16,4096]{2,1,0:T(8,128)(2,1)}), bf16[32,16,4096]{2,1,0:T(8,128)(2,1)}, u32[]{:S(2)}, u32[]{:S(2)}) async-start(bf16[32,16,4096]{2,1,0:T(8,128)(2,1)} %bitcast.95), calls=%async_computation | async-start | bytes 8388608 | tf_op jit(solution)/shard_map/all_to_all | solution.py:67
  20.7 3.2 %convolution_convert_fusion.1 = bf16[512,2048]{1,0:T(8,128)(2,1)} fusion(pred[128,512]{1,0:T(8,128)(4,1)S(1)} %fusion.37, bf16[128,2048]{1,0:T(8,128)(2,1)} %param.9), kind=kOutput, calls=%fused_computation.23 | convolution fusion | flops 269484032 | bytes 2686976 | tf_op jit(solution)/shard_map/dot_general | solution.py:32
  23.9 91.3 %all-to-all-done = bf16[32,16,4096]{2,1,0:T(8,128)(2,1)} async-done(((bf16[32,16,4096]{2,1,0:T(8,128)(2,1)}), bf16[32,16,4096]{2,1,0:T(8,128)(2,1)}, u32[]{:S(2)}, u32[]{:S(2)}) %all-to-all-start) | async-done | bytes 4194336 | tf_op jit(solution)/shard_map/all_to_all | solution.py:67
  115.2 7.7 %all-to-all-start.1 = ((bf16[32,16,2048]{2,1,0:T(8,128)(2,1)}), bf16[32,16,2048]{2,1,0:T(8,128)(2,1)}, u32[]{:S(2)}, u32[]{:S(2)}) async-start(bf16[32,16,2048]{2,1,0:T(8,128)(2,1)} %bitcast.98), calls=%async_computation.1 | async-start | bytes 4194304 | tf_op jit(solution)/shard_map/all_to_all | solution.py:75
  122.9 4.7 %fusion.8 = f32[512,768]{1,0:T(8,128)} fusion(bf16[1,2048,768]{2,1,0:T(8,128)(2,1)S(1)} %copy-done, bf16[512,4096]{1,0:T(8,128)(2,1)} %bitcast.1), kind=kOutput, calls=%fused_computation.18 | convolution fusion | flops 1610612736 | bytes 6815744 | tf_op jit(solution)/shard_map/dot_general | solution.py:87
  127.6 4.8 %fusion.2 = f32[512,768]{1,0:T(8,128)} fusion(bf16[1,2048,768]{2,1,0:T(8,128)(2,1)S(1)} %copy-done.7, bf16[512,4096]{1,0:T(8,128)(2,1)} %bitcast.1), kind=kOutput, calls=%fused_computation.12 | convolution fusion | flops 1610612736 | bytes 6815744 | tf_op jit(solution)/shard_map/dot_general | solution.py:93
  132.4 4.5 %fusion.10 = f32[512,768]{1,0:T(8,128)} fusion(bf16[1,768,2048]{2,1,0:T(8,128)(2,1)S(1)} %copy-done.6, bf16[512,4096]{1,0:T(8,128)(2,1)} %bitcast.1), kind=kOutput, calls=%fused_computation.20 | convolution fusion | flops 1610612736 | bytes 6815744 | tf_op jit(solution)/shard_map/dot_general | solution.py:91
  137.0 33.5 %all-to-all-done.1 = bf16[32,16,2048]{2,1,0:T(8,128)(2,1)} async-done(((bf16[32,16,2048]{2,1,0:T(8,128)(2,1)}), bf16[32,16,2048]{2,1,0:T(8,128)(2,1)}, u32[]{:S(2)}, u32[]{:S(2)}) %all-to-all-start.1) | async-done | bytes 2097184 | tf_op jit(solution)/shard_map/all_to_all | solution.py:75
  170.5 6.6 %fusion.22 = (bf16[512,768]{1,0:T(8,128)(2,1)}, bf16[512,768]{1,0:T(8,128)(2,1)}, f32[512,768]{1,0:T(8,128)S(1)}) fusion(f32[512,768]{1,0:T(8,128)} %fusion.10, f32[512,768]{1,0:T(8,128)} %fusion.8, f32[512,768]{1,0:T(8,128)} %fusion.2, bf16[512,2048]{1,0:T(8,128)(2,1)} %bitcast.5, bf16[1,2048,768]{2,1,0:T(8,128)(2,1)S(1)} %copy-done), kind=kOutput, calls=%fused_computation.36 | convolution fusion | flops 1618083840 | bytes 13107200 | tf_op jit(solution)/shard_map/dot_general | solution.py:95
  177.1 3.6 %multiply_convert_fusion = bf16[2048,768]{1,0:T(8,128)(2,1)S(1)} fusion(bf16[512,4096]{1,0:T(8,128)(2,1)} %bitcast.1, f32[512,768]{1,0:T(8,128)S(1)} %get-tuple-element.21, f32[512,768]{1,0:T(8,128)S(1)} %copy-done.8), kind=kOutput, calls=%fused_computation | convolution fusion | flops 1617297408 | bytes 8388608 | tf_op jit(solution)/shard_map/dot_general | solution.py:108
  182.6 2.6 copy.34
  185.2 4.0 %fusion = f32[512,2048]{1,0:T(8,128)S(1)} fusion(bf16[512,768]{1,0:T(8,128)(2,1)} %get-tuple-element.14, bf16[1,2048,768]{2,1,0:T(8,128)(2,1)} %param.15), kind=kOutput, calls=%fused_computation.10 | convolution fusion | flops 1610612736 | bytes 8126464 | tf_op jit(solution)/shard_map/dot_general | solution.py:94
  189.3 3.2 %add_convert_fusion = bf16[512,2048]{1,0:T(8,128)(2,1)} fusion(f32[512,2048]{1,0:T(8,128)S(1)} %fusion, bf16[512,768]{1,0:T(8,128)(2,1)S(1)} %copy-done.3, bf16[1,2048,768]{2,1,0:T(8,128)(2,1)S(1)} %copy-done), kind=kOutput, calls=%fused_computation.3 | convolution fusion | flops 1612709888 | bytes 10223616 | tf_op jit(solution)/shard_map/dot_general | solution.py:98
  192.5 8.8 %all-to-all-start.2 = ((bf16[32,16,2048]{2,1,0:T(8,128)(2,1)}), bf16[32,16,2048]{2,1,0:T(8,128)(2,1)}, u32[]{:S(2)}, u32[]{:S(2)}) async-start(bf16[32,16,2048]{2,1,0:T(8,128)(2,1)} %bitcast.100), calls=%async_computation.2 | async-start | bytes 4194304 | tf_op jit(solution)/shard_map/all_to_all | solution.py:101
  201.4 3.7 %fusion.46 = f32[2048,768]{1,0:T(8,128)S(1)} fusion(bf16[512,2048]{1,0:T(8,128)(2,1)} %bitcast.5, bf16[512,768]{1,0:T(8,128)(2,1)} %get-tuple-element.14), kind=kOutput, calls=%fused_computation.77 | convolution fusion | flops 1610612736 | bytes 9175040 | tf_op jit(solution)/shard_map/dot_general | solution.py:111
  205.1 3.6 %multiply_convert_fusion.1 = bf16[2048,768]{1,0:T(8,128)(2,1)S(1)} fusion(f32[2048,768]{1,0:T(8,128)S(1)} %fusion.46, bf16[512,768]{1,0:T(8,128)(2,1)S(1)} %copy-done.4, bf16[512,4096]{1,0:T(8,128)(2,1)} %bitcast.1), kind=kOutput, calls=%fused_computation.1 | convolution fusion | flops 1615331328 | bytes 12320768 | tf_op jit(solution)/shard_map/dot_general | solution.py:111
  211.7 2.6 copy.36
  214.3 3.9 %convert_add_fusion = (f32[4,256,768]{1,2,0:T(8,128)}, bf16[4,256,768]{1,2,0:T(8,128)(2,1)S(1)}) fusion(bf16[4,256,768]{1,2,0:T(8,128)(2,1)} %collective-permute-done.4, bf16[4,1,256,768]{2,3,0,1:T(8,128)(2,1)} %copy.36), kind=kLoop, calls=%fused_computation.8 | loop fusion | flops 3145728 | bytes 7864320 | tf_op jit(solution)/shard_map/add | solution.py:46
  221.2 3.1 %collective-permute-start.6 = (bf16[256,768]{0,1:T(8,128)(2,1)}, bf16[256,768]{0,1:T(8,128)(2,1)}, u32[]{:S(2)}, u32[]{:S(2)}) collective-permute-start(bf16[256,768]{0,1:T(8,128)(2,1)} %get-tuple-element.16), channel_id=1, source_target_pairs={{0,128},{32,160},{64,192},{96,224},{128,0},{160,32},{192,64},{224,... | collective-permute-start | bytes 1179656 | tf_op jit(solution)/shard_map/ppermute | solution.py:52
  225.7 3.5 %fusion.45 = (bf16[4,256,768]{2,1,0:T(8,128)(2,1)S(1)}, f32[4,256,768]{2,1,0:T(8,128)}) fusion(bf16[4,256,768]{2,1,0:T(8,128)(2,1)} %collective-permute-done, bf16[4,2,256,768]{3,2,1,0:T(8,128)(2,1)S(1)} %bitcast.97, s32[]{:T(128)S(6)} %select_n.38), kind=kLoop, calls=%fused_computation.76 | loop fusion | flops 3145728 | bytes 7864324 | tf_op jit(solution)/shard_map/convert_element_type | solution.py:47
  234.9 7.9 %collective-permute-done.6 = bf16[256,768]{0,1:T(8,128)(2,1)} collective-permute-done((bf16[256,768]{0,1:T(8,128)(2,1)}, bf16[256,768]{0,1:T(8,128)(2,1)}, u32[]{:S(2)}, u32[]{:S(2)}) %collective-permute-start.6) | collective-permute-done | bytes 393248 | tf_op jit(solution)/shard_map/ppermute | solution.py:52
  245.3 5.9 %collective-permute-done.1 = bf16[256,768]{1,0:T(8,128)(2,1)} collective-permute-done((bf16[256,768]{1,0:T(8,128)(2,1)}, bf16[256,768]{1,0:T(8,128)(2,1)}, u32[]{:S(2)}, u32[]{:S(2)}) %collective-permute-start.1) | collective-permute-done | bytes 393248 | tf_op jit(solution)/shard_map/ppermute | solution.py:52
  251.2 8.1 %collective-permute-done.2 = bf16[256,768]{1,0:T(8,128)(2,1)} collective-permute-done((bf16[256,768]{1,0:T(8,128)(2,1)}, bf16[256,768]{1,0:T(8,128)(2,1)}, u32[]{:S(2)}, u32[]{:S(2)}) %collective-permute-start.2) | collective-permute-done | bytes 393248 | tf_op jit(solution)/shard_map/ppermute | solution.py:52
  261.7 2.8 %convolution_convert_fusion.3 = bf16[128,2048]{1,0:T(8,128)(2,1)} fusion(pred[128,512]{1,0:T(8,128)(4,1)S(1)} %fusion.37, bf16[512,2048]{1,0:T(8,128)(2,1)} %bitcast.8), kind=kOutput, calls=%fused_computation.25 | convolution fusion | flops 268697600 | bytes 2686976 | tf_op jit(solution)/shard_map/dot_general | solution.py:110
  (52 shorter events, 28.2 us)
Async XLA Ops:
  0.6 122.3 %copy-start = (bf16[1,2048,768]{2,1,0:T(8,128)(2,1)S(1)}, bf16[1,2048,768]{2,1,0:T(8,128)(2,1)}, u32[]{:S(2)}) copy-start(bf16[1,2048,768]{2,1,0:T(8,128)(2,1)} %param.13) | copy-start | bytes 9437188
  2.9 2.8 %copy-start.5 = (bf16[128,2048]{1,0:T(8,128)(2,1)S(1)}, bf16[128,2048]{1,0:T(8,128)(2,1)}, u32[]{:S(2)}) copy-start(bf16[128,2048]{1,0:T(8,128)(2,1)} %param.8) | copy-start | bytes 1572868
  9.0 106.2 %all-to-all-start = ((bf16[32,16,4096]{2,1,0:T(8,128)(2,1)}), bf16[32,16,4096]{2,1,0:T(8,128)(2,1)}, u32[]{:S(2)}, u32[]{:S(2)}) async-start(bf16[32,16,4096]{2,1,0:T(8,128)(2,1)} %bitcast.95), calls=%async_computation | async-start | bytes 8388608 | tf_op jit(solution)/shard_map/all_to_all | solution.py:67
  115.2 55.3 %all-to-all-start.1 = ((bf16[32,16,2048]{2,1,0:T(8,128)(2,1)}), bf16[32,16,2048]{2,1,0:T(8,128)(2,1)}, u32[]{:S(2)}, u32[]{:S(2)}) async-start(bf16[32,16,2048]{2,1,0:T(8,128)(2,1)} %bitcast.98), calls=%async_computation.1 | async-start | bytes 4194304 | tf_op jit(solution)/shard_map/all_to_all | solution.py:75
  122.9 4.7 %copy-start.7 = (bf16[1,2048,768]{2,1,0:T(8,128)(2,1)S(1)}, bf16[1,2048,768]{2,1,0:T(8,128)(2,1)}, u32[]{:S(2)}) copy-start(bf16[1,2048,768]{2,1,0:T(8,128)(2,1)} %param.15) | copy-start | bytes 9437188
  127.6 4.8 %copy-start.6 = (bf16[1,768,2048]{2,1,0:T(8,128)(2,1)S(1)}, bf16[1,768,2048]{2,1,0:T(8,128)(2,1)}, u32[]{:S(2)}) copy-start(bf16[1,768,2048]{2,1,0:T(8,128)(2,1)} %param.14) | copy-start | bytes 9437188
  170.5 6.6 %copy-start.8 = (f32[512,768]{1,0:T(8,128)S(1)}, f32[512,768]{1,0:T(8,128)}, u32[]{:S(2)}) copy-start(f32[512,768]{1,0:T(8,128)} %fusion.8) | copy-start | bytes 4718596
  185.2 29.0 %collective-permute-start.4 = (bf16[4,256,768]{1,2,0:T(8,128)(2,1)}, bf16[4,256,768]{1,2,0:T(8,128)(2,1)}, u32[]{:S(2)}, u32[]{:S(2)}) collective-permute-start(bf16[4,256,768]{1,2,0:T(8,128)(2,1)} %bitcast.101), channel_id=1, source_target_pairs={{0,32},{32,0},{64,96},{96,64},{128,160},{160,128},{192,224},{224,1... | collective-permute-start | bytes 4718600 | tf_op jit(solution)/shard_map/ppermute | solution.py:45
  185.2 4.0 %copy-start.3 = (bf16[512,768]{1,0:T(8,128)(2,1)S(1)}, bf16[512,768]{1,0:T(8,128)(2,1)}, u32[]{:S(2)}) copy-start(bf16[512,768]{1,0:T(8,128)(2,1)} %get-tuple-element.13) | copy-start | bytes 2359300
  192.5 69.2 %all-to-all-start.2 = ((bf16[32,16,2048]{2,1,0:T(8,128)(2,1)}), bf16[32,16,2048]{2,1,0:T(8,128)(2,1)}, u32[]{:S(2)}, u32[]{:S(2)}) async-start(bf16[32,16,2048]{2,1,0:T(8,128)(2,1)} %bitcast.100), calls=%async_computation.2 | async-start | bytes 4194304 | tf_op jit(solution)/shard_map/all_to_all | solution.py:101
  201.3 3.7 %copy-start.4 = (bf16[512,768]{1,0:T(8,128)(2,1)S(1)}, bf16[512,768]{1,0:T(8,128)(2,1)}, u32[]{:S(2)}) copy-start(bf16[512,768]{1,0:T(8,128)(2,1)} %get-tuple-element.13) | copy-start | bytes 2359300
  208.7 1.7 copy-start.1
  211.7 14.0 %collective-permute-start = (bf16[4,256,768]{2,1,0:T(8,128)(2,1)}, bf16[4,256,768]{2,1,0:T(8,128)(2,1)}, u32[]{:S(2)}, u32[]{:S(2)}) collective-permute-start(bf16[4,256,768]{2,1,0:T(8,128)(2,1)} %dynamic-slice_bitcast_fusion), channel_id=1, source_target_pairs={{0,32},{32,0},{64,96},{96,64},{128,160},{160,128},{192,224},{224,1... | collective-permute-start | bytes 4718600 | tf_op jit(solution)/shard_map/ppermute | solution.py:45
  218.2 7.5 %copy-start.2 = (bf16[2048,768]{1,0:T(8,128)(2,1)S(1)}, bf16[2048,768]{1,0:T(8,128)(2,1)}, u32[]{:S(2)}) copy-start(bf16[2048,768]{1,0:T(8,128)(2,1)} %copy-done.1) | copy-start | bytes 9437188
  219.7 13.0 %collective-permute-start.5 = (bf16[256,768]{0,1:T(8,128)(2,1)S(1)}, bf16[256,768]{0,1:T(8,128)(2,1)}, u32[]{:S(2)}, u32[]{:S(2)}) collective-permute-start(bf16[256,768]{0,1:T(8,128)(2,1)S(1)} %get-tuple-element.15), channel_id=1, source_target_pairs={{0,64},{32,96},{64,128},{96,160},{128,192},{160,224},{192,0},{224,... | collective-permute-start | bytes 1179656 | tf_op jit(solution)/shard_map/ppermute | solution.py:52
  221.2 21.7 %collective-permute-start.6 = (bf16[256,768]{0,1:T(8,128)(2,1)}, bf16[256,768]{0,1:T(8,128)(2,1)}, u32[]{:S(2)}, u32[]{:S(2)}) collective-permute-start(bf16[256,768]{0,1:T(8,128)(2,1)} %get-tuple-element.16), channel_id=1, source_target_pairs={{0,128},{32,160},{64,192},{96,224},{128,0},{160,32},{192,64},{224,... | collective-permute-start | bytes 1179656 | tf_op jit(solution)/shard_map/ppermute | solution.py:52
  224.3 18.5 %collective-permute-start.7 = (bf16[256,768]{0,1:T(8,128)(2,1)}, bf16[256,768]{0,1:T(8,128)(2,1)}, u32[]{:S(2)}, u32[]{:S(2)}) collective-permute-start(bf16[256,768]{0,1:T(8,128)(2,1)} %get-tuple-element.17), channel_id=1, source_target_pairs={{0,192},{32,224},{64,0},{96,32},{128,64},{160,96},{192,128},{224,1... | collective-permute-start | bytes 1179656 | tf_op jit(solution)/shard_map/ppermute | solution.py:52
  230.8 20.4 %collective-permute-start.1 = (bf16[256,768]{1,0:T(8,128)(2,1)}, bf16[256,768]{1,0:T(8,128)(2,1)}, u32[]{:S(2)}, u32[]{:S(2)}) collective-permute-start(bf16[256,768]{1,0:T(8,128)(2,1)} %get-tuple-element.18), channel_id=1, source_target_pairs={{0,64},{32,96},{64,128},{96,160},{128,192},{160,224},{192,0},{224,... | collective-permute-start | bytes 1179656 | tf_op jit(solution)/shard_map/ppermute | solution.py:52
  231.4 27.8 %collective-permute-start.2 = (bf16[256,768]{1,0:T(8,128)(2,1)}, bf16[256,768]{1,0:T(8,128)(2,1)}, u32[]{:S(2)}, u32[]{:S(2)}) collective-permute-start(bf16[256,768]{1,0:T(8,128)(2,1)} %get-tuple-element.19), channel_id=1, source_target_pairs={{0,128},{32,160},{64,192},{96,224},{128,0},{160,32},{192,64},{224,... | collective-permute-start | bytes 1179656 | tf_op jit(solution)/shard_map/ppermute | solution.py:52
  232.7 26.5 %collective-permute-start.3 = (bf16[256,768]{1,0:T(8,128)(2,1)}, bf16[256,768]{1,0:T(8,128)(2,1)}, u32[]{:S(2)}, u32[]{:S(2)}) collective-permute-start(bf16[256,768]{1,0:T(8,128)(2,1)} %get-tuple-element.20), channel_id=1, source_target_pairs={{0,192},{32,224},{64,0},{96,32},{128,64},{160,96},{192,128},{224,1... | collective-permute-start | bytes 1179656 | tf_op jit(solution)/shard_map/ppermute | solution.py:52

commit v8 on v7

--- a/solution.py
+++ b/solution.py
@@ -98,6 +98,9 @@
     input_hvp = (jnp.dot(back_tan, up_proj.T, preferred_element_type=jnp.float32) + hvp_mix).astype(
         jnp.bfloat16
     )
+    input_hvp, back_pre, back_tan, hidden_tan = lax.optimization_barrier(
+        (input_hvp, back_pre, back_tan, hidden_tan)
+    )
     returned = lax.all_to_all(
         input_hvp.reshape(expert_count, capacity, width),
         "expert",

time: 265 us -> 259 us (0.977)
  local copies, waits for them, and re-layouts: 13.4 us -> 9.13 us
where the time goes in v8:
time: 259 us
  waiting for transfers between devices  146 us (56%)
  matrix products  45.6 us (18%)
  starting transfers between devices  38.6 us (15%)
  other arithmetic  17.9 us (7%)
  local copies, waits for them, and re-layouts  9.13 us (4%)
    all_to_all x1, waiting for transfers between devices, per_device(): lax.all_to_all(send_xg.reshape(expert_count, capacity, 2 * width), 'exper...  91.3 us
    all_to_all x1, waiting for transfers between devices, per_device(): lax.all_to_all(send_tan.reshape(expert_count, capacity, width), 'expert',...  32.7 us
    ppermute x6, waiting for transfers between devices, reduce_over_dp(): total = total + lax.ppermute(wire[step], 'dp', pairs).astype(jnp.float32)  22.4 us
    all_to_all x1, starting transfers between devices, per_device(): lax.all_to_all(send_xg.reshape(expert_count, capacity, 2 * width), 'exper...  11.7 us
    ppermute x6, starting transfers between devices, reduce_over_dp(): total = total + lax.ppermute(wire[step], 'dp', pairs).astype(jnp.float32)  10.1 us
    all_to_all x1, starting transfers between devices, per_device(): lax.all_to_all(input_hvp.reshape(expert_count, capacity, width), 'expert'...  8.76 us
    all_to_all x1, starting transfers between devices, per_device(): lax.all_to_all(send_tan.reshape(expert_count, capacity, width), 'expert',...  7.6 us
    dot_general x1, matrix products, per_device(): jnp.dot(tangent, up_proj, preferred_element_type=jnp.float32) + pre_mix  6.47 us
  transfers between devices with their start and end apart: 11, of which 6 were waited for; matrix products, arithmetic and copies ran while one was open for 19% of the time, Pallas kernels for 0%

profile of v8, /device:TPU:2, one launch (start us, length us, event | category | flops | bytes accessed | tf_op | source)
XLA Modules:
  0.0 258.5 jit_solution(5648580078790449691)
XLA Ops:
  9.0 11.7 %all-to-all-start = ((bf16[32,16,4096]{2,1,0:T(8,128)(2,1)}), bf16[32,16,4096]{2,1,0:T(8,128)(2,1)}, u32[]{:S(2)}, u32[]{:S(2)}) async-start(bf16[32,16,4096]{2,1,0:T(8,128)(2,1)} %bitcast.96), calls=%async_computation | async-start | bytes 8388608 | tf_op jit(solution)/shard_map/all_to_all | solution.py:67
  20.7 3.2 %convolution_convert_fusion.1 = bf16[512,2048]{1,0:T(8,128)(2,1)} fusion(pred[128,512]{1,0:T(8,128)(4,1)S(1)} %fusion.37, bf16[128,2048]{1,0:T(8,128)(2,1)} %param.9), kind=kOutput, calls=%fused_computation.23 | convolution fusion | flops 269484032 | bytes 2686976 | tf_op jit(solution)/shard_map/dot_general | solution.py:32
  23.9 91.3 %all-to-all-done = bf16[32,16,4096]{2,1,0:T(8,128)(2,1)} async-done(((bf16[32,16,4096]{2,1,0:T(8,128)(2,1)}), bf16[32,16,4096]{2,1,0:T(8,128)(2,1)}, u32[]{:S(2)}, u32[]{:S(2)}) %all-to-all-start) | async-done | bytes 4194336 | tf_op jit(solution)/shard_map/all_to_all | solution.py:67
  115.2 7.6 %all-to-all-start.1 = ((bf16[32,16,2048]{2,1,0:T(8,128)(2,1)}), bf16[32,16,2048]{2,1,0:T(8,128)(2,1)}, u32[]{:S(2)}, u32[]{:S(2)}) async-start(bf16[32,16,2048]{2,1,0:T(8,128)(2,1)} %bitcast.99), calls=%async_computation.1 | async-start | bytes 4194304 | tf_op jit(solution)/shard_map/all_to_all | solution.py:75
  122.8 5.6 %fusion.2 = f32[512,768]{1,0:T(8,128)} fusion(bf16[1,2048,768]{2,1,0:T(8,128)(2,1)} %param.15, bf16[512,4096]{1,0:T(8,128)(2,1)} %bitcast.1), kind=kOutput, calls=%fused_computation.12 | convolution fusion | flops 1610612736 | bytes 6815744 | tf_op jit(solution)/shard_map/dot_general | solution.py:93
  128.4 4.7 %fusion.8 = f32[512,768]{1,0:T(8,128)} fusion(bf16[1,2048,768]{2,1,0:T(8,128)(2,1)S(1)} %copy-done, bf16[512,4096]{1,0:T(8,128)(2,1)} %bitcast.1), kind=kOutput, calls=%fused_computation.18 | convolution fusion | flops 1610612736 | bytes 6815744 | tf_op jit(solution)/shard_map/dot_general | solution.py:87
  133.1 4.6 %fusion.10 = f32[512,768]{1,0:T(8,128)} fusion(bf16[1,768,2048]{2,1,0:T(8,128)(2,1)S(1)} %copy-done.7, bf16[512,4096]{1,0:T(8,128)(2,1)} %bitcast.1), kind=kOutput, calls=%fused_computation.20 | convolution fusion | flops 1610612736 | bytes 6815744 | tf_op jit(solution)/shard_map/dot_general | solution.py:91
  137.6 32.7 %all-to-all-done.1 = bf16[32,16,2048]{2,1,0:T(8,128)(2,1)} async-done(((bf16[32,16,2048]{2,1,0:T(8,128)(2,1)}), bf16[32,16,2048]{2,1,0:T(8,128)(2,1)}, u32[]{:S(2)}, u32[]{:S(2)}) %all-to-all-start.1) | async-done | bytes 2097184 | tf_op jit(solution)/shard_map/all_to_all | solution.py:75
  170.3 6.5 %multiply_convert_fusion.2 = (bf16[512,768]{1,0:T(8,128)(2,1)}, bf16[512,768]{1,0:T(8,128)(2,1)S(1)}, bf16[512,768]{1,0:T(8,128)(2,1)S(1)}) fusion(f32[512,768]{1,0:T(8,128)} %fusion.8, f32[512,768]{1,0:T(8,128)} %fusion.10, f32[512,768]{1,0:T(8,128)} %fusion.2, bf16[512,2048]{1,0:T(8,128)(2,1)} %bitcast.5, bf16[1,2048,768]{2,1,0:T(8,128)(2,1)S(1)} %copy-done), kind=kOutput, calls=%fused_computation.42 | convolution fusion | flops 1618870272 | bytes 12320768 | tf_op jit(solution)/shard_map/dot_general | solution.py:95
  178.7 3.2 %add_convert_fusion = bf16[512,2048]{1,0:T(8,128)(2,1)} fusion(f32[512,2048]{1,0:T(8,128)S(1)} %fusion, bf16[512,768]{1,0:T(8,128)(2,1)S(1)} %get-tuple-element.13, bf16[1,2048,768]{2,1,0:T(8,128)(2,1)S(1)} %copy-done), kind=kOutput, calls=%fused_computation.3 | convolution fusion | flops 1612709888 | bytes 10223616 | tf_op jit(solution)/shard_map/dot_general | solution.py:98
  181.9 8.8 %all-to-all-start.2 = ((bf16[32,16,2048]{2,1,0:T(8,128)(2,1)}), bf16[32,16,2048]{2,1,0:T(8,128)(2,1)}, u32[]{:S(2)}, u32[]{:S(2)}) async-start(bf16[32,16,2048]{2,1,0:T(8,128)(2,1)} %bitcast.101), calls=%async_computation.2 | async-start | bytes 4194304 | tf_op jit(solution)/shard_map/all_to_all | solution.py:104
  190.7 3.4 %multiply_convert_fusion = bf16[2048,768]{1,0:T(8,128)(2,1)S(1)} fusion(bf16[512,768]{1,0:T(8,128)(2,1)S(1)} %copy-done.9, bf16[512,4096]{1,0:T(8,128)(2,1)} %bitcast.1), kind=kOutput, calls=%fused_computation | convolution fusion | flops 1613758464 | bytes 6029312 | tf_op jit(solution)/shard_map/dot_general | solution.py:111
  197.1 3.5 %fusion.45 = f32[2048,768]{1,0:T(8,128)S(1)} fusion(bf16[512,2048]{1,0:T(8,128)(2,1)} %bitcast.5, bf16[512,768]{1,0:T(8,128)(2,1)S(1)} %copy-done.5), kind=kOutput, calls=%fused_computation.77 | convolution fusion | flops 1610612736 | bytes 9175040 | tf_op jit(solution)/shard_map/dot_general | solution.py:114
  200.6 3.6 %multiply_convert_fusion.1 = bf16[2048,768]{1,0:T(8,128)(2,1)S(1)} fusion(f32[2048,768]{1,0:T(8,128)S(1)} %fusion.45, bf16[512,768]{1,0:T(8,128)(2,1)S(1)} %copy-done.3, bf16[512,4096]{1,0:T(8,128)(2,1)} %bitcast.1), kind=kOutput, calls=%fused_computation.1 | convolution fusion | flops 1615331328 | bytes 12320768 | tf_op jit(solution)/shard_map/dot_general | solution.py:114
  205.9 2.6 %copy.36 = bf16[4,1,256,768]{2,3,0,1:T(8,128)(2,1)} copy(bf16[4,1,256,768]{3,2,1,0:T(8,128)(2,1)} %get-tuple-element.19) | data formatting | bytes 3145728
  208.5 3.9 %convert_add_fusion = (f32[4,256,768]{1,2,0:T(8,128)}, bf16[4,256,768]{1,2,0:T(8,128)(2,1)S(1)}) fusion(bf16[4,256,768]{1,2,0:T(8,128)(2,1)} %collective-permute-done.4, bf16[4,1,256,768]{2,3,0,1:T(8,128)(2,1)} %copy.36), kind=kLoop, calls=%fused_computation.8 | loop fusion | flops 3145728 | bytes 7864320 | tf_op jit(solution)/shard_map/add | solution.py:46
  215.6 3.0 %collective-permute-start.6 = (bf16[256,768]{0,1:T(8,128)(2,1)}, bf16[256,768]{0,1:T(8,128)(2,1)}, u32[]{:S(2)}, u32[]{:S(2)}) collective-permute-start(bf16[256,768]{0,1:T(8,128)(2,1)} %get-tuple-element.25), channel_id=1, source_target_pairs={{0,128},{32,160},{64,192},{96,224},{128,0},{160,32},{192,64},{224,... | collective-permute-start | bytes 1179656 | tf_op jit(solution)/shard_map/ppermute | solution.py:52
  220.0 3.5 %fusion.44 = (bf16[4,256,768]{2,1,0:T(8,128)(2,1)S(1)}, f32[4,256,768]{2,1,0:T(8,128)}) fusion(bf16[4,256,768]{2,1,0:T(8,128)(2,1)} %collective-permute-done, bf16[4,2,256,768]{3,2,1,0:T(8,128)(2,1)S(1)} %bitcast.98, s32[]{:T(128)S(6)} %select_n.38), kind=kLoop, calls=%fused_computation.76 | loop fusion | flops 3145728 | bytes 7864324 | tf_op jit(solution)/shard_map/convert_element_type | solution.py:47
  226.6 2.6 %collective-permute-start.3 = (bf16[256,768]{1,0:T(8,128)(2,1)S(1)}, bf16[256,768]{1,0:T(8,128)(2,1)}, u32[]{:S(2)}, u32[]{:S(2)}) collective-permute-start(bf16[256,768]{1,0:T(8,128)(2,1)S(1)} %get-tuple-element.29), channel_id=1, source_target_pairs={{0,192},{32,224},{64,0},{96,32},{128,64},{160,96},{192,128},{224,1... | collective-permute-start | bytes 1179656 | tf_op jit(solution)/shard_map/ppermute | solution.py:52
  229.2 7.9 %collective-permute-done.6 = bf16[256,768]{0,1:T(8,128)(2,1)} collective-permute-done((bf16[256,768]{0,1:T(8,128)(2,1)}, bf16[256,768]{0,1:T(8,128)(2,1)}, u32[]{:S(2)}, u32[]{:S(2)}) %collective-permute-start.6) | collective-permute-done | bytes 393248 | tf_op jit(solution)/shard_map/ppermute | solution.py:52
  239.6 4.6 %collective-permute-done.1 = bf16[256,768]{1,0:T(8,128)(2,1)} collective-permute-done((bf16[256,768]{1,0:T(8,128)(2,1)S(1)}, bf16[256,768]{1,0:T(8,128)(2,1)}, u32[]{:S(2)}, u32[]{:S(2)}) %collective-permute-start.1) | collective-permute-done | bytes 393248 | tf_op jit(solution)/shard_map/ppermute | solution.py:52
  244.2 9.0 %collective-permute-done.2 = bf16[256,768]{1,0:T(8,128)(2,1)} collective-permute-done((bf16[256,768]{1,0:T(8,128)(2,1)S(1)}, bf16[256,768]{1,0:T(8,128)(2,1)}, u32[]{:S(2)}, u32[]{:S(2)}) %collective-permute-start.2) | collective-permute-done | bytes 393248 | tf_op jit(solution)/shard_map/ppermute | solution.py:52
  253.1 2.6 fusion.38
  255.7 2.8 %convolution_convert_fusion.3 = bf16[128,2048]{1,0:T(8,128)(2,1)} fusion(pred[128,512]{1,0:T(8,128)(4,1)S(1)} %fusion.37, bf16[512,2048]{1,0:T(8,128)(2,1)} %bitcast.8), kind=kOutput, calls=%fused_computation.25 | convolution fusion | flops 268697600 | bytes 2686976 | tf_op jit(solution)/shard_map/dot_general | solution.py:113
  (54 shorter events, 24.8 us)
Async XLA Ops:
  0.6 127.8 %copy-start = (bf16[1,2048,768]{2,1,0:T(8,128)(2,1)S(1)}, bf16[1,2048,768]{2,1,0:T(8,128)(2,1)}, u32[]{:S(2)}) copy-start(bf16[1,2048,768]{2,1,0:T(8,128)(2,1)} %param.13) | copy-start | bytes 9437188
  2.9 2.8 %copy-start.6 = (bf16[128,2048]{1,0:T(8,128)(2,1)S(1)}, bf16[128,2048]{1,0:T(8,128)(2,1)}, u32[]{:S(2)}) copy-start(bf16[128,2048]{1,0:T(8,128)(2,1)} %param.8) | copy-start | bytes 1572868
  9.0 106.2 %all-to-all-start = ((bf16[32,16,4096]{2,1,0:T(8,128)(2,1)}), bf16[32,16,4096]{2,1,0:T(8,128)(2,1)}, u32[]{:S(2)}, u32[]{:S(2)}) async-start(bf16[32,16,4096]{2,1,0:T(8,128)(2,1)} %bitcast.96), calls=%async_computation | async-start | bytes 8388608 | tf_op jit(solution)/shard_map/all_to_all | solution.py:67
  115.2 55.1 %all-to-all-start.1 = ((bf16[32,16,2048]{2,1,0:T(8,128)(2,1)}), bf16[32,16,2048]{2,1,0:T(8,128)(2,1)}, u32[]{:S(2)}, u32[]{:S(2)}) async-start(bf16[32,16,2048]{2,1,0:T(8,128)(2,1)} %bitcast.99), calls=%async_computation.1 | async-start | bytes 4194304 | tf_op jit(solution)/shard_map/all_to_all | solution.py:75
  128.4 4.7 %copy-start.7 = (bf16[1,768,2048]{2,1,0:T(8,128)(2,1)S(1)}, bf16[1,768,2048]{2,1,0:T(8,128)(2,1)}, u32[]{:S(2)}) copy-start(bf16[1,768,2048]{2,1,0:T(8,128)(2,1)} %param.14) | copy-start | bytes 9437188
  170.3 6.5 %copy-start.8 = (bf16[1,2048,768]{2,1,0:T(8,128)(2,1)S(1)}, bf16[1,2048,768]{2,1,0:T(8,128)(2,1)}, u32[]{:S(2)}) copy-start(bf16[1,2048,768]{2,1,0:T(8,128)(2,1)} %param.15) | copy-start | bytes 9437188
  176.8 1.8 copy-start.4
  176.8 1.8 copy-start.2
  181.9 8.8 %copy-start.9 = (bf16[512,768]{1,0:T(8,128)(2,1)S(1)}, bf16[512,768]{1,0:T(8,128)(2,1)}, u32[]{:S(2)}) copy-start(bf16[512,768]{1,0:T(8,128)(2,1)} %get-tuple-element.14) | copy-start | bytes 2359300
  181.9 73.8 %all-to-all-start.2 = ((bf16[32,16,2048]{2,1,0:T(8,128)(2,1)}), bf16[32,16,2048]{2,1,0:T(8,128)(2,1)}, u32[]{:S(2)}, u32[]{:S(2)}) async-start(bf16[32,16,2048]{2,1,0:T(8,128)(2,1)} %bitcast.101), calls=%async_computation.2 | async-start | bytes 4194304 | tf_op jit(solution)/shard_map/all_to_all | solution.py:104
  195.5 1.6 copy-start.5
  197.0 3.6 %copy-start.3 = (bf16[512,768]{1,0:T(8,128)(2,1)S(1)}, bf16[512,768]{1,0:T(8,128)(2,1)}, u32[]{:S(2)}) copy-start(bf16[512,768]{1,0:T(8,128)(2,1)} %copy-done.2) | copy-start | bytes 2359300
  197.0 11.5 %collective-permute-start.4 = (bf16[4,256,768]{1,2,0:T(8,128)(2,1)}, bf16[4,256,768]{1,2,0:T(8,128)(2,1)}, u32[]{:S(2)}, u32[]{:S(2)}) collective-permute-start(bf16[4,256,768]{1,2,0:T(8,128)(2,1)} %bitcast.19), channel_id=1, source_target_pairs={{0,32},{32,0},{64,96},{96,64},{128,160},{160,128},{192,224},{224,1... | collective-permute-start | bytes 4718600 | tf_op jit(solution)/shard_map/ppermute | solution.py:45
  205.5 14.5 %collective-permute-start = (bf16[4,256,768]{2,1,0:T(8,128)(2,1)}, bf16[4,256,768]{2,1,0:T(8,128)(2,1)}, u32[]{:S(2)}, u32[]{:S(2)}) collective-permute-start(bf16[4,256,768]{2,1,0:T(8,128)(2,1)} %dynamic-slice_bitcast_fusion), channel_id=1, source_target_pairs={{0,32},{32,0},{64,96},{96,64},{128,160},{160,128},{192,224},{224,1... | collective-permute-start | bytes 4718600 | tf_op jit(solution)/shard_map/ppermute | solution.py:45
  214.0 12.6 %collective-permute-start.5 = (bf16[256,768]{0,1:T(8,128)(2,1)S(1)}, bf16[256,768]{0,1:T(8,128)(2,1)}, u32[]{:S(2)}, u32[]{:S(2)}) collective-permute-start(bf16[256,768]{0,1:T(8,128)(2,1)S(1)} %get-tuple-element.24), channel_id=1, source_target_pairs={{0,64},{32,96},{64,128},{96,160},{128,192},{160,224},{192,0},{224,... | collective-permute-start | bytes 1179656 | tf_op jit(solution)/shard_map/ppermute | solution.py:52
  215.6 21.6 %collective-permute-start.6 = (bf16[256,768]{0,1:T(8,128)(2,1)}, bf16[256,768]{0,1:T(8,128)(2,1)}, u32[]{:S(2)}, u32[]{:S(2)}) collective-permute-start(bf16[256,768]{0,1:T(8,128)(2,1)} %get-tuple-element.25), channel_id=1, source_target_pairs={{0,128},{32,160},{64,192},{96,224},{128,0},{160,32},{192,64},{224,... | collective-permute-start | bytes 1179656 | tf_op jit(solution)/shard_map/ppermute | solution.py:52
  218.6 18.5 %collective-permute-start.7 = (bf16[256,768]{0,1:T(8,128)(2,1)}, bf16[256,768]{0,1:T(8,128)(2,1)}, u32[]{:S(2)}, u32[]{:S(2)}) collective-permute-start(bf16[256,768]{0,1:T(8,128)(2,1)} %get-tuple-element.26), channel_id=1, source_target_pairs={{0,192},{32,224},{64,0},{96,32},{128,64},{160,96},{192,128},{224,1... | collective-permute-start | bytes 1179656 | tf_op jit(solution)/shard_map/ppermute | solution.py:52
  224.1 20.0 %collective-permute-start.1 = (bf16[256,768]{1,0:T(8,128)(2,1)S(1)}, bf16[256,768]{1,0:T(8,128)(2,1)}, u32[]{:S(2)}, u32[]{:S(2)}) collective-permute-start(bf16[256,768]{1,0:T(8,128)(2,1)S(1)} %get-tuple-element.27), channel_id=1, source_target_pairs={{0,64},{32,96},{64,128},{96,160},{128,192},{160,224},{192,0},{224,... | collective-permute-start | bytes 1179656 | tf_op jit(solution)/shard_map/ppermute | solution.py:52
  224.9 28.2 %collective-permute-start.2 = (bf16[256,768]{1,0:T(8,128)(2,1)S(1)}, bf16[256,768]{1,0:T(8,128)(2,1)}, u32[]{:S(2)}, u32[]{:S(2)}) collective-permute-start(bf16[256,768]{1,0:T(8,128)(2,1)S(1)} %get-tuple-element.28), channel_id=1, source_target_pairs={{0,128},{32,160},{64,192},{96,224},{128,0},{160,32},{192,64},{224,... | collective-permute-start | bytes 1179656 | tf_op jit(solution)/shard_map/ppermute | solution.py:52
  226.6 26.5 %collective-permute-start.3 = (bf16[256,768]{1,0:T(8,128)(2,1)S(1)}, bf16[256,768]{1,0:T(8,128)(2,1)}, u32[]{:S(2)}, u32[]{:S(2)}) collective-permute-start(bf16[256,768]{1,0:T(8,128)(2,1)S(1)} %get-tuple-element.29), channel_id=1, source_target_pairs={{0,192},{32,224},{64,0},{96,32},{128,64},{160,96},{192,128},{224,1... | collective-permute-start | bytes 1179656 | tf_op jit(solution)/shard_map/ppermute | solution.py:52
  253.1 5.4 %copy-start.1 = (bf16[1,2048,768]{2,1,0:T(8,128)(2,1)S(1)}, bf16[1,2048,768]{2,1,0:T(8,128)(2,1)}, u32[]{:S(2)}) copy-start(bf16[1,2048,768]{2,1,0:T(8,128)(2,1)} %param.13) | copy-start | bytes 9437188

commit v9 on v8

--- a/solution.py
+++ b/solution.py
@@ -22,10 +22,8 @@
     slot_ids = jnp.arange(slots, dtype=jnp.int32)
     hit = target[:, :, None] == slot_ids[None, None, :]
     pick = jnp.any(hit, axis=1).astype(jnp.bfloat16)
-    gate_pick = jnp.sum(
-        jnp.where(hit, gate_rows.astype(jnp.float32)[:, :, None], 0.0), axis=1
-    ).astype(jnp.bfloat16)
-    return pick, gate_pick
+    gate_slot = jnp.sum(jnp.where(hit, gate_rows.astype(jnp.float32)[:, :, None], 0.0), axis=(0, 1))
+    return pick, gate_slot
 
 
 def to_slots(pick, rows):
@@ -61,8 +59,15 @@
     capacity = max(2, token_count * route_count * 2 // expert_count)
     scale = 1.0 / math.sqrt(token_count * route_count * replicas)
     slots = expert_count * capacity
-    pick, gate_pick = slot_matrices(routes, gates, expert_count, capacity)
-    send_xg = jnp.concatenate([to_slots(pick, tokens), to_slots(gate_pick, cotangents)], axis=1)
+    pick, gate_slot = slot_matrices(routes, gates, expert_count, capacity)
+    rows_xg = lax.dot_general(
+        pick,
+        jnp.concatenate([tokens, cotangents], axis=1),
+        (((0,), (0,)), ((), ())),
+        preferred_element_type=jnp.float32,
+    )
+    column = jnp.arange(2 * width, dtype=jnp.int32)[None, :]
+    send_xg = (rows_xg * jnp.where(column < width, 1.0, gate_slot[:, None])).astype(jnp.bfloat16)
     send_tan = to_slots(pick, tangents)
     recv_xg = lax.all_to_all(
         send_xg.reshape(expert_count, capacity, 2 * width),

time: 259 us -> 259 us (level)
  other arithmetic: 17.9 us -> 15.3 us
    dot_general x0 -> x1, matrix products: none -> 4.49 us  [per_device(): lax.dot_general(pick, jnp.concatenate([tokens, cotangents], axis=1), (((0...]
    dot_general x3 -> x1, matrix products: 5.71 us -> 3.19 us  [to_slots(): lax.dot_general(pick, rows, (((0,), (0,)), ((), ())), preferred_element_t...]
where the time goes in v9:
time: 259 us; the launch traced here: 258 us
  waiting for transfers between devices  146 us (56%)
  matrix products  47.6 us (18%)
  starting transfers between devices  38.7 us (15%)
  other arithmetic  15.3 us (6%)
  local copies, waits for them, and re-layouts  9.13 us (4%)
    all_to_all x1, waiting for transfers between devices, per_device(): lax.all_to_all(send_xg.reshape(expert_count, capacity, 2 * width), 'exper...  91.3 us
    all_to_all x1, waiting for transfers between devices, per_device(): lax.all_to_all(send_tan.reshape(expert_count, capacity, width), 'expert',...  32.7 us
    ppermute x6, waiting for transfers between devices, reduce_over_dp(): total = total + lax.ppermute(wire[step], 'dp', pairs).astype(jnp.float32)  22.4 us
    all_to_all x1, starting transfers between devices, per_device(): lax.all_to_all(send_xg.reshape(expert_count, capacity, 2 * width), 'exper...  11.7 us
    ppermute x6, starting transfers between devices, reduce_over_dp(): total = total + lax.ppermute(wire[step], 'dp', pairs).astype(jnp.float32)  10.2 us
    all_to_all x1, starting transfers between devices, per_device(): lax.all_to_all(input_hvp.reshape(expert_count, capacity, width), 'expert'...  8.77 us
    all_to_all x1, starting transfers between devices, per_device(): lax.all_to_all(send_tan.reshape(expert_count, capacity, width), 'expert',...  7.6 us
    dot_general x1, matrix products, per_device(): jnp.dot(tangent, up_proj, preferred_element_type=jnp.float32) + pre_mix  6.45 us
  transfers between devices with their start and end apart: 11, of which 6 were waited for; matrix products, arithmetic and copies ran while one was open for 19% of the time, Pallas kernels for 0%

profile of v9, /device:TPU:2, one launch (start us, length us, event | category | flops | bytes accessed | tf_op | source)
XLA Modules:
  0.0 258.0 jit_solution(6740524334182778016)
XLA Ops:
  3.9 4.5 %multiply_convert_fusion = bf16[512,4096]{1,0:T(8,128)(2,1)} fusion(pred[128,512]{1,0:T(8,128)(4,1)S(1)} %fusion.40, f32[512]{0:T(512)S(1)} %select_reduce_fusion, pred[4096]{0:T(1024)(128)(4,1)S(1)} %iota_compare_fusion.5, bf16[128,2048]{1,0:T(8,128)(2,1)} %param.10, bf16[128,2048]{1,0:T(8,128)(2,1)} %param.8), kind=kOutput, calls=%fused_computation | convolution fusion | flops 545259520 | bytes 5314560 | tf_op jit(solution)/shard_map/dot_general | solution.py:63
  8.4 11.7 %all-to-all-start = ((bf16[32,16,4096]{2,1,0:T(8,128)(2,1)}), bf16[32,16,4096]{2,1,0:T(8,128)(2,1)}, u32[]{:S(2)}, u32[]{:S(2)}) async-start(bf16[32,16,4096]{2,1,0:T(8,128)(2,1)} %bitcast.96), calls=%async_computation | async-start | bytes 8388608 | tf_op jit(solution)/shard_map/all_to_all | solution.py:72
  20.1 3.2 %convolution_convert_fusion = bf16[512,2048]{1,0:T(8,128)(2,1)} fusion(pred[128,512]{1,0:T(8,128)(4,1)S(1)} %fusion.40, bf16[128,2048]{1,0:T(8,128)(2,1)} %param.9), kind=kOutput, calls=%fused_computation.22 | convolution fusion | flops 269484032 | bytes 2686976 | tf_op jit(solution)/shard_map/dot_general | solution.py:30
  23.3 91.3 %all-to-all-done = bf16[32,16,4096]{2,1,0:T(8,128)(2,1)} async-done(((bf16[32,16,4096]{2,1,0:T(8,128)(2,1)}), bf16[32,16,4096]{2,1,0:T(8,128)(2,1)}, u32[]{:S(2)}, u32[]{:S(2)}) %all-to-all-start) | async-done | bytes 4194336 | tf_op jit(solution)/shard_map/all_to_all | solution.py:72
  114.6 7.6 %all-to-all-start.1 = ((bf16[32,16,2048]{2,1,0:T(8,128)(2,1)}), bf16[32,16,2048]{2,1,0:T(8,128)(2,1)}, u32[]{:S(2)}, u32[]{:S(2)}) async-start(bf16[32,16,2048]{2,1,0:T(8,128)(2,1)} %bitcast.95), calls=%async_computation.1 | async-start | bytes 4194304 | tf_op jit(solution)/shard_map/all_to_all | solution.py:80
  122.2 5.5 %fusion.2 = f32[512,768]{1,0:T(8,128)} fusion(bf16[1,2048,768]{2,1,0:T(8,128)(2,1)} %param.15, bf16[512,4096]{1,0:T(8,128)(2,1)} %bitcast.1), kind=kOutput, calls=%fused_computation.12 | convolution fusion | flops 1610612736 | bytes 6815744 | tf_op jit(solution)/shard_map/dot_general | solution.py:98
  127.8 4.7 %fusion.8 = f32[512,768]{1,0:T(8,128)} fusion(bf16[1,2048,768]{2,1,0:T(8,128)(2,1)S(1)} %copy-done, bf16[512,4096]{1,0:T(8,128)(2,1)} %bitcast.1), kind=kOutput, calls=%fused_computation.18 | convolution fusion | flops 1610612736 | bytes 6815744 | tf_op jit(solution)/shard_map/dot_general | solution.py:92
  132.4 4.6 %fusion.10 = f32[512,768]{1,0:T(8,128)} fusion(bf16[1,768,2048]{2,1,0:T(8,128)(2,1)S(1)} %copy-done.6, bf16[512,4096]{1,0:T(8,128)(2,1)} %bitcast.1), kind=kOutput, calls=%fused_computation.20 | convolution fusion | flops 1610612736 | bytes 6815744 | tf_op jit(solution)/shard_map/dot_general | solution.py:96
  137.0 32.7 %all-to-all-done.1 = bf16[32,16,2048]{2,1,0:T(8,128)(2,1)} async-done(((bf16[32,16,2048]{2,1,0:T(8,128)(2,1)}), bf16[32,16,2048]{2,1,0:T(8,128)(2,1)}, u32[]{:S(2)}, u32[]{:S(2)}) %all-to-all-start.1) | async-done | bytes 2097184 | tf_op jit(solution)/shard_map/all_to_all | solution.py:80
  169.7 6.5 %multiply_convert_fusion.3 = (bf16[512,768]{1,0:T(8,128)(2,1)}, bf16[512,768]{1,0:T(8,128)(2,1)S(1)}, bf16[512,768]{1,0:T(8,128)(2,1)S(1)}) fusion(f32[512,768]{1,0:T(8,128)} %fusion.8, f32[512,768]{1,0:T(8,128)} %fusion.10, f32[512,768]{1,0:T(8,128)} %fusion.2, bf16[512,2048]{1,0:T(8,128)(2,1)} %bitcast.5, bf16[1,2048,768]{2,1,0:T(8,128)(2,1)S(1)} %copy-done), kind=kOutput, calls=%fused_computation.40 | convolution fusion | flops 1618870272 | bytes 12320768 | tf_op jit(solution)/shard_map/dot_general | solution.py:100
  178.1 3.2 %add_convert_fusion = bf16[512,2048]{1,0:T(8,128)(2,1)} fusion(f32[512,2048]{1,0:T(8,128)S(1)} %fusion, bf16[512,768]{1,0:T(8,128)(2,1)S(1)} %get-tuple-element.13, bf16[1,2048,768]{2,1,0:T(8,128)(2,1)S(1)} %copy-done), kind=kOutput, calls=%fused_computation.3 | convolution fusion | flops 1612709888 | bytes 10223616 | tf_op jit(solution)/shard_map/dot_general | solution.py:103
  181.3 8.8 %all-to-all-start.2 = ((bf16[32,16,2048]{2,1,0:T(8,128)(2,1)}), bf16[32,16,2048]{2,1,0:T(8,128)(2,1)}, u32[]{:S(2)}, u32[]{:S(2)}) async-start(bf16[32,16,2048]{2,1,0:T(8,128)(2,1)} %bitcast.98), calls=%async_computation.2 | async-start | bytes 4194304 | tf_op jit(solution)/shard_map/all_to_all | solution.py:109
  190.1 3.4 %multiply_convert_fusion.1 = bf16[2048,768]{1,0:T(8,128)(2,1)S(1)} fusion(bf16[512,768]{1,0:T(8,128)(2,1)S(1)} %copy-done.8, bf16[512,4096]{1,0:T(8,128)(2,1)} %bitcast.1), kind=kOutput, calls=%fused_computation.1 | convolution fusion | flops 1613758464 | bytes 6029312 | tf_op jit(solution)/shard_map/dot_general | solution.py:116
  196.5 3.5 %fusion.48 = f32[2048,768]{1,0:T(8,128)S(1)} fusion(bf16[512,2048]{1,0:T(8,128)(2,1)} %bitcast.5, bf16[512,768]{1,0:T(8,128)(2,1)S(1)} %copy-done.5), kind=kOutput, calls=%fused_computation.79 | convolution fusion | flops 1610612736 | bytes 9175040 | tf_op jit(solution)/shard_map/dot_general | solution.py:119
  200.0 3.6 %multiply_convert_fusion.2 = bf16[2048,768]{1,0:T(8,128)(2,1)S(1)} fusion(f32[2048,768]{1,0:T(8,128)S(1)} %fusion.48, bf16[512,768]{1,0:T(8,128)(2,1)S(1)} %copy-done.3, bf16[512,4096]{1,0:T(8,128)(2,1)} %bitcast.1), kind=kOutput, calls=%fused_computation.2 | convolution fusion | flops 1615331328 | bytes 12320768 | tf_op jit(solution)/shard_map/dot_general | solution.py:119
  205.3 2.6 %copy.36 = bf16[4,1,256,768]{2,3,0,1:T(8,128)(2,1)} copy(bf16[4,1,256,768]{3,2,1,0:T(8,128)(2,1)} %get-tuple-element.19) | data formatting | bytes 3145728
  207.9 3.9 %convert_add_fusion = (f32[4,256,768]{1,2,0:T(8,128)}, bf16[4,256,768]{1,2,0:T(8,128)(2,1)S(1)}) fusion(bf16[4,256,768]{1,2,0:T(8,128)(2,1)} %collective-permute-done.4, bf16[4,1,256,768]{2,3,0,1:T(8,128)(2,1)} %copy.36), kind=kLoop, calls=%fused_computation.8 | loop fusion | flops 3145728 | bytes 7864320 | tf_op jit(solution)/shard_map/add | solution.py:44
  215.0 3.1 %collective-permute-start.6 = (bf16[256,768]{0,1:T(8,128)(2,1)}, bf16[256,768]{0,1:T(8,128)(2,1)}, u32[]{:S(2)}, u32[]{:S(2)}) collective-permute-start(bf16[256,768]{0,1:T(8,128)(2,1)} %get-tuple-element.25), channel_id=1, source_target_pairs={{0,128},{32,160},{64,192},{96,224},{128,0},{160,32},{192,64},{224,... | collective-permute-start | bytes 1179656 | tf_op jit(solution)/shard_map/ppermute | solution.py:50
  219.5 3.5 %fusion.47 = (bf16[4,256,768]{2,1,0:T(8,128)(2,1)S(1)}, f32[4,256,768]{2,1,0:T(8,128)}) fusion(bf16[4,256,768]{2,1,0:T(8,128)(2,1)} %collective-permute-done, bf16[4,2,256,768]{3,2,1,0:T(8,128)(2,1)S(1)} %bitcast.94, s32[]{:T(128)S(6)} %select_n.43), kind=kLoop, calls=%fused_computation.78 | loop fusion | flops 3145728 | bytes 7864324 | tf_op jit(solution)/shard_map/convert_element_type | solution.py:45
  226.1 2.6 %collective-permute-start.3 = (bf16[256,768]{1,0:T(8,128)(2,1)S(1)}, bf16[256,768]{1,0:T(8,128)(2,1)}, u32[]{:S(2)}, u32[]{:S(2)}) collective-permute-start(bf16[256,768]{1,0:T(8,128)(2,1)S(1)} %get-tuple-element.29), channel_id=1, source_target_pairs={{0,192},{32,224},{64,0},{96,32},{128,64},{160,96},{192,128},{224,1... | collective-permute-start | bytes 1179656 | tf_op jit(solution)/shard_map/ppermute | solution.py:50
  228.7 7.9 %collective-permute-done.6 = bf16[256,768]{0,1:T(8,128)(2,1)} collective-permute-done((bf16[256,768]{0,1:T(8,128)(2,1)}, bf16[256,768]{0,1:T(8,128)(2,1)}, u32[]{:S(2)}, u32[]{:S(2)}) %collective-permute-start.6) | collective-permute-done | bytes 393248 | tf_op jit(solution)/shard_map/ppermute | solution.py:50
  239.1 4.6 %collective-permute-done.1 = bf16[256,768]{1,0:T(8,128)(2,1)} collective-permute-done((bf16[256,768]{1,0:T(8,128)(2,1)S(1)}, bf16[256,768]{1,0:T(8,128)(2,1)}, u32[]{:S(2)}, u32[]{:S(2)}) %collective-permute-start.1) | collective-permute-done | bytes 393248 | tf_op jit(solution)/shard_map/ppermute | solution.py:50
  243.7 9.0 %collective-permute-done.2 = bf16[256,768]{1,0:T(8,128)(2,1)} collective-permute-done((bf16[256,768]{1,0:T(8,128)(2,1)S(1)}, bf16[256,768]{1,0:T(8,128)(2,1)}, u32[]{:S(2)}, u32[]{:S(2)}) %collective-permute-start.2) | collective-permute-done | bytes 393248 | tf_op jit(solution)/shard_map/ppermute | solution.py:50
  255.2 2.8 %convolution_convert_fusion.1 = bf16[128,2048]{1,0:T(8,128)(2,1)} fusion(pred[128,512]{1,0:T(8,128)(4,1)S(1)} %fusion.40, bf16[512,2048]{1,0:T(8,128)(2,1)} %bitcast.8), kind=kOutput, calls=%fused_computation.23 | convolution fusion | flops 268697600 | bytes 2686976 | tf_op jit(solution)/shard_map/dot_general | solution.py:118
  (51 shorter events, 22.3 us)
Async XLA Ops:
  0.6 127.1 %copy-start = (bf16[1,2048,768]{2,1,0:T(8,128)(2,1)S(1)}, bf16[1,2048,768]{2,1,0:T(8,128)(2,1)}, u32[]{:S(2)}) copy-start(bf16[1,2048,768]{2,1,0:T(8,128)(2,1)} %param.13) | copy-start | bytes 9437188
  8.4 106.2 %all-to-all-start = ((bf16[32,16,4096]{2,1,0:T(8,128)(2,1)}), bf16[32,16,4096]{2,1,0:T(8,128)(2,1)}, u32[]{:S(2)}, u32[]{:S(2)}) async-start(bf16[32,16,4096]{2,1,0:T(8,128)(2,1)} %bitcast.96), calls=%async_computation | async-start | bytes 8388608 | tf_op jit(solution)/shard_map/all_to_all | solution.py:72
  114.6 55.1 %all-to-all-start.1 = ((bf16[32,16,2048]{2,1,0:T(8,128)(2,1)}), bf16[32,16,2048]{2,1,0:T(8,128)(2,1)}, u32[]{:S(2)}, u32[]{:S(2)}) async-start(bf16[32,16,2048]{2,1,0:T(8,128)(2,1)} %bitcast.95), calls=%async_computation.1 | async-start | bytes 4194304 | tf_op jit(solution)/shard_map/all_to_all | solution.py:80
  127.8 4.7 %copy-start.6 = (bf16[1,768,2048]{2,1,0:T(8,128)(2,1)S(1)}, bf16[1,768,2048]{2,1,0:T(8,128)(2,1)}, u32[]{:S(2)}) copy-start(bf16[1,768,2048]{2,1,0:T(8,128)(2,1)} %param.14) | copy-start | bytes 9437188
  169.7 6.5 %copy-start.7 = (bf16[1,2048,768]{2,1,0:T(8,128)(2,1)S(1)}, bf16[1,2048,768]{2,1,0:T(8,128)(2,1)}, u32[]{:S(2)}) copy-start(bf16[1,2048,768]{2,1,0:T(8,128)(2,1)} %param.15) | copy-start | bytes 9437188
  176.2 1.8 copy-start.4
  176.2 1.9 copy-start.2
  181.3 8.8 %copy-start.8 = (bf16[512,768]{1,0:T(8,128)(2,1)S(1)}, bf16[512,768]{1,0:T(8,128)(2,1)}, u32[]{:S(2)}) copy-start(bf16[512,768]{1,0:T(8,128)(2,1)} %get-tuple-element.14) | copy-start | bytes 2359300
  181.3 73.9 %all-to-all-start.2 = ((bf16[32,16,2048]{2,1,0:T(8,128)(2,1)}), bf16[32,16,2048]{2,1,0:T(8,128)(2,1)}, u32[]{:S(2)}, u32[]{:S(2)}) async-start(bf16[32,16,2048]{2,1,0:T(8,128)(2,1)} %bitcast.98), calls=%async_computation.2 | async-start | bytes 4194304 | tf_op jit(solution)/shard_map/all_to_all | solution.py:109
  194.9 1.6 copy-start.5
  196.4 3.6 %copy-start.3 = (bf16[512,768]{1,0:T(8,128)(2,1)S(1)}, bf16[512,768]{1,0:T(8,128)(2,1)}, u32[]{:S(2)}) copy-start(bf16[512,768]{1,0:T(8,128)(2,1)} %copy-done.2) | copy-start | bytes 2359300
  196.4 11.5 %collective-permute-start.4 = (bf16[4,256,768]{1,2,0:T(8,128)(2,1)}, bf16[4,256,768]{1,2,0:T(8,128)(2,1)}, u32[]{:S(2)}, u32[]{:S(2)}) collective-permute-start(bf16[4,256,768]{1,2,0:T(8,128)(2,1)} %bitcast.19), channel_id=1, source_target_pairs={{0,32},{32,0},{64,96},{96,64},{128,160},{160,128},{192,224},{224,1... | collective-permute-start | bytes 4718600 | tf_op jit(solution)/shard_map/ppermute | solution.py:43
  204.9 14.6 %collective-permute-start = (bf16[4,256,768]{2,1,0:T(8,128)(2,1)}, bf16[4,256,768]{2,1,0:T(8,128)(2,1)}, u32[]{:S(2)}, u32[]{:S(2)}) collective-permute-start(bf16[4,256,768]{2,1,0:T(8,128)(2,1)} %dynamic-slice_bitcast_fusion), channel_id=1, source_target_pairs={{0,32},{32,0},{64,96},{96,64},{128,160},{160,128},{192,224},{224,1... | collective-permute-start | bytes 4718600 | tf_op jit(solution)/shard_map/ppermute | solution.py:43
  213.4 12.7 %collective-permute-start.5 = (bf16[256,768]{0,1:T(8,128)(2,1)S(1)}, bf16[256,768]{0,1:T(8,128)(2,1)}, u32[]{:S(2)}, u32[]{:S(2)}) collective-permute-start(bf16[256,768]{0,1:T(8,128)(2,1)S(1)} %get-tuple-element.24), channel_id=1, source_target_pairs={{0,64},{32,96},{64,128},{96,160},{128,192},{160,224},{192,0},{224,... | collective-permute-start | bytes 1179656 | tf_op jit(solution)/shard_map/ppermute | solution.py:50
  215.0 21.7 %collective-permute-start.6 = (bf16[256,768]{0,1:T(8,128)(2,1)}, bf16[256,768]{0,1:T(8,128)(2,1)}, u32[]{:S(2)}, u32[]{:S(2)}) collective-permute-start(bf16[256,768]{0,1:T(8,128)(2,1)} %get-tuple-element.25), channel_id=1, source_target_pairs={{0,128},{32,160},{64,192},{96,224},{128,0},{160,32},{192,64},{224,... | collective-permute-start | bytes 1179656 | tf_op jit(solution)/shard_map/ppermute | solution.py:50
  218.1 18.5 %collective-permute-start.7 = (bf16[256,768]{0,1:T(8,128)(2,1)}, bf16[256,768]{0,1:T(8,128)(2,1)}, u32[]{:S(2)}, u32[]{:S(2)}) collective-permute-start(bf16[256,768]{0,1:T(8,128)(2,1)} %get-tuple-element.26), channel_id=1, source_target_pairs={{0,192},{32,224},{64,0},{96,32},{128,64},{160,96},{192,128},{224,1... | collective-permute-start | bytes 1179656 | tf_op jit(solution)/shard_map/ppermute | solution.py:50
  223.6 20.0 %collective-permute-start.1 = (bf16[256,768]{1,0:T(8,128)(2,1)S(1)}, bf16[256,768]{1,0:T(8,128)(2,1)}, u32[]{:S(2)}, u32[]{:S(2)}) collective-permute-start(bf16[256,768]{1,0:T(8,128)(2,1)S(1)} %get-tuple-element.27), channel_id=1, source_target_pairs={{0,64},{32,96},{64,128},{96,160},{128,192},{160,224},{192,0},{224,... | collective-permute-start | bytes 1179656 | tf_op jit(solution)/shard_map/ppermute | solution.py:50
  224.4 28.2 %collective-permute-start.2 = (bf16[256,768]{1,0:T(8,128)(2,1)S(1)}, bf16[256,768]{1,0:T(8,128)(2,1)}, u32[]{:S(2)}, u32[]{:S(2)}) collective-permute-start(bf16[256,768]{1,0:T(8,128)(2,1)S(1)} %get-tuple-element.28), channel_id=1, source_target_pairs={{0,128},{32,160},{64,192},{96,224},{128,0},{160,32},{192,64},{224,... | collective-permute-start | bytes 1179656 | tf_op jit(solution)/shard_map/ppermute | solution.py:50
  226.1 26.5 %collective-permute-start.3 = (bf16[256,768]{1,0:T(8,128)(2,1)S(1)}, bf16[256,768]{1,0:T(8,128)(2,1)}, u32[]{:S(2)}, u32[]{:S(2)}) collective-permute-start(bf16[256,768]{1,0:T(8,128)(2,1)S(1)} %get-tuple-element.29), channel_id=1, source_target_pairs={{0,192},{32,224},{64,0},{96,32},{128,64},{160,96},{192,128},{224,1... | collective-permute-start | bytes 1179656 | tf_op jit(solution)/shard_map/ppermute | solution.py:50
  252.6 5.4 %copy-start.1 = (bf16[1,2048,768]{2,1,0:T(8,128)(2,1)S(1)}, bf16[1,2048,768]{2,1,0:T(8,128)(2,1)}, u32[]{:S(2)}) copy-start(bf16[1,2048,768]{2,1,0:T(8,128)(2,1)} %param.13) | copy-start | bytes 9437188

commit v10 on v9

--- a/solution.py
+++ b/solution.py
@@ -103,8 +103,10 @@
     input_hvp = (jnp.dot(back_tan, up_proj.T, preferred_element_type=jnp.float32) + hvp_mix).astype(
         jnp.bfloat16
     )
-    input_hvp, back_pre, back_tan, hidden_tan = lax.optimization_barrier(
-        (input_hvp, back_pre, back_tan, hidden_tan)
+    second = jnp.dot(scaled_cot.T, hidden_tan, preferred_element_type=jnp.float32)
+    down_part = (second * scale).astype(jnp.bfloat16)
+    input_hvp, back_pre, back_tan, down_part = lax.optimization_barrier(
+        (input_hvp, back_pre, back_tan, down_part)
     )
     returned = lax.all_to_all(
         input_hvp.reshape(expert_count, capacity, width),
@@ -113,8 +115,7 @@
         concat_axis=0,
         tiled=True,
     ).reshape(slots, width)
-    second = jnp.dot(scaled_cot.T, hidden_tan, preferred_element_type=jnp.float32)
-    down_sum = reduce_over_dp((second * scale).astype(jnp.bfloat16), replicas)
+    down_sum = reduce_over_dp(down_part, replicas)
     hvp_tokens = jnp.dot(pick, returned, preferred_element_type=jnp.float32).astype(jnp.bfloat16)
     first = jnp.dot(tangent.T, back_pre, preferred_element_type=jnp.float32) + jnp.dot(
         primal.T, back_tan, preferred_element_type=jnp.float32

time: 259 us -> 258 us (level)
  transfers between devices with their start and end apart: 11 -> 11, of which waited for: 6 -> 6; matrix products, arithmetic and copies ran while one was open for 19% -> 17% of each run, Pallas kernels for 0% -> 0%
where the time goes in v10:
time: 258 us; the launch traced here: 257 us
  waiting for transfers between devices  148 us (57%)
  matrix products  46.1 us (18%)
  starting transfers between devices  38.1 us (15%)
  other arithmetic  15.2 us (6%)
  local copies, waits for them, and re-layouts  9.26 us (4%)
    all_to_all x1, waiting for transfers between devices, per_device(): lax.all_to_all(send_xg.reshape(expert_count, capacity, 2 * width), 'exper...  91.3 us
    all_to_all x1, waiting for transfers between devices, per_device(): lax.all_to_all(send_tan.reshape(expert_count, capacity, width), 'expert',...  33.5 us
    ppermute x6, waiting for transfers between devices, reduce_over_dp(): total = total + lax.ppermute(wire[step], 'dp', pairs).astype(jnp.float32)  23.3 us
    all_to_all x1, starting transfers between devices, per_device(): lax.all_to_all(send_xg.reshape(expert_count, capacity, 2 * width), 'exper...  11.7 us
    ppermute x6, starting transfers between devices, reduce_over_dp(): total = total + lax.ppermute(wire[step], 'dp', pairs).astype(jnp.float32)  9.81 us
    all_to_all x1, starting transfers between devices, per_device(): lax.all_to_all(input_hvp.reshape(expert_count, capacity, width), 'expert'...  8.98 us
    all_to_all x1, starting transfers between devices, per_device(): lax.all_to_all(send_tan.reshape(expert_count, capacity, width), 'expert',...  7.6 us
    dot_general x1, matrix products, per_device(): jnp.dot(tangent, up_proj, preferred_element_type=jnp.float32) + pre_mix  5.5 us
  transfers between devices with their start and end apart: 11, of which 6 were waited for; matrix products, arithmetic and copies ran while one was open for 17% of the time, Pallas kernels for 0%

profile of v10, /device:TPU:2, one launch (start us, length us, event | category | flops | bytes accessed | tf_op | source)
XLA Modules:
  0.0 257.5 jit_solution(374363266443830151)
XLA Ops:
  3.8 4.5 %multiply_convert_fusion = bf16[512,4096]{1,0:T(8,128)(2,1)} fusion(pred[128,512]{1,0:T(8,128)(4,1)S(1)} %fusion.40, f32[512]{0:T(512)S(1)} %select_reduce_fusion, pred[4096]{0:T(1024)(128)(4,1)S(1)} %iota_compare_fusion.5, bf16[128,2048]{1,0:T(8,128)(2,1)} %param.10, bf16[128,2048]{1,0:T(8,128)(2,1)} %param.8), kind=kOutput, calls=%fused_computation | convolution fusion | flops 545259520 | bytes 5314560 | tf_op jit(solution)/shard_map/dot_general | solution.py:63
  8.3 11.7 %all-to-all-start = ((bf16[32,16,4096]{2,1,0:T(8,128)(2,1)}), bf16[32,16,4096]{2,1,0:T(8,128)(2,1)}, u32[]{:S(2)}, u32[]{:S(2)}) async-start(bf16[32,16,4096]{2,1,0:T(8,128)(2,1)} %bitcast.95), calls=%async_computation | async-start | bytes 8388608 | tf_op jit(solution)/shard_map/all_to_all | solution.py:72
  20.0 3.2 %convolution_convert_fusion = bf16[512,2048]{1,0:T(8,128)(2,1)} fusion(pred[128,512]{1,0:T(8,128)(4,1)S(1)} %fusion.40, bf16[128,2048]{1,0:T(8,128)(2,1)} %param.9), kind=kOutput, calls=%fused_computation.22 | convolution fusion | flops 269484032 | bytes 2686976 | tf_op jit(solution)/shard_map/dot_general | solution.py:30
  23.2 91.3 %all-to-all-done = bf16[32,16,4096]{2,1,0:T(8,128)(2,1)} async-done(((bf16[32,16,4096]{2,1,0:T(8,128)(2,1)}), bf16[32,16,4096]{2,1,0:T(8,128)(2,1)}, u32[]{:S(2)}, u32[]{:S(2)}) %all-to-all-start) | async-done | bytes 4194336 | tf_op jit(solution)/shard_map/all_to_all | solution.py:72
  114.5 7.6 %all-to-all-start.1 = ((bf16[32,16,2048]{2,1,0:T(8,128)(2,1)}), bf16[32,16,2048]{2,1,0:T(8,128)(2,1)}, u32[]{:S(2)}, u32[]{:S(2)}) async-start(bf16[32,16,2048]{2,1,0:T(8,128)(2,1)} %bitcast.94), calls=%async_computation.1 | async-start | bytes 4194304 | tf_op jit(solution)/shard_map/all_to_all | solution.py:80
  122.1 4.7 %fusion.8 = f32[512,768]{1,0:T(8,128)} fusion(bf16[1,2048,768]{2,1,0:T(8,128)(2,1)S(1)} %copy-done, bf16[512,4096]{1,0:T(8,128)(2,1)} %bitcast.1), kind=kOutput, calls=%fused_computation.18 | convolution fusion | flops 1610612736 | bytes 6815744 | tf_op jit(solution)/shard_map/dot_general | solution.py:92
  126.8 4.7 %fusion.10 = f32[512,768]{1,0:T(8,128)} fusion(bf16[1,768,2048]{2,1,0:T(8,128)(2,1)S(1)} %copy-done.6, bf16[512,4096]{1,0:T(8,128)(2,1)} %bitcast.1), kind=kOutput, calls=%fused_computation.20 | convolution fusion | flops 1610612736 | bytes 6815744 | tf_op jit(solution)/shard_map/dot_general | solution.py:96
  131.5 4.6 %fusion.2 = f32[512,768]{1,0:T(8,128)} fusion(bf16[1,2048,768]{2,1,0:T(8,128)(2,1)S(1)} %copy-done.7, bf16[512,4096]{1,0:T(8,128)(2,1)} %bitcast.1), kind=kOutput, calls=%fused_computation.12 | convolution fusion | flops 1610612736 | bytes 6815744 | tf_op jit(solution)/shard_map/dot_general | solution.py:98
  136.2 33.5 %all-to-all-done.1 = bf16[32,16,2048]{2,1,0:T(8,128)(2,1)} async-done(((bf16[32,16,2048]{2,1,0:T(8,128)(2,1)}), bf16[32,16,2048]{2,1,0:T(8,128)(2,1)}, u32[]{:S(2)}, u32[]{:S(2)}) %all-to-all-start.1) | async-done | bytes 2097184 | tf_op jit(solution)/shard_map/all_to_all | solution.py:80
  169.6 5.5 %fusion.22 = (bf16[512,768]{1,0:T(8,128)(2,1)S(1)}, bf16[512,768]{1,0:T(8,128)(2,1)S(1)}, f32[512,768]{1,0:T(8,128)S(1)}) fusion(f32[512,768]{1,0:T(8,128)} %fusion.10, f32[512,768]{1,0:T(8,128)} %fusion.8, f32[512,768]{1,0:T(8,128)} %fusion.2, bf16[512,2048]{1,0:T(8,128)(2,1)} %bitcast.5, bf16[1,2048,768]{2,1,0:T(8,128)(2,1)S(1)} %copy-done), kind=kOutput, calls=%fused_computation.34 | convolution fusion | flops 1618083840 | bytes 13107200 | tf_op jit(solution)/shard_map/dot_general | solution.py:100
  177.1 3.6 %multiply_convert_fusion.2 = bf16[2048,768]{1,0:T(8,128)(2,1)S(1)} fusion(bf16[512,4096]{1,0:T(8,128)(2,1)} %bitcast.1, f32[512,768]{1,0:T(8,128)S(1)} %get-tuple-element.29, f32[512,768]{1,0:T(8,128)S(1)} %copy-done.9), kind=kOutput, calls=%fused_computation.2 | convolution fusion | flops 1617297408 | bytes 8388608 | tf_op jit(solution)/shard_map/dot_general | solution.py:106
  180.8 3.2 %add_convert_fusion = bf16[512,2048]{1,0:T(8,128)(2,1)} fusion(f32[512,2048]{1,0:T(8,128)S(1)} %fusion, bf16[512,768]{1,0:T(8,128)(2,1)S(1)} %get-tuple-element.13, bf16[1,2048,768]{2,1,0:T(8,128)(2,1)S(1)} %copy-done), kind=kOutput, calls=%fused_computation.3 | convolution fusion | flops 1612709888 | bytes 10223616 | tf_op jit(solution)/shard_map/dot_general | solution.py:103
  186.9 9.0 %all-to-all-start.2 = ((bf16[32,16,2048]{2,1,0:T(8,128)(2,1)}), bf16[32,16,2048]{2,1,0:T(8,128)(2,1)}, u32[]{:S(2)}, u32[]{:S(2)}) async-start(bf16[32,16,2048]{2,1,0:T(8,128)(2,1)} %bitcast.97), calls=%async_computation.2 | async-start | bytes 4194304 | tf_op jit(solution)/shard_map/all_to_all | solution.py:111
  195.9 3.5 %fusion.49 = f32[2048,768]{1,0:T(8,128)S(1)} fusion(bf16[512,2048]{1,0:T(8,128)(2,1)} %bitcast.5, bf16[512,768]{1,0:T(8,128)(2,1)S(1)} %copy-done.5), kind=kOutput, calls=%fused_computation.79 | convolution fusion | flops 1610612736 | bytes 9175040 | tf_op jit(solution)/shard_map/dot_general | solution.py:120
  199.5 3.6 %multiply_convert_fusion.1 = bf16[2048,768]{1,0:T(8,128)(2,1)S(1)} fusion(f32[2048,768]{1,0:T(8,128)S(1)} %fusion.49, bf16[512,768]{1,0:T(8,128)(2,1)S(1)} %copy-done.3, bf16[512,4096]{1,0:T(8,128)(2,1)} %bitcast.1), kind=kOutput, calls=%fused_computation.1 | convolution fusion | flops 1615331328 | bytes 12320768 | tf_op jit(solution)/shard_map/dot_general | solution.py:120
  204.4 2.6 %copy.36 = bf16[4,1,256,768]{2,3,0,1:T(8,128)(2,1)} copy(bf16[4,1,256,768]{3,2,1,0:T(8,128)(2,1)} %get-tuple-element.19) | data formatting | bytes 3145728
  207.0 3.9 %convert_add_fusion = (f32[4,256,768]{1,2,0:T(8,128)}, bf16[4,256,768]{1,2,0:T(8,128)(2,1)S(1)}) fusion(bf16[4,256,768]{1,2,0:T(8,128)(2,1)} %collective-permute-done.4, bf16[4,1,256,768]{2,3,0,1:T(8,128)(2,1)} %copy.36), kind=kLoop, calls=%fused_computation.8 | loop fusion | flops 3145728 | bytes 7864320 | tf_op jit(solution)/shard_map/add | solution.py:44
  214.3 2.9 %collective-permute-start.6 = (bf16[256,768]{0,1:T(8,128)(2,1)}, bf16[256,768]{0,1:T(8,128)(2,1)}, u32[]{:S(2)}, u32[]{:S(2)}) collective-permute-start(bf16[256,768]{0,1:T(8,128)(2,1)} %get-tuple-element.24), channel_id=1, source_target_pairs={{0,128},{32,160},{64,192},{96,224},{128,0},{160,32},{192,64},{224,... | collective-permute-start | bytes 1179656 | tf_op jit(solution)/shard_map/ppermute | solution.py:50
  218.5 3.5 %fusion.48 = (bf16[4,256,768]{2,1,0:T(8,128)(2,1)S(1)}, f32[4,256,768]{2,1,0:T(8,128)}) fusion(bf16[4,256,768]{2,1,0:T(8,128)(2,1)} %collective-permute-done, bf16[4,2,256,768]{3,2,1,0:T(8,128)(2,1)S(1)} %bitcast.93, s32[]{:T(128)S(6)} %select_n.43), kind=kLoop, calls=%fused_computation.78 | loop fusion | flops 3145728 | bytes 7864324 | tf_op jit(solution)/shard_map/convert_element_type | solution.py:45
  227.8 7.9 %collective-permute-done.6 = bf16[256,768]{0,1:T(8,128)(2,1)} collective-permute-done((bf16[256,768]{0,1:T(8,128)(2,1)}, bf16[256,768]{0,1:T(8,128)(2,1)}, u32[]{:S(2)}, u32[]{:S(2)}) %collective-permute-start.6) | collective-permute-done | bytes 393248 | tf_op jit(solution)/shard_map/ppermute | solution.py:50
  238.1 5.1 %collective-permute-done.1 = bf16[256,768]{1,0:T(8,128)(2,1)} collective-permute-done((bf16[256,768]{1,0:T(8,128)(2,1)S(1)}, bf16[256,768]{1,0:T(8,128)(2,1)}, u32[]{:S(2)}, u32[]{:S(2)}) %collective-permute-start.1) | collective-permute-done | bytes 393248 | tf_op jit(solution)/shard_map/ppermute | solution.py:50
  243.2 8.9 %collective-permute-done.2 = bf16[256,768]{1,0:T(8,128)(2,1)} collective-permute-done((bf16[256,768]{1,0:T(8,128)(2,1)S(1)}, bf16[256,768]{1,0:T(8,128)(2,1)}, u32[]{:S(2)}, u32[]{:S(2)}) %collective-permute-start.2) | collective-permute-done | bytes 393248 | tf_op jit(solution)/shard_map/ppermute | solution.py:50
  252.1 2.6 fusion.41
  254.6 2.8 %convolution_convert_fusion.1 = bf16[128,2048]{1,0:T(8,128)(2,1)} fusion(pred[128,512]{1,0:T(8,128)(4,1)S(1)} %fusion.40, bf16[512,2048]{1,0:T(8,128)(2,1)} %bitcast.8), kind=kOutput, calls=%fused_computation.23 | convolution fusion | flops 268697600 | bytes 2686976 | tf_op jit(solution)/shard_map/dot_general | solution.py:119
  (53 shorter events, 22.2 us)
Async XLA Ops:
  0.6 121.5 %copy-start = (bf16[1,2048,768]{2,1,0:T(8,128)(2,1)S(1)}, bf16[1,2048,768]{2,1,0:T(8,128)(2,1)}, u32[]{:S(2)}) copy-start(bf16[1,2048,768]{2,1,0:T(8,128)(2,1)} %param.13) | copy-start | bytes 9437188
  8.3 106.2 %all-to-all-start = ((bf16[32,16,4096]{2,1,0:T(8,128)(2,1)}), bf16[32,16,4096]{2,1,0:T(8,128)(2,1)}, u32[]{:S(2)}, u32[]{:S(2)}) async-start(bf16[32,16,4096]{2,1,0:T(8,128)(2,1)} %bitcast.95), calls=%async_computation | async-start | bytes 8388608 | tf_op jit(solution)/shard_map/all_to_all | solution.py:72
  114.5 55.1 %all-to-all-start.1 = ((bf16[32,16,2048]{2,1,0:T(8,128)(2,1)}), bf16[32,16,2048]{2,1,0:T(8,128)(2,1)}, u32[]{:S(2)}, u32[]{:S(2)}) async-start(bf16[32,16,2048]{2,1,0:T(8,128)(2,1)} %bitcast.94), calls=%async_computation.1 | async-start | bytes 4194304 | tf_op jit(solution)/shard_map/all_to_all | solution.py:80
  122.1 4.7 %copy-start.6 = (bf16[1,768,2048]{2,1,0:T(8,128)(2,1)S(1)}, bf16[1,768,2048]{2,1,0:T(8,128)(2,1)}, u32[]{:S(2)}) copy-start(bf16[1,768,2048]{2,1,0:T(8,128)(2,1)} %param.14) | copy-start | bytes 9437188
  126.8 4.7 %copy-start.7 = (bf16[1,2048,768]{2,1,0:T(8,128)(2,1)S(1)}, bf16[1,2048,768]{2,1,0:T(8,128)(2,1)}, u32[]{:S(2)}) copy-start(bf16[1,2048,768]{2,1,0:T(8,128)(2,1)} %param.15) | copy-start | bytes 9437188
  169.6 5.5 %copy-start.8 = (bf16[1,2048,768]{2,1,0:T(8,128)(2,1)S(1)}, bf16[1,2048,768]{2,1,0:T(8,128)(2,1)}, u32[]{:S(2)}) copy-start(bf16[1,2048,768]{2,1,0:T(8,128)(2,1)} %param.15) | copy-start | bytes 9437188
  175.1 1.9 copy-start.4
  175.1 5.6 %copy-start.2 = (bf16[512,768]{1,0:T(8,128)(2,1)}, bf16[512,768]{1,0:T(8,128)(2,1)S(1)}, u32[]{:S(2)}) copy-start(bf16[512,768]{1,0:T(8,128)(2,1)S(1)} %get-tuple-element.13) | copy-start | bytes 2359300
  175.2 2.0 copy-start.9
  186.9 20.1 %collective-permute-start.4 = (bf16[4,256,768]{1,2,0:T(8,128)(2,1)}, bf16[4,256,768]{1,2,0:T(8,128)(2,1)}, u32[]{:S(2)}, u32[]{:S(2)}) collective-permute-start(bf16[4,256,768]{1,2,0:T(8,128)(2,1)} %bitcast.19), channel_id=1, source_target_pairs={{0,32},{32,0},{64,96},{96,64},{128,160},{160,128},{192,224},{224,1... | collective-permute-start | bytes 4718600 | tf_op jit(solution)/shard_map/ppermute | solution.py:43
  186.9 9.0 %copy-start.5 = (bf16[512,768]{1,0:T(8,128)(2,1)S(1)}, bf16[512,768]{1,0:T(8,128)(2,1)}, u32[]{:S(2)}) copy-start(bf16[512,768]{1,0:T(8,128)(2,1)} %copy-done.4) | copy-start | bytes 2359300
  186.9 67.7 %all-to-all-start.2 = ((bf16[32,16,2048]{2,1,0:T(8,128)(2,1)}), bf16[32,16,2048]{2,1,0:T(8,128)(2,1)}, u32[]{:S(2)}, u32[]{:S(2)}) async-start(bf16[32,16,2048]{2,1,0:T(8,128)(2,1)} %bitcast.97), calls=%async_computation.2 | async-start | bytes 4194304 | tf_op jit(solution)/shard_map/all_to_all | solution.py:111
  195.9 3.6 %copy-start.3 = (bf16[512,768]{1,0:T(8,128)(2,1)S(1)}, bf16[512,768]{1,0:T(8,128)(2,1)}, u32[]{:S(2)}) copy-start(bf16[512,768]{1,0:T(8,128)(2,1)} %copy-done.2) | copy-start | bytes 2359300
  204.4 14.1 %collective-permute-start = (bf16[4,256,768]{2,1,0:T(8,128)(2,1)}, bf16[4,256,768]{2,1,0:T(8,128)(2,1)}, u32[]{:S(2)}, u32[]{:S(2)}) collective-permute-start(bf16[4,256,768]{2,1,0:T(8,128)(2,1)} %dynamic-slice_bitcast_fusion), channel_id=1, source_target_pairs={{0,32},{32,0},{64,96},{96,64},{128,160},{160,128},{192,224},{224,1... | collective-permute-start | bytes 4718600 | tf_op jit(solution)/shard_map/ppermute | solution.py:43
  212.4 13.1 %collective-permute-start.5 = (bf16[256,768]{0,1:T(8,128)(2,1)S(1)}, bf16[256,768]{0,1:T(8,128)(2,1)}, u32[]{:S(2)}, u32[]{:S(2)}) collective-permute-start(bf16[256,768]{0,1:T(8,128)(2,1)S(1)} %get-tuple-element.23), channel_id=1, source_target_pairs={{0,64},{32,96},{64,128},{96,160},{128,192},{160,224},{192,0},{224,... | collective-permute-start | bytes 1179656 | tf_op jit(solution)/shard_map/ppermute | solution.py:50
  214.3 21.4 %collective-permute-start.6 = (bf16[256,768]{0,1:T(8,128)(2,1)}, bf16[256,768]{0,1:T(8,128)(2,1)}, u32[]{:S(2)}, u32[]{:S(2)}) collective-permute-start(bf16[256,768]{0,1:T(8,128)(2,1)} %get-tuple-element.24), channel_id=1, source_target_pairs={{0,128},{32,160},{64,192},{96,224},{128,0},{160,32},{192,64},{224,... | collective-permute-start | bytes 1179656 | tf_op jit(solution)/shard_map/ppermute | solution.py:50
  217.2 18.5 %collective-permute-start.7 = (bf16[256,768]{0,1:T(8,128)(2,1)}, bf16[256,768]{0,1:T(8,128)(2,1)}, u32[]{:S(2)}, u32[]{:S(2)}) collective-permute-start(bf16[256,768]{0,1:T(8,128)(2,1)} %get-tuple-element.25), channel_id=1, source_target_pairs={{0,192},{32,224},{64,0},{96,32},{128,64},{160,96},{192,128},{224,1... | collective-permute-start | bytes 1179656 | tf_op jit(solution)/shard_map/ppermute | solution.py:50
  222.7 20.5 %collective-permute-start.1 = (bf16[256,768]{1,0:T(8,128)(2,1)S(1)}, bf16[256,768]{1,0:T(8,128)(2,1)}, u32[]{:S(2)}, u32[]{:S(2)}) collective-permute-start(bf16[256,768]{1,0:T(8,128)(2,1)S(1)} %get-tuple-element.26), channel_id=1, source_target_pairs={{0,64},{32,96},{64,128},{96,160},{128,192},{160,224},{192,0},{224,... | collective-permute-start | bytes 1179656 | tf_op jit(solution)/shard_map/ppermute | solution.py:50
  223.4 28.7 %collective-permute-start.2 = (bf16[256,768]{1,0:T(8,128)(2,1)S(1)}, bf16[256,768]{1,0:T(8,128)(2,1)}, u32[]{:S(2)}, u32[]{:S(2)}) collective-permute-start(bf16[256,768]{1,0:T(8,128)(2,1)S(1)} %get-tuple-element.27), channel_id=1, source_target_pairs={{0,128},{32,160},{64,192},{96,224},{128,0},{160,32},{192,64},{224,... | collective-permute-start | bytes 1179656 | tf_op jit(solution)/shard_map/ppermute | solution.py:50
  225.6 26.5 %collective-permute-start.3 = (bf16[256,768]{1,0:T(8,128)(2,1)S(1)}, bf16[256,768]{1,0:T(8,128)(2,1)}, u32[]{:S(2)}, u32[]{:S(2)}) collective-permute-start(bf16[256,768]{1,0:T(8,128)(2,1)S(1)} %get-tuple-element.28), channel_id=1, source_target_pairs={{0,192},{32,224},{64,0},{96,32},{128,64},{160,96},{192,128},{224,1... | collective-permute-start | bytes 1179656 | tf_op jit(solution)/shard_map/ppermute | solution.py:50
  252.1 5.4 %copy-start.1 = (bf16[1,2048,768]{2,1,0:T(8,128)(2,1)S(1)}, bf16[1,2048,768]{2,1,0:T(8,128)(2,1)}, u32[]{:S(2)}) copy-start(bf16[1,2048,768]{2,1,0:T(8,128)(2,1)} %param.13) | copy-start | bytes 9437188

commit v11 on v9

--- a/solution.py
+++ b/solution.py
@@ -32,7 +32,7 @@
     ).astype(jnp.bfloat16)
 
 
-def reduce_over_dp(part, replicas):
+def reduce_over_dp(part, replicas, anchor=None):
     half = replicas // 2
     me = lax.axis_index("dp")
     core = me % 2
@@ -44,11 +44,16 @@
     partial = keep.astype(jnp.float32) + got.astype(jnp.float32)
     wire = partial.astype(jnp.bfloat16)
     wire = lax.dynamic_slice_in_dim(jnp.concatenate([wire, wire], 0), row, half, 0)
-    total = lax.dynamic_index_in_dim(partial, row, axis=0, keepdims=False)
+    received = []
     for step in range(1, half):
         pairs = [(i, (i + 2 * step) % replicas) for i in range(replicas)]
-        total = total + lax.ppermute(wire[step], "dp", pairs).astype(jnp.float32)
-    return total.astype(jnp.bfloat16)
+        received.append(lax.ppermute(wire[step], "dp", pairs))
+    if anchor is not None:
+        anchor, received = lax.optimization_barrier((anchor, received))
+    total = lax.dynamic_index_in_dim(partial, row, axis=0, keepdims=False)
+    for piece in received:
+        total = total + piece.astype(jnp.float32)
+    return total.astype(jnp.bfloat16), anchor
 
 
 def per_device(tokens, tangents, cotangents, routes, gates, w_up, w_down, v_up):
@@ -114,12 +119,14 @@
         tiled=True,
     ).reshape(slots, width)
     second = jnp.dot(scaled_cot.T, hidden_tan, preferred_element_type=jnp.float32)
-    down_sum = reduce_over_dp((second * scale).astype(jnp.bfloat16), replicas)
+    down_sum, _ = reduce_over_dp((second * scale).astype(jnp.bfloat16), replicas)
     hvp_tokens = jnp.dot(pick, returned, preferred_element_type=jnp.float32).astype(jnp.bfloat16)
     first = jnp.dot(tangent.T, back_pre, preferred_element_type=jnp.float32) + jnp.dot(
         primal.T, back_tan, preferred_element_type=jnp.float32
     )
-    up_sum = reduce_over_dp((first * scale).astype(jnp.bfloat16), replicas)
+    up_sum, hvp_tokens = reduce_over_dp(
+        (first * scale).astype(jnp.bfloat16), replicas, hvp_tokens
+    )
     hvp_up = up_sum[None]
     hvp_down = down_sum.T[None]
     return (hvp_tokens, hvp_up, hvp_down)

time: 259 us -> 254 us (0.981)
  waiting for transfers between devices: 146 us -> 131 us
  starting transfers between devices: 38.7 us -> 51.7 us
  other arithmetic: 15.3 us -> 12 us
    ppermute x6, waiting for transfers between devices: 22.4 us -> 7 us  [reduce_over_dp(): received.append(lax.ppermute(wire[step], 'dp', pairs))]
    ppermute x6, starting transfers between devices: 10.2 us -> 23.3 us  [reduce_over_dp(): received.append(lax.ppermute(wire[step], 'dp', pairs))]
  transfers between devices with their start and end apart: 11 -> 11, of which waited for: 6 -> 3; matrix products, arithmetic and copies ran while one was open for 19% -> 19% of each run, Pallas kernels for 0% -> 0%
where the time goes in v11:
time: 254 us; the launch traced here: 253 us
  waiting for transfers between devices  131 us (52%)
  starting transfers between devices  51.7 us (20%)
  matrix products  47.7 us (19%)
  other arithmetic  12 us (5%)
  local copies, waits for them, and re-layouts  9.23 us (4%)
    all_to_all x1, waiting for transfers between devices, per_device(): lax.all_to_all(send_xg.reshape(expert_count, capacity, 2 * width), 'exper...  91.4 us
    all_to_all x1, waiting for transfers between devices, per_device(): lax.all_to_all(send_tan.reshape(expert_count, capacity, width), 'expert',...  32.7 us
    ppermute x6, starting transfers between devices, reduce_over_dp(): received.append(lax.ppermute(wire[step], 'dp', pairs))  23.3 us
    all_to_all x1, starting transfers between devices, per_device(): lax.all_to_all(send_xg.reshape(expert_count, capacity, 2 * width), 'exper...  11.7 us
    all_to_all x1, starting transfers between devices, per_device(): lax.all_to_all(input_hvp.reshape(expert_count, capacity, width), 'expert'...  8.77 us
    all_to_all x1, starting transfers between devices, per_device(): lax.all_to_all(send_tan.reshape(expert_count, capacity, width), 'expert',...  7.6 us
    ppermute x6, waiting for transfers between devices, reduce_over_dp(): received.append(lax.ppermute(wire[step], 'dp', pairs))  7 us
    dot_general x1, matrix products, per_device(): jnp.dot(tangent, up_proj, preferred_element_type=jnp.float32) + pre_mix  6.47 us
  transfers between devices with their start and end apart: 11, of which 3 were waited for; matrix products, arithmetic and copies ran while one was open for 19% of the time, Pallas kernels for 0%

profile of v11, /device:TPU:2, one launch (start us, length us, event | category | flops | bytes accessed | tf_op | source)
XLA Modules:
  0.0 252.6 jit_solution(18359232525645365413)
XLA Ops:
  3.9 4.5 %multiply_convert_fusion = bf16[512,4096]{1,0:T(8,128)(2,1)} fusion(pred[128,512]{1,0:T(8,128)(4,1)S(1)} %fusion.40, f32[512]{0:T(512)S(1)} %select_reduce_fusion, pred[4096]{0:T(1024)(128)(4,1)S(1)} %iota_compare_fusion.5, bf16[128,2048]{1,0:T(8,128)(2,1)} %param.10, bf16[128,2048]{1,0:T(8,128)(2,1)} %param.8), kind=kOutput, calls=%fused_computation | convolution fusion | flops 545259520 | bytes 5314560 | tf_op jit(solution)/shard_map/dot_general | solution.py:68
  8.4 11.7 %all-to-all-start = ((bf16[32,16,4096]{2,1,0:T(8,128)(2,1)}), bf16[32,16,4096]{2,1,0:T(8,128)(2,1)}, u32[]{:S(2)}, u32[]{:S(2)}) async-start(bf16[32,16,4096]{2,1,0:T(8,128)(2,1)} %bitcast.96), calls=%async_computation | async-start | bytes 8388608 | tf_op jit(solution)/shard_map/all_to_all | solution.py:77
  20.1 3.1 %convolution_convert_fusion = bf16[512,2048]{1,0:T(8,128)(2,1)} fusion(pred[128,512]{1,0:T(8,128)(4,1)S(1)} %fusion.40, bf16[128,2048]{1,0:T(8,128)(2,1)} %param.9), kind=kOutput, calls=%fused_computation.22 | convolution fusion | flops 269484032 | bytes 2686976 | tf_op jit(solution)/shard_map/dot_general | solution.py:30
  23.2 91.4 %all-to-all-done = bf16[32,16,4096]{2,1,0:T(8,128)(2,1)} async-done(((bf16[32,16,4096]{2,1,0:T(8,128)(2,1)}), bf16[32,16,4096]{2,1,0:T(8,128)(2,1)}, u32[]{:S(2)}, u32[]{:S(2)}) %all-to-all-start) | async-done | bytes 4194336 | tf_op jit(solution)/shard_map/all_to_all | solution.py:77
  114.6 7.6 %all-to-all-start.1 = ((bf16[32,16,2048]{2,1,0:T(8,128)(2,1)}), bf16[32,16,2048]{2,1,0:T(8,128)(2,1)}, u32[]{:S(2)}, u32[]{:S(2)}) async-start(bf16[32,16,2048]{2,1,0:T(8,128)(2,1)} %bitcast.95), calls=%async_computation.1 | async-start | bytes 4194304 | tf_op jit(solution)/shard_map/all_to_all | solution.py:85
  122.2 5.5 %fusion.2 = f32[512,768]{1,0:T(8,128)} fusion(bf16[1,2048,768]{2,1,0:T(8,128)(2,1)} %param.15, bf16[512,4096]{1,0:T(8,128)(2,1)} %bitcast.1), kind=kOutput, calls=%fused_computation.12 | convolution fusion | flops 1610612736 | bytes 6815744 | tf_op jit(solution)/shard_map/dot_general | solution.py:103
  127.7 4.7 %fusion.8 = f32[512,768]{1,0:T(8,128)} fusion(bf16[1,2048,768]{2,1,0:T(8,128)(2,1)S(1)} %copy-done, bf16[512,4096]{1,0:T(8,128)(2,1)} %bitcast.1), kind=kOutput, calls=%fused_computation.18 | convolution fusion | flops 1610612736 | bytes 6815744 | tf_op jit(solution)/shard_map/dot_general | solution.py:97
  132.4 4.6 %fusion.10 = f32[512,768]{1,0:T(8,128)} fusion(bf16[1,768,2048]{2,1,0:T(8,128)(2,1)S(1)} %copy-done.6, bf16[512,4096]{1,0:T(8,128)(2,1)} %bitcast.1), kind=kOutput, calls=%fused_computation.20 | convolution fusion | flops 1610612736 | bytes 6815744 | tf_op jit(solution)/shard_map/dot_general | solution.py:101
  137.1 32.7 %all-to-all-done.1 = bf16[32,16,2048]{2,1,0:T(8,128)(2,1)} async-done(((bf16[32,16,2048]{2,1,0:T(8,128)(2,1)}), bf16[32,16,2048]{2,1,0:T(8,128)(2,1)}, u32[]{:S(2)}, u32[]{:S(2)}) %all-to-all-start.1) | async-done | bytes 2097184 | tf_op jit(solution)/shard_map/all_to_all | solution.py:85
  169.7 6.5 %multiply_convert_fusion.3 = (bf16[512,768]{1,0:T(8,128)(2,1)}, bf16[512,768]{1,0:T(8,128)(2,1)S(1)}, bf16[512,768]{1,0:T(8,128)(2,1)S(1)}) fusion(f32[512,768]{1,0:T(8,128)} %fusion.8, f32[512,768]{1,0:T(8,128)} %fusion.10, f32[512,768]{1,0:T(8,128)} %fusion.2, bf16[512,2048]{1,0:T(8,128)(2,1)} %bitcast.5, bf16[1,2048,768]{2,1,0:T(8,128)(2,1)S(1)} %copy-done), kind=kOutput, calls=%fused_computation.40 | convolution fusion | flops 1618870272 | bytes 12320768 | tf_op jit(solution)/shard_map/dot_general | solution.py:105
  178.1 3.2 %add_convert_fusion = bf16[512,2048]{1,0:T(8,128)(2,1)} fusion(f32[512,2048]{1,0:T(8,128)S(1)} %fusion, bf16[512,768]{1,0:T(8,128)(2,1)S(1)} %get-tuple-element.17, bf16[1,2048,768]{2,1,0:T(8,128)(2,1)S(1)} %copy-done), kind=kOutput, calls=%fused_computation.3 | convolution fusion | flops 1612709888 | bytes 10223616 | tf_op jit(solution)/shard_map/dot_general | solution.py:108
  181.3 8.8 %all-to-all-start.2 = ((bf16[32,16,2048]{2,1,0:T(8,128)(2,1)}), bf16[32,16,2048]{2,1,0:T(8,128)(2,1)}, u32[]{:S(2)}, u32[]{:S(2)}) async-start(bf16[32,16,2048]{2,1,0:T(8,128)(2,1)} %bitcast.98), calls=%async_computation.2 | async-start | bytes 4194304 | tf_op jit(solution)/shard_map/all_to_all | solution.py:114
  190.0 3.4 %multiply_convert_fusion.1 = bf16[2048,768]{1,0:T(8,128)(2,1)S(1)} fusion(bf16[512,768]{1,0:T(8,128)(2,1)S(1)} %copy-done.8, bf16[512,4096]{1,0:T(8,128)(2,1)} %bitcast.1), kind=kOutput, calls=%fused_computation.1 | convolution fusion | flops 1613758464 | bytes 6029312 | tf_op jit(solution)/shard_map/dot_general | solution.py:121
  196.5 3.5 %fusion.48 = f32[2048,768]{1,0:T(8,128)S(1)} fusion(bf16[512,2048]{1,0:T(8,128)(2,1)} %bitcast.5, bf16[512,768]{1,0:T(8,128)(2,1)S(1)} %copy-done.5), kind=kOutput, calls=%fused_computation.79 | convolution fusion | flops 1610612736 | bytes 9175040 | tf_op jit(solution)/shard_map/dot_general | solution.py:124
  200.0 3.6 %multiply_convert_fusion.2 = bf16[2048,768]{1,0:T(8,128)(2,1)S(1)} fusion(f32[2048,768]{1,0:T(8,128)S(1)} %fusion.48, bf16[512,768]{1,0:T(8,128)(2,1)S(1)} %copy-done.3, bf16[512,4096]{1,0:T(8,128)(2,1)} %bitcast.1), kind=kOutput, calls=%fused_computation.2 | convolution fusion | flops 1615331328 | bytes 12320768 | tf_op jit(solution)/shard_map/dot_general | solution.py:124
  205.3 2.6 %copy.36 = bf16[4,1,256,768]{2,3,0,1:T(8,128)(2,1)} copy(bf16[4,1,256,768]{3,2,1,0:T(8,128)(2,1)} %get-tuple-element.27) | data formatting | bytes 3145728
  207.9 2.3 convert_add_fusion
  212.5 3.1 %collective-permute-start.6 = (bf16[256,768]{0,1:T(8,128)(2,1)S(1)}, bf16[256,768]{0,1:T(8,128)(2,1)S(1)}, u32[]{:S(2)}, u32[]{:S(2)}) collective-permute-start(bf16[256,768]{0,1:T(8,128)(2,1)S(1)} %get-tuple-element.33), channel_id=1, source_target_pairs={{0,128},{32,160},{64,192},{96,224},{128,0},{160,32},{192,64},{224,... | collective-permute-start | bytes 1179656 | tf_op jit(solution)/shard_map/ppermute | solution.py:50
  217.0 3.5 %fusion.47 = (bf16[4,256,768]{2,1,0:T(8,128)(2,1)S(1)}, f32[4,256,768]{2,1,0:T(8,128)}) fusion(bf16[4,256,768]{2,1,0:T(8,128)(2,1)} %collective-permute-done, bf16[4,2,256,768]{3,2,1,0:T(8,128)(2,1)S(1)} %bitcast.94, s32[]{:T(128)S(6)} %select_n.43), kind=kLoop, calls=%fused_computation.78 | loop fusion | flops 3145728 | bytes 7864324 | tf_op jit(solution)/shard_map/convert_element_type | solution.py:45
  222.1 2.7 %collective-permute-start.2 = (bf16[256,768]{1,0:T(8,128)(2,1)}, bf16[256,768]{1,0:T(8,128)(2,1)}, u32[]{:S(2)}, u32[]{:S(2)}) collective-permute-start(bf16[256,768]{1,0:T(8,128)(2,1)} %get-tuple-element.36), channel_id=1, source_target_pairs={{0,128},{32,160},{64,192},{96,224},{128,0},{160,32},{192,64},{224,... | collective-permute-start | bytes 1179656 | tf_op jit(solution)/shard_map/ppermute | solution.py:50
  224.9 14.4 %collective-permute-start.1 = (bf16[256,768]{1,0:T(8,128)(2,1)}, bf16[256,768]{1,0:T(8,128)(2,1)}, u32[]{:S(2)}, u32[]{:S(2)}) collective-permute-start(bf16[256,768]{1,0:T(8,128)(2,1)} %get-tuple-element.37), channel_id=1, source_target_pairs={{0,64},{32,96},{64,128},{96,160},{128,192},{160,224},{192,0},{224,... | collective-permute-start | bytes 1179656 | tf_op jit(solution)/shard_map/ppermute | solution.py:50
  240.2 3.0 %convolution_convert_fusion.1 = bf16[128,2048]{1,0:T(8,128)(2,1)} fusion(pred[128,512]{1,0:T(8,128)(4,1)S(1)} %fusion.40, bf16[512,2048]{1,0:T(8,128)(2,1)} %bitcast.8), kind=kOutput, calls=%fused_computation.23 | convolution fusion | flops 268697600 | bytes 2686976 | tf_op jit(solution)/shard_map/dot_general | solution.py:123
  243.2 7.0 %collective-permute-done.1 = bf16[256,768]{1,0:T(8,128)(2,1)} collective-permute-done((bf16[256,768]{1,0:T(8,128)(2,1)}, bf16[256,768]{1,0:T(8,128)(2,1)}, u32[]{:S(2)}, u32[]{:S(2)}) %collective-permute-start.1) | collective-permute-done | bytes 393248 | tf_op jit(solution)/shard_map/ppermute | solution.py:50
  250.1 2.4 fusion.41
  (51 shorter events, 16.0 us)
Async XLA Ops:
  0.6 127.1 %copy-start = (bf16[1,2048,768]{2,1,0:T(8,128)(2,1)S(1)}, bf16[1,2048,768]{2,1,0:T(8,128)(2,1)}, u32[]{:S(2)}) copy-start(bf16[1,2048,768]{2,1,0:T(8,128)(2,1)} %param.13) | copy-start | bytes 9437188
  8.4 106.2 %all-to-all-start = ((bf16[32,16,4096]{2,1,0:T(8,128)(2,1)}), bf16[32,16,4096]{2,1,0:T(8,128)(2,1)}, u32[]{:S(2)}, u32[]{:S(2)}) async-start(bf16[32,16,4096]{2,1,0:T(8,128)(2,1)} %bitcast.96), calls=%async_computation | async-start | bytes 8388608 | tf_op jit(solution)/shard_map/all_to_all | solution.py:77
  114.6 55.1 %all-to-all-start.1 = ((bf16[32,16,2048]{2,1,0:T(8,128)(2,1)}), bf16[32,16,2048]{2,1,0:T(8,128)(2,1)}, u32[]{:S(2)}, u32[]{:S(2)}) async-start(bf16[32,16,2048]{2,1,0:T(8,128)(2,1)} %bitcast.95), calls=%async_computation.1 | async-start | bytes 4194304 | tf_op jit(solution)/shard_map/all_to_all | solution.py:85
  127.7 4.7 %copy-start.6 = (bf16[1,768,2048]{2,1,0:T(8,128)(2,1)S(1)}, bf16[1,768,2048]{2,1,0:T(8,128)(2,1)}, u32[]{:S(2)}) copy-start(bf16[1,768,2048]{2,1,0:T(8,128)(2,1)} %param.14) | copy-start | bytes 9437188
  169.7 6.5 %copy-start.7 = (bf16[1,2048,768]{2,1,0:T(8,128)(2,1)S(1)}, bf16[1,2048,768]{2,1,0:T(8,128)(2,1)}, u32[]{:S(2)}) copy-start(bf16[1,2048,768]{2,1,0:T(8,128)(2,1)} %param.15) | copy-start | bytes 9437188
  176.2 1.8 copy-start.4
  176.2 1.8 copy-start.2
  181.3 8.8 %copy-start.8 = (bf16[512,768]{1,0:T(8,128)(2,1)S(1)}, bf16[512,768]{1,0:T(8,128)(2,1)}, u32[]{:S(2)}) copy-start(bf16[512,768]{1,0:T(8,128)(2,1)} %get-tuple-element.22) | copy-start | bytes 2359300
  181.3 58.9 %all-to-all-start.2 = ((bf16[32,16,2048]{2,1,0:T(8,128)(2,1)}), bf16[32,16,2048]{2,1,0:T(8,128)(2,1)}, u32[]{:S(2)}, u32[]{:S(2)}) async-start(bf16[32,16,2048]{2,1,0:T(8,128)(2,1)} %bitcast.98), calls=%async_computation.2 | async-start | bytes 4194304 | tf_op jit(solution)/shard_map/all_to_all | solution.py:114
  194.8 1.6 copy-start.5
  196.4 3.6 %copy-start.3 = (bf16[512,768]{1,0:T(8,128)(2,1)S(1)}, bf16[512,768]{1,0:T(8,128)(2,1)}, u32[]{:S(2)}) copy-start(bf16[512,768]{1,0:T(8,128)(2,1)} %copy-done.2) | copy-start | bytes 2359300
  196.4 11.5 %collective-permute-start.4 = (bf16[4,256,768]{1,2,0:T(8,128)(2,1)}, bf16[4,256,768]{1,2,0:T(8,128)(2,1)}, u32[]{:S(2)}, u32[]{:S(2)}) collective-permute-start(bf16[4,256,768]{1,2,0:T(8,128)(2,1)} %bitcast.19), channel_id=1, source_target_pairs={{0,32},{32,0},{64,96},{96,64},{128,160},{160,128},{192,224},{224,1... | collective-permute-start | bytes 4718600 | tf_op jit(solution)/shard_map/ppermute | solution.py:43
  204.9 12.1 %collective-permute-start = (bf16[4,256,768]{2,1,0:T(8,128)(2,1)}, bf16[4,256,768]{2,1,0:T(8,128)(2,1)}, u32[]{:S(2)}, u32[]{:S(2)}) collective-permute-start(bf16[4,256,768]{2,1,0:T(8,128)(2,1)} %dynamic-slice_bitcast_fusion), channel_id=1, source_target_pairs={{0,32},{32,0},{64,96},{96,64},{128,160},{160,128},{192,224},{224,1... | collective-permute-start | bytes 4718600 | tf_op jit(solution)/shard_map/ppermute | solution.py:43
  210.9 14.0 %collective-permute-start.5 = (bf16[256,768]{0,1:T(8,128)(2,1)S(1)}, bf16[256,768]{0,1:T(8,128)(2,1)S(1)}, u32[]{:S(2)}, u32[]{:S(2)}) collective-permute-start(bf16[256,768]{0,1:T(8,128)(2,1)S(1)} %get-tuple-element.32), channel_id=1, source_target_pairs={{0,64},{32,96},{64,128},{96,160},{128,192},{160,224},{192,0},{224,... | collective-permute-start | bytes 1179656 | tf_op jit(solution)/shard_map/ppermute | solution.py:50
  212.5 26.7 %collective-permute-start.6 = (bf16[256,768]{0,1:T(8,128)(2,1)S(1)}, bf16[256,768]{0,1:T(8,128)(2,1)S(1)}, u32[]{:S(2)}, u32[]{:S(2)}) collective-permute-start(bf16[256,768]{0,1:T(8,128)(2,1)S(1)} %get-tuple-element.33), channel_id=1, source_target_pairs={{0,128},{32,160},{64,192},{96,224},{128,0},{160,32},{192,64},{224,... | collective-permute-start | bytes 1179656 | tf_op jit(solution)/shard_map/ppermute | solution.py:50
  215.7 23.6 %collective-permute-start.7 = (bf16[256,768]{0,1:T(8,128)(2,1)S(1)}, bf16[256,768]{0,1:T(8,128)(2,1)S(1)}, u32[]{:S(2)}, u32[]{:S(2)}) collective-permute-start(bf16[256,768]{0,1:T(8,128)(2,1)S(1)} %get-tuple-element.34), channel_id=1, source_target_pairs={{0,192},{32,224},{64,0},{96,32},{128,64},{160,96},{192,128},{224,1... | collective-permute-start | bytes 1179656 | tf_op jit(solution)/shard_map/ppermute | solution.py:50
  222.1 21.0 %collective-permute-start.3 = (bf16[256,768]{1,0:T(8,128)(2,1)}, bf16[256,768]{1,0:T(8,128)(2,1)}, u32[]{:S(2)}, u32[]{:S(2)}) collective-permute-start(bf16[256,768]{1,0:T(8,128)(2,1)} %get-tuple-element.35), channel_id=1, source_target_pairs={{0,192},{32,224},{64,0},{96,32},{128,64},{160,96},{192,128},{224,1... | collective-permute-start | bytes 1179656 | tf_op jit(solution)/shard_map/ppermute | solution.py:50
  222.1 21.0 %collective-permute-start.2 = (bf16[256,768]{1,0:T(8,128)(2,1)}, bf16[256,768]{1,0:T(8,128)(2,1)}, u32[]{:S(2)}, u32[]{:S(2)}) collective-permute-start(bf16[256,768]{1,0:T(8,128)(2,1)} %get-tuple-element.36), channel_id=1, source_target_pairs={{0,128},{32,160},{64,192},{96,224},{128,0},{160,32},{192,64},{224,... | collective-permute-start | bytes 1179656 | tf_op jit(solution)/shard_map/ppermute | solution.py:50
  224.9 25.3 %collective-permute-start.1 = (bf16[256,768]{1,0:T(8,128)(2,1)}, bf16[256,768]{1,0:T(8,128)(2,1)}, u32[]{:S(2)}, u32[]{:S(2)}) collective-permute-start(bf16[256,768]{1,0:T(8,128)(2,1)} %get-tuple-element.37), channel_id=1, source_target_pairs={{0,64},{32,96},{64,128},{96,160},{128,192},{160,224},{192,0},{224,... | collective-permute-start | bytes 1179656 | tf_op jit(solution)/shard_map/ppermute | solution.py:50
  240.2 12.4 %copy-start.1 = (bf16[1,2048,768]{2,1,0:T(8,128)(2,1)S(1)}, bf16[1,2048,768]{2,1,0:T(8,128)(2,1)}, u32[]{:S(2)}) copy-start(bf16[1,2048,768]{2,1,0:T(8,128)(2,1)} %param.13) | copy-start | bytes 9437188

commit v12 on v11

--- a/solution.py
+++ b/solution.py
@@ -108,9 +108,11 @@
     input_hvp = (jnp.dot(back_tan, up_proj.T, preferred_element_type=jnp.float32) + hvp_mix).astype(
         jnp.bfloat16
     )
-    input_hvp, back_pre, back_tan, hidden_tan = lax.optimization_barrier(
-        (input_hvp, back_pre, back_tan, hidden_tan)
+    first = jnp.dot(tangent.T, back_pre, preferred_element_type=jnp.float32) + jnp.dot(
+        primal.T, back_tan, preferred_element_type=jnp.float32
     )
+    up_part = (first * scale).astype(jnp.bfloat16)
+    input_hvp, up_part, hidden_tan = lax.optimization_barrier((input_hvp, up_part, hidden_tan))
     returned = lax.all_to_all(
         input_hvp.reshape(expert_count, capacity, width),
         "expert",
@@ -121,12 +123,7 @@
     second = jnp.dot(scaled_cot.T, hidden_tan, preferred_element_type=jnp.float32)
     down_sum, _ = reduce_over_dp((second * scale).astype(jnp.bfloat16), replicas)
     hvp_tokens = jnp.dot(pick, returned, preferred_element_type=jnp.float32).astype(jnp.bfloat16)
-    first = jnp.dot(tangent.T, back_pre, preferred_element_type=jnp.float32) + jnp.dot(
-        primal.T, back_tan, preferred_element_type=jnp.float32
-    )
-    up_sum, hvp_tokens = reduce_over_dp(
-        (first * scale).astype(jnp.bfloat16), replicas, hvp_tokens
-    )
+    up_sum, hvp_tokens = reduce_over_dp(up_part, replicas, hvp_tokens)
     hvp_up = up_sum[None]
     hvp_down = down_sum.T[None]
     return (hvp_tokens, hvp_up, hvp_down)

time: 254 us -> 258 us (1.016)
  starting transfers between devices: 51.7 us -> 38.6 us
  waiting for transfers between devices: 131 us -> 144 us
  local copies, waits for them, and re-layouts: 9.23 us -> 12.3 us
    ppermute x6, starting transfers between devices: 23.3 us -> 9.7 us  [reduce_over_dp(): received.append(lax.ppermute(wire[step], 'dp', pairs))]
    all_to_all x1, waiting for transfers between devices: 0.01 us -> 6.59 us  [per_device(): lax.all_to_all(input_hvp.reshape(expert_count, capacity, width), 'expert'...]
    ppermute x6, waiting for transfers between devices: 7 us -> 13.6 us  [reduce_over_dp(): received.append(lax.ppermute(wire[step], 'dp', pairs))]
  transfers between devices with their start and end apart: 11 -> 11, of which waited for: 3 -> 5; matrix products, arithmetic and copies ran while one was open for 19% -> 17% of each run, Pallas kernels for 0% -> 0%
where the time goes in v12:
time: 258 us; the launch traced here: 257 us
  waiting for transfers between devices  144 us (56%)
  matrix products  49.6 us (19%)
  starting transfers between devices  38.6 us (15%)
  local copies, waits for them, and re-layouts  12.3 us (5%)
  other arithmetic  11.9 us (5%)
    all_to_all x1, waiting for transfers between devices, per_device(): lax.all_to_all(send_xg.reshape(expert_count, capacity, 2 * width), 'exper...  91.4 us
    all_to_all x1, waiting for transfers between devices, per_device(): lax.all_to_all(send_tan.reshape(expert_count, capacity, width), 'expert',...  32.4 us
    ppermute x6, waiting for transfers between devices, reduce_over_dp(): received.append(lax.ppermute(wire[step], 'dp', pairs))  13.6 us
    all_to_all x1, starting transfers between devices, per_device(): lax.all_to_all(send_xg.reshape(expert_count, capacity, 2 * width), 'exper...  11.7 us
    ppermute x6, starting transfers between devices, reduce_over_dp(): received.append(lax.ppermute(wire[step], 'dp', pairs))  9.7 us
    all_to_all x1, starting transfers between devices, per_device(): lax.all_to_all(input_hvp.reshape(expert_count, capacity, width), 'expert'...  8.75 us
    all_to_all x1, starting transfers between devices, per_device(): lax.all_to_all(send_tan.reshape(expert_count, capacity, width), 'expert',...  7.98 us
    all_to_all x1, waiting for transfers between devices, per_device(): lax.all_to_all(input_hvp.reshape(expert_count, capacity, width), 'expert'...  6.59 us
  transfers between devices with their start and end apart: 11, of which 5 were waited for; matrix products, arithmetic and copies ran while one was open for 17% of the time, Pallas kernels for 0%

profile of v12, /device:TPU:2, one launch (start us, length us, event | category | flops | bytes accessed | tf_op | source)
XLA Modules:
  0.0 257.2 jit_solution(5589285702516506265)
XLA Ops:
  3.8 4.5 %multiply_convert_fusion = bf16[512,4096]{1,0:T(8,128)(2,1)} fusion(pred[128,512]{1,0:T(8,128)(4,1)S(1)} %fusion.40, f32[512]{0:T(512)S(1)} %select_reduce_fusion, pred[4096]{0:T(1024)(128)(4,1)S(1)} %iota_compare_fusion.5, bf16[128,2048]{1,0:T(8,128)(2,1)} %param.10, bf16[128,2048]{1,0:T(8,128)(2,1)} %param.8), kind=kOutput, calls=%fused_computation | convolution fusion | flops 545259520 | bytes 5314560 | tf_op jit(solution)/shard_map/dot_general | solution.py:68
  8.3 11.7 %all-to-all-start = ((bf16[32,16,4096]{2,1,0:T(8,128)(2,1)}), bf16[32,16,4096]{2,1,0:T(8,128)(2,1)}, u32[]{:S(2)}, u32[]{:S(2)}) async-start(bf16[32,16,4096]{2,1,0:T(8,128)(2,1)} %bitcast.96), calls=%async_computation | async-start | bytes 8388608 | tf_op jit(solution)/shard_map/all_to_all | solution.py:77
  20.0 3.1 %convolution_convert_fusion = bf16[512,2048]{1,0:T(8,128)(2,1)} fusion(pred[128,512]{1,0:T(8,128)(4,1)S(1)} %fusion.40, bf16[128,2048]{1,0:T(8,128)(2,1)} %param.9), kind=kOutput, calls=%fused_computation.22 | convolution fusion | flops 269484032 | bytes 2686976 | tf_op jit(solution)/shard_map/dot_general | solution.py:30
  23.1 91.4 %all-to-all-done = bf16[32,16,4096]{2,1,0:T(8,128)(2,1)} async-done(((bf16[32,16,4096]{2,1,0:T(8,128)(2,1)}), bf16[32,16,4096]{2,1,0:T(8,128)(2,1)}, u32[]{:S(2)}, u32[]{:S(2)}) %all-to-all-start) | async-done | bytes 4194336 | tf_op jit(solution)/shard_map/all_to_all | solution.py:77
  114.5 8.0 %all-to-all-start.1 = ((bf16[32,16,2048]{2,1,0:T(8,128)(2,1)}), bf16[32,16,2048]{2,1,0:T(8,128)(2,1)}, u32[]{:S(2)}, u32[]{:S(2)}) async-start(bf16[32,16,2048]{2,1,0:T(8,128)(2,1)} %bitcast.95), calls=%async_computation.1 | async-start | bytes 4194304 | tf_op jit(solution)/shard_map/all_to_all | solution.py:85
  122.5 5.7 %fusion.10 = f32[512,768]{1,0:T(8,128)} fusion(bf16[1,768,2048]{2,1,0:T(8,128)(2,1)} %param.14, bf16[512,4096]{1,0:T(8,128)(2,1)} %bitcast.1), kind=kOutput, calls=%fused_computation.20 | convolution fusion | flops 1610612736 | bytes 6815744 | tf_op jit(solution)/shard_map/dot_general | solution.py:101
  128.2 4.6 %fusion.2 = f32[512,768]{1,0:T(8,128)} fusion(bf16[1,2048,768]{2,1,0:T(8,128)(2,1)S(1)} %copy-done.2, bf16[512,4096]{1,0:T(8,128)(2,1)} %bitcast.1), kind=kOutput, calls=%fused_computation.12 | convolution fusion | flops 1610612736 | bytes 6815744 | tf_op jit(solution)/shard_map/dot_general | solution.py:103
  132.8 4.6 %fusion.8 = f32[512,768]{1,0:T(8,128)} fusion(bf16[1,2048,768]{2,1,0:T(8,128)(2,1)S(1)} %copy-done, bf16[512,4096]{1,0:T(8,128)(2,1)} %bitcast.1), kind=kOutput, calls=%fused_computation.18 | convolution fusion | flops 1610612736 | bytes 6815744 | tf_op jit(solution)/shard_map/dot_general | solution.py:97
  137.4 32.4 %all-to-all-done.1 = bf16[32,16,2048]{2,1,0:T(8,128)(2,1)} async-done(((bf16[32,16,2048]{2,1,0:T(8,128)(2,1)}), bf16[32,16,2048]{2,1,0:T(8,128)(2,1)}, u32[]{:S(2)}, u32[]{:S(2)}) %all-to-all-start.1) | async-done | bytes 2097184 | tf_op jit(solution)/shard_map/all_to_all | solution.py:85
  169.8 6.3 %multiply_convert_fusion.3 = (bf16[512,768]{1,0:T(8,128)(2,1)}, bf16[512,768]{1,0:T(8,128)(2,1)S(1)}, bf16[512,768]{1,0:T(8,128)(2,1)S(1)}) fusion(f32[512,768]{1,0:T(8,128)} %fusion.8, f32[512,768]{1,0:T(8,128)} %fusion.10, f32[512,768]{1,0:T(8,128)} %fusion.2, bf16[512,2048]{1,0:T(8,128)(2,1)} %bitcast.5, bf16[1,2048,768]{2,1,0:T(8,128)(2,1)S(1)} %copy-done), kind=kOutput, calls=%fused_computation.40 | convolution fusion | flops 1618870272 | bytes 12320768 | tf_op jit(solution)/shard_map/dot_general | solution.py:105
  176.1 3.6 %fusion.48 = f32[2048,768]{1,0:T(8,128)S(1)} fusion(bf16[512,2048]{1,0:T(8,128)(2,1)} %bitcast.5, bf16[512,768]{1,0:T(8,128)(2,1)S(1)} %get-tuple-element.29), kind=kOutput, calls=%fused_computation.79 | convolution fusion | flops 1610612736 | bytes 9175040 | tf_op jit(solution)/shard_map/dot_general | solution.py:111
  181.6 5.3 %multiply_convert_fusion.2 = bf16[2048,768]{1,0:T(8,128)(2,1)} fusion(f32[2048,768]{1,0:T(8,128)S(1)} %fusion.48, bf16[512,768]{1,0:T(8,128)(2,1)S(1)} %get-tuple-element.28, bf16[512,4096]{1,0:T(8,128)(2,1)} %bitcast.1), kind=kOutput, calls=%fused_computation.2 | convolution fusion | flops 1615331328 | bytes 12320768 | tf_op jit(solution)/shard_map/dot_general | solution.py:111
  186.9 3.4 %add_convert_fusion = bf16[512,2048]{1,0:T(8,128)(2,1)} fusion(f32[512,2048]{1,0:T(8,128)S(1)} %fusion, bf16[512,768]{1,0:T(8,128)(2,1)S(1)} %get-tuple-element.28, bf16[1,2048,768]{2,1,0:T(8,128)(2,1)S(1)} %copy-done), kind=kOutput, calls=%fused_computation.3 | convolution fusion | flops 1612709888 | bytes 10223616 | tf_op jit(solution)/shard_map/dot_general | solution.py:108
  190.3 8.7 %all-to-all-start.2 = ((bf16[32,16,2048]{2,1,0:T(8,128)(2,1)}), bf16[32,16,2048]{2,1,0:T(8,128)(2,1)}, u32[]{:S(2)}, u32[]{:S(2)}) async-start(bf16[32,16,2048]{2,1,0:T(8,128)(2,1)} %bitcast.98), calls=%async_computation.2 | async-start | bytes 4194304 | tf_op jit(solution)/shard_map/all_to_all | solution.py:116
  199.1 3.6 %multiply_convert_fusion.1 = bf16[2048,768]{1,0:T(8,128)(2,1)S(1)} fusion(bf16[512,768]{1,0:T(8,128)(2,1)} %get-tuple-element.20, bf16[512,4096]{1,0:T(8,128)(2,1)} %bitcast.1), kind=kOutput, calls=%fused_computation.1 | convolution fusion | flops 1613758464 | bytes 6029312 | tf_op jit(solution)/shard_map/dot_general | solution.py:123
  204.6 2.6 %copy.34 = bf16[4,1,256,768]{2,3,0,1:T(8,128)(2,1)} copy(bf16[4,1,256,768]{3,2,1,0:T(8,128)(2,1)} %get-tuple-element.26) | data formatting | bytes 3145728 | tf_op jit(solution)/shard_map/jit(dynamic_index_in_dim)/dynamic_slice | solution.py:42
  207.3 2.7 %dynamic-slice_bitcast_fusion = bf16[4,256,768]{2,1,0:T(8,128)(2,1)} fusion(bf16[4,2,256,768]{3,2,1,0:T(8,128)(2,1)} %bitcast.93, s32[]{:T(128)S(6)} %select_n.44), kind=kLoop, calls=%fused_computation.39 | loop fusion | bytes 3145732 | tf_op jit(solution)/shard_map/jit(dynamic_index_in_dim)/squeeze | solution.py:42
  210.4 2.6 %copy.36 = bf16[4,1,256,768]{2,3,0,1:T(8,128)(2,1)} copy(bf16[4,1,256,768]{3,2,1,0:T(8,128)(2,1)} %get-tuple-element.25) | data formatting | bytes 3145728
  217.7 2.7 %collective-permute-start.6 = (bf16[256,768]{0,1:T(8,128)(2,1)S(1)}, bf16[256,768]{0,1:T(8,128)(2,1)S(1)}, u32[]{:S(2)}, u32[]{:S(2)}) collective-permute-start(bf16[256,768]{0,1:T(8,128)(2,1)S(1)} %get-tuple-element.31), channel_id=1, source_target_pairs={{0,128},{32,160},{64,192},{96,224},{128,0},{160,32},{192,64},{224,... | collective-permute-start | bytes 1179656 | tf_op jit(solution)/shard_map/ppermute | solution.py:50
  221.7 3.5 %fusion.47 = (bf16[4,256,768]{2,1,0:T(8,128)(2,1)S(1)}, f32[4,256,768]{2,1,0:T(8,128)}) fusion(bf16[4,256,768]{2,1,0:T(8,128)(2,1)} %collective-permute-done, bf16[4,2,256,768]{3,2,1,0:T(8,128)(2,1)S(1)} %bitcast.94, s32[]{:T(128)S(6)} %select_n.43), kind=kLoop, calls=%fused_computation.78 | loop fusion | flops 3145728 | bytes 7864324 | tf_op jit(solution)/shard_map/convert_element_type | solution.py:45
  230.9 7.9 %collective-permute-done.6 = bf16[256,768]{0,1:T(8,128)(2,1)S(1)} collective-permute-done((bf16[256,768]{0,1:T(8,128)(2,1)S(1)}, bf16[256,768]{0,1:T(8,128)(2,1)S(1)}, u32[]{:S(2)}, u32[]{:S(2)}) %collective-permute-start.6) | collective-permute-done | bytes 393248 | tf_op jit(solution)/shard_map/ppermute | solution.py:50
  239.7 6.6 %all-to-all-done.2 = bf16[32,16,2048]{2,1,0:T(8,128)(2,1)} async-done(((bf16[32,16,2048]{2,1,0:T(8,128)(2,1)}), bf16[32,16,2048]{2,1,0:T(8,128)(2,1)}, u32[]{:S(2)}, u32[]{:S(2)}) %all-to-all-start.2) | async-done | bytes 2097184 | tf_op jit(solution)/shard_map/all_to_all | solution.py:116
  246.3 2.8 %convolution_convert_fusion.1 = bf16[128,2048]{1,0:T(8,128)(2,1)} fusion(pred[128,512]{1,0:T(8,128)(4,1)S(1)} %fusion.40, bf16[512,2048]{1,0:T(8,128)(2,1)} %bitcast.8), kind=kOutput, calls=%fused_computation.23 | convolution fusion | flops 268697600 | bytes 2686976 | tf_op jit(solution)/shard_map/dot_general | solution.py:125
  249.1 5.6 %collective-permute-done.2 = bf16[256,768]{1,0:T(8,128)(2,1)} collective-permute-done((bf16[256,768]{1,0:T(8,128)(2,1)}, bf16[256,768]{1,0:T(8,128)(2,1)}, u32[]{:S(2)}, u32[]{:S(2)}) %collective-permute-start.2) | collective-permute-done | bytes 393248 | tf_op jit(solution)/shard_map/ppermute | solution.py:50
  (41 shorter events, 22.4 us)
Async XLA Ops:
  0.6 132.2 %copy-start = (bf16[1,2048,768]{2,1,0:T(8,128)(2,1)S(1)}, bf16[1,2048,768]{2,1,0:T(8,128)(2,1)}, u32[]{:S(2)}) copy-start(bf16[1,2048,768]{2,1,0:T(8,128)(2,1)} %param.13) | copy-start | bytes 9437188
  8.3 106.2 %all-to-all-start = ((bf16[32,16,4096]{2,1,0:T(8,128)(2,1)}), bf16[32,16,4096]{2,1,0:T(8,128)(2,1)}, u32[]{:S(2)}, u32[]{:S(2)}) async-start(bf16[32,16,4096]{2,1,0:T(8,128)(2,1)} %bitcast.96), calls=%async_computation | async-start | bytes 8388608 | tf_op jit(solution)/shard_map/all_to_all | solution.py:77
  114.5 55.3 %all-to-all-start.1 = ((bf16[32,16,2048]{2,1,0:T(8,128)(2,1)}), bf16[32,16,2048]{2,1,0:T(8,128)(2,1)}, u32[]{:S(2)}, u32[]{:S(2)}) async-start(bf16[32,16,2048]{2,1,0:T(8,128)(2,1)} %bitcast.95), calls=%async_computation.1 | async-start | bytes 4194304 | tf_op jit(solution)/shard_map/all_to_all | solution.py:85
  122.5 5.7 %copy-start.2 = (bf16[1,2048,768]{2,1,0:T(8,128)(2,1)S(1)}, bf16[1,2048,768]{2,1,0:T(8,128)(2,1)}, u32[]{:S(2)}) copy-start(bf16[1,2048,768]{2,1,0:T(8,128)(2,1)} %param.15) | copy-start | bytes 9437188
  176.1 3.6 %copy-start.3 = (bf16[1,2048,768]{2,1,0:T(8,128)(2,1)S(1)}, bf16[1,2048,768]{2,1,0:T(8,128)(2,1)}, u32[]{:S(2)}) copy-start(bf16[1,2048,768]{2,1,0:T(8,128)(2,1)} %param.15) | copy-start | bytes 9437188
  190.3 56.0 %all-to-all-start.2 = ((bf16[32,16,2048]{2,1,0:T(8,128)(2,1)}), bf16[32,16,2048]{2,1,0:T(8,128)(2,1)}, u32[]{:S(2)}, u32[]{:S(2)}) async-start(bf16[32,16,2048]{2,1,0:T(8,128)(2,1)} %bitcast.98), calls=%async_computation.2 | async-start | bytes 4194304 | tf_op jit(solution)/shard_map/all_to_all | solution.py:116
  207.3 5.8 %collective-permute-start.4 = (bf16[4,256,768]{1,2,0:T(8,128)(2,1)}, bf16[4,256,768]{1,2,0:T(8,128)(2,1)}, u32[]{:S(2)}, u32[]{:S(2)}) collective-permute-start(bf16[4,256,768]{1,2,0:T(8,128)(2,1)} %bitcast.99), channel_id=1, source_target_pairs={{0,32},{32,0},{64,96},{96,64},{128,160},{160,128},{192,224},{224,1... | collective-permute-start | bytes 4718600 | tf_op jit(solution)/shard_map/ppermute | solution.py:43
  209.9 11.8 %collective-permute-start = (bf16[4,256,768]{2,1,0:T(8,128)(2,1)}, bf16[4,256,768]{2,1,0:T(8,128)(2,1)}, u32[]{:S(2)}, u32[]{:S(2)}) collective-permute-start(bf16[4,256,768]{2,1,0:T(8,128)(2,1)} %dynamic-slice_bitcast_fusion), channel_id=1, source_target_pairs={{0,32},{32,0},{64,96},{96,64},{128,160},{160,128},{192,224},{224,1... | collective-permute-start | bytes 4718600 | tf_op jit(solution)/shard_map/ppermute | solution.py:43
  215.3 6.4 %copy-start.1 = (bf16[2048,768]{1,0:T(8,128)(2,1)S(1)}, bf16[2048,768]{1,0:T(8,128)(2,1)}, u32[]{:S(2)}) copy-start(bf16[2048,768]{1,0:T(8,128)(2,1)} %multiply_convert_fusion.2) | copy-start | bytes 9437188
  216.0 12.4 %collective-permute-start.5 = (bf16[256,768]{0,1:T(8,128)(2,1)S(1)}, bf16[256,768]{0,1:T(8,128)(2,1)S(1)}, u32[]{:S(2)}, u32[]{:S(2)}) collective-permute-start(bf16[256,768]{0,1:T(8,128)(2,1)S(1)} %get-tuple-element.30), channel_id=1, source_target_pairs={{0,64},{32,96},{64,128},{96,160},{128,192},{160,224},{192,0},{224,... | collective-permute-start | bytes 1179656 | tf_op jit(solution)/shard_map/ppermute | solution.py:50
  217.7 21.1 %collective-permute-start.6 = (bf16[256,768]{0,1:T(8,128)(2,1)S(1)}, bf16[256,768]{0,1:T(8,128)(2,1)S(1)}, u32[]{:S(2)}, u32[]{:S(2)}) collective-permute-start(bf16[256,768]{0,1:T(8,128)(2,1)S(1)} %get-tuple-element.31), channel_id=1, source_target_pairs={{0,128},{32,160},{64,192},{96,224},{128,0},{160,32},{192,64},{224,... | collective-permute-start | bytes 1179656 | tf_op jit(solution)/shard_map/ppermute | solution.py:50
  220.3 18.4 %collective-permute-start.7 = (bf16[256,768]{0,1:T(8,128)(2,1)S(1)}, bf16[256,768]{0,1:T(8,128)(2,1)S(1)}, u32[]{:S(2)}, u32[]{:S(2)}) collective-permute-start(bf16[256,768]{0,1:T(8,128)(2,1)S(1)} %get-tuple-element.32), channel_id=1, source_target_pairs={{0,192},{32,224},{64,0},{96,32},{128,64},{160,96},{192,128},{224,1... | collective-permute-start | bytes 1179656 | tf_op jit(solution)/shard_map/ppermute | solution.py:50
  226.8 22.3 %collective-permute-start.1 = (bf16[256,768]{1,0:T(8,128)(2,1)}, bf16[256,768]{1,0:T(8,128)(2,1)}, u32[]{:S(2)}, u32[]{:S(2)}) collective-permute-start(bf16[256,768]{1,0:T(8,128)(2,1)} %get-tuple-element.35), channel_id=1, source_target_pairs={{0,64},{32,96},{64,128},{96,160},{128,192},{160,224},{192,0},{224,... | collective-permute-start | bytes 1179656 | tf_op jit(solution)/shard_map/ppermute | solution.py:50
  227.5 27.3 %collective-permute-start.2 = (bf16[256,768]{1,0:T(8,128)(2,1)}, bf16[256,768]{1,0:T(8,128)(2,1)}, u32[]{:S(2)}, u32[]{:S(2)}) collective-permute-start(bf16[256,768]{1,0:T(8,128)(2,1)} %get-tuple-element.34), channel_id=1, source_target_pairs={{0,128},{32,160},{64,192},{96,224},{128,0},{160,32},{192,64},{224,... | collective-permute-start | bytes 1179656 | tf_op jit(solution)/shard_map/ppermute | solution.py:50
  228.4 26.4 %collective-permute-start.3 = (bf16[256,768]{1,0:T(8,128)(2,1)}, bf16[256,768]{1,0:T(8,128)(2,1)}, u32[]{:S(2)}, u32[]{:S(2)}) collective-permute-start(bf16[256,768]{1,0:T(8,128)(2,1)} %get-tuple-element.33), channel_id=1, source_target_pairs={{0,192},{32,224},{64,0},{96,32},{128,64},{160,96},{192,128},{224,1... | collective-permute-start | bytes 1179656 | tf_op jit(solution)/shard_map/ppermute | solution.py:50
